TPU v7x, 32 devices: a whole 2x2x4 slice. The times are simulated.
32 devices in a mesh: view: 4 (over y, x), tile: 8 (over z, core).
Axes of the slice: x: 2, y: 2, z: 4, core: 2. Of those that a mesh axis runs over, the one named last changes fastest.
Arguments:
- initial_estimate: float32 [4, 256, 2048], P('view', 'tile'), may hold values from 0.5 to 1.5
- raw_views: bfloat16 [4, 4, 256, 2048], P('view', None, 'tile'), may hold values from 1 to 3
- route_tile: int32 [4, 512, 1], replicated, may hold values from 0 to 7; in each aligned block of 64 rows (0 to 63, 64 to 127, ..., all dimensions but the last counted through in order) at most 16 rows name the same one
- route_block: int32 [4, 512], replicated, may hold values from 0 to 63
- interp: bfloat16 [4, 128, 128], replicated, may hold values from 0 to 1, as said below
- row_kernel: float32 [4, 4, 17], replicated, may hold values from 0.05 to 1
- col_kernel: float32 [4, 4, 17], replicated, may hold values from 0.05 to 1
- psf_band: int32 [4], replicated, may hold values from 0 to 3
- background: float32 [4], replicated, may hold values from 0.2 to 1
Outputs:
- final_estimate: float32 [4, 256, 2048], P('view', 'tile')
Inputs may be any that keep to these rules, and one draw needn't show every extreme that they name: `route_tile`: entry [v, t * 64 + b, 0] is the tile on which block b of tile t lands in view v; in each view the 64 blocks of one tile name any one tile at most 16 times. `route_block`: entry [v, t * 64 + b] is the block of the receiving tile on which that block lands; several may land on one block and some blocks receive none. `interp`: entries are positive.
All inputs are finite; a program needn't handle non-finite values.
Results may differ from a plain program's by a relative error of at most 0.0091.
Values may be sent and summed in bfloat16 or wider, within the bound.
No kernel may reach another device: no remote copies, remote signals or barrier semaphores. Data moves between devices by JAX's collectives and lax.ppermute only.
A program may use at most 64 MiB of HBM per device.

v0:
```python
import jax
import jax.numpy as jnp
from jax import lax
from jax.sharding import PartitionSpec as P
from jax.experimental import pallas as pl
from jax.experimental.pallas import tpu as pltpu

BR = 8
BW = 128
TAPS = 17


def passed_along(x, axis, by):
    count = lax.axis_size(axis)
    return lax.ppermute(x, axis, [(i, (i + by) % count) for i in range(count)])


def to_blocks(values_in):
    rows, plane_width = values_in.shape
    shaped = values_in.reshape(rows // BR, BR, plane_width // BW, BW)
    return shaped.transpose(0, 2, 1, 3).reshape(-1, BR * BW)


def from_blocks(pieces, rows, plane_width):
    shaped = pieces.reshape(rows // BR, plane_width // BW, BR, BW)
    return shaped.transpose(0, 2, 1, 3).reshape(rows, plane_width)


def banded(taps_in, diff):
    result = jnp.zeros(diff.shape, jnp.float32)
    for tap_index in range(TAPS):
        result = result + jnp.where(diff == tap_index, taps_in[tap_index].astype(jnp.float32), 0.0)
    return result.astype(jnp.bfloat16)


def column_mats(taps_in, flipped):
    radius = (TAPS - 1) // 2
    source_lane = jnp.arange(BW, dtype=jnp.int32)[:, None]
    target_lane = jnp.arange(BW, dtype=jnp.int32)[None, :]
    mats = []
    for offset in (-1, 0, 1):
        if flipped:
            diff = target_lane - source_lane - offset * BW + radius
        else:
            diff = source_lane + offset * BW - target_lane + radius
        mats.append(banded(taps_in, diff))
    return mats


def row_mat(taps_in, rows):
    radius = (TAPS - 1) // 2
    out_row = jnp.arange(rows, dtype=jnp.int32)[:, None]
    src_row = jnp.arange(rows, dtype=jnp.int32)[None, :]
    return banded(taps_in, src_row - out_row + radius)


def column_pass(values_in, mats):
    rows, plane_width = values_in.shape
    col_count = plane_width // BW
    grid_cells = values_in.reshape(rows, col_count, BW)
    padded = jnp.pad(grid_cells, ((0, 0), (1, 1), (0, 0)))
    result_sum = jnp.zeros(grid_cells.shape, jnp.float32)
    for position in range(3):
        result_sum = result_sum + jnp.einsum(
            "rcj,jk->rck",
            padded[:, position : position + col_count],
            mats[position],
            preferred_element_type=jnp.float32,
        )
    return result_sum.reshape(rows, plane_width)


def update_plane(estimate, raw_plane, matrix, landing, row_taps, col_taps, level):
    rows, plane_width = estimate.shape
    blocks = (rows // BR) * (plane_width // BW)
    block_iota = jnp.arange(blocks, dtype=jnp.int32)
    rounded = estimate.astype(jnp.bfloat16).reshape(rows, plane_width // BW, BW)
    moved = jnp.einsum("rcj,jk->rck", rounded, matrix, preferred_element_type=jnp.float32)
    moved = moved.astype(jnp.bfloat16).reshape(rows, plane_width)
    gather_mat = landing[None, :] == block_iota[:, None]
    land_count = jnp.sum(gather_mat.astype(jnp.float32), axis=1)
    summed = jnp.dot(
        gather_mat.astype(jnp.bfloat16), to_blocks(moved), preferred_element_type=jnp.float32
    )
    summed = (summed / jnp.maximum(land_count, 1.0)[:, None]).astype(jnp.bfloat16)
    joined = from_blocks(summed, rows, plane_width)
    across = column_pass(joined, column_mats(col_taps, False)).astype(jnp.bfloat16)
    band = row_mat(row_taps, rows)
    blurred = jnp.dot(band, across, preferred_element_type=jnp.float32) + level
    ratio = (raw_plane.astype(jnp.float32) / blurred).astype(jnp.bfloat16)
    rows_back = jnp.dot(band.T, ratio, preferred_element_type=jnp.float32).astype(jnp.bfloat16)
    spread = column_pass(rows_back, column_mats(col_taps, True)).astype(jnp.bfloat16)
    returned = jnp.einsum(
        "rcj,kj->rck",
        spread.reshape(rows, plane_width // BW, BW),
        matrix,
        preferred_element_type=jnp.float32,
    ).astype(jnp.bfloat16)
    correction = jnp.take(to_blocks(returned.reshape(rows, plane_width)), landing, axis=0)
    return estimate * from_blocks(correction, rows, plane_width).astype(jnp.float32)


def plane_kernel(est_ref, raw_ref, m_ref, mt_ref, s_ref, cnt_ref, g_ref, bf_ref, bb_ref, a_ref,
                 at_ref, bg_ref, out_ref, work, joined, across, ratio):
    rows, plane_width = est_ref.shape
    nt = rows // BR
    nc = plane_width // BW
    f32 = jnp.float32
    bf16 = jnp.bfloat16

    def cols(c):
        return slice(c * BW, (c + 1) * BW)

    for c in range(nc):
        blk = est_ref[:, cols(c)].astype(bf16)
        moved = jnp.dot(blk, m_ref[...], preferred_element_type=f32)
        work[c] = moved.astype(bf16).astype(f32)

    def regroup(src, mat_ref, dst, post):
        for r in range(BR):
            stacked = jnp.concatenate(
                [src[c, pl.ds(r, nt, stride=BR), :] for c in range(nc)], axis=0
            )
            result = jnp.dot(mat_ref[...], stacked.astype(bf16), preferred_element_type=f32)
            result = post(result)
            for c in range(nc):
                dst[c, pl.ds(r, nt, stride=BR), :] = result[c * nt:(c + 1) * nt, :]

    regroup(work, s_ref, joined,
            lambda v: (v / cnt_ref[...]).astype(bf16).astype(f32))

    def column_blur(take, mats_ref, c):
        total = None
        for offset in (-1, 0, 1):
            if 0 <= c + offset < nc:
                part = jnp.dot(take(c + offset).astype(bf16), mats_ref[offset + 1],
                               preferred_element_type=f32)
                total = part if total is None else total + part
        return total

    for c in range(nc):
        across[:, cols(c)] = column_blur(lambda i: joined[i], bf_ref, c).astype(bf16)
    level = bg_ref[0]
    for c in range(nc):
        blurred = jnp.dot(a_ref[...], across[:, cols(c)], preferred_element_type=f32) + level
        quotient = (raw_ref[:, cols(c)].astype(f32) / blurred).astype(bf16)
        ratio[:, cols(c)] = jnp.dot(at_ref[...], quotient, preferred_element_type=f32).astype(bf16)
    for c in range(nc):
        spread = column_blur(lambda i: ratio[:, cols(i)], bb_ref, c).astype(bf16)
        back = jnp.dot(spread, mt_ref[...], preferred_element_type=f32)
        work[c] = back.astype(bf16).astype(f32)
    regroup(work, g_ref, joined, lambda v: v)
    for c in range(nc):
        out_ref[:, cols(c)] = est_ref[:, cols(c)] * joined[c]


def kernel_update(estimate, raw_plane, matrix, landing, row_taps, col_taps, level):
    rows, plane_width = estimate.shape
    nt = rows // BR
    nc = plane_width // BW
    blocks = nt * nc
    order = landing.reshape(nt, nc).T.reshape(-1)
    place = (order % nc) * nt + order // nc
    spots = jnp.arange(blocks, dtype=jnp.int32)
    sum_mat = place[None, :] == spots[:, None]
    pick_mat = place[:, None] == spots[None, :]
    count = jnp.sum(sum_mat.astype(jnp.float32), axis=1)
    count = jnp.broadcast_to(jnp.maximum(count, 1.0)[:, None], (blocks, BW))
    band = row_mat(row_taps, rows)
    vmem = pl.BlockSpec(memory_space=pltpu.VMEM)
    return pl.pallas_call(
        plane_kernel,
        out_shape=jax.ShapeDtypeStruct((rows, plane_width), jnp.float32),
        in_specs=[vmem] * 11 + [pl.BlockSpec(memory_space=pltpu.SMEM)],
        out_specs=vmem,
        scratch_shapes=[
            pltpu.VMEM((nc, rows, BW), jnp.float32),
            pltpu.VMEM((nc, rows, BW), jnp.float32),
            pltpu.VMEM((rows, plane_width), jnp.bfloat16),
            pltpu.VMEM((rows, plane_width), jnp.bfloat16),
        ],
        compiler_params=pltpu.CompilerParams(vmem_limit_bytes=48 * 1024 * 1024),
        cost_estimate=pl.CostEstimate(
            flops=2 * rows * plane_width * (4 * BW + 2 * rows + 2 * blocks // BR * BR),
            bytes_accessed=rows * plane_width * 10,
            transcendentals=0,
        ),
    )(
        estimate,
        raw_plane,
        matrix,
        matrix.T,
        sum_mat.astype(jnp.bfloat16),
        count,
        pick_mat.astype(jnp.bfloat16),
        jnp.stack(column_mats(col_taps, False)),
        jnp.stack(column_mats(col_taps, True)),
        band,
        band.T,
        jnp.reshape(level, (1,)).astype(jnp.float32),
    )


def with_halo(cells, sides, width):
    for axis, dim in sides:
        count = lax.axis_size(axis)
        ends = count - 1
        head = lax.slice_in_dim(cells, 0, width, axis=dim)
        tail = lax.slice_in_dim(cells, cells.shape[dim] - width, cells.shape[dim], axis=dim)
        cells = jnp.concatenate(
            [
                lax.ppermute(tail, axis, [(i, (i + 1) % count) for i in range(ends)]),
                cells,
                lax.ppermute(head, axis, [((i + 1) % count, i) for i in range(ends)]),
            ],
            axis=dim,
        )
    return cells


def sharded_to_blocks(values_in):
    planes, tile_rows, plane_width = values_in.shape
    shaped = values_in.reshape(planes, tile_rows // BR, BR, plane_width // BW, BW)
    return shaped.transpose(1, 3, 0, 2, 4).reshape(-1, planes, BR, BW)


def sharded_from_blocks(pieces, tile_rows, plane_width):
    planes = pieces.shape[1]
    shaped = pieces.reshape(tile_rows // BR, plane_width // BW, planes, BR, BW)
    return shaped.transpose(2, 0, 3, 1, 4).reshape(planes, tile_rows, plane_width)


def sharded_column_pass(values_in, taps_in, flipped):
    planes, tile_rows, plane_width = values_in.shape
    radius = (taps_in.shape[1] - 1) // 2
    lane_iota = jnp.arange(BW, dtype=jnp.int32)
    source_lane = lane_iota[:, None]
    target_lane = lane_iota[None, :]
    zero_bf = jnp.zeros((), jnp.bfloat16)
    band_mats = []
    for offset in (-1, 0, 1):
        if flipped:
            tap_index = target_lane - source_lane - offset * BW + radius
        else:
            tap_index = source_lane + offset * BW - target_lane + radius
        inside = (tap_index >= 0) & (tap_index <= 2 * radius)
        picked = taps_in[:, jnp.clip(tap_index, 0, 2 * radius)]
        band_mats.append(jnp.where(inside[None, :, :], picked, zero_bf))
    col_count = plane_width // BW
    grid_cells = values_in.reshape(planes, tile_rows, col_count, BW)
    padded = jnp.pad(grid_cells, ((0, 0), (0, 0), (1, 1), (0, 0)))
    result_sum = jnp.zeros(grid_cells.shape, jnp.float32)
    for position in range(3):
        result_sum = result_sum + jnp.einsum(
            "prcj,pjk->prck",
            padded[:, :, position : position + col_count],
            band_mats[position],
            preferred_element_type=jnp.float32,
        )
    return result_sum.reshape(planes, tile_rows, plane_width)


def row_pass(padded, taps_in, flipped):
    planes, extended, plane_width = padded.shape
    radius = (taps_in.shape[1] - 1) // 2
    tile_rows = extended - 2 * radius
    row_iota = jnp.arange(tile_rows, dtype=jnp.int32)[:, None]
    src_iota = jnp.arange(extended, dtype=jnp.int32)[None, :]
    if flipped:
        tap_index = row_iota + 2 * radius - src_iota
    else:
        tap_index = src_iota - row_iota
    inside = (tap_index >= 0) & (tap_index <= 2 * radius)
    band_rows = jnp.where(
        inside[None, :, :],
        taps_in[:, jnp.clip(tap_index, 0, 2 * radius)],
        jnp.zeros((), jnp.bfloat16),
    )
    return jnp.einsum("prs,psw->prw", band_rows, padded, preferred_element_type=jnp.float32)


def sharded_update(
    estimate,
    raw_piece,
    view_index,
    slab_index,
    route_tile,
    route_block,
    interp,
    row_psf,
    col_psf,
    psf_band,
    background,
):
    tile_count = lax.axis_size("tile")
    my_tile = lax.axis_index("tile")
    planes, tile_rows, plane_width = estimate.shape
    blocks = tile_rows // BR * (plane_width // BW)
    capacity = max(2, 2 * blocks // tile_count)
    radius = (TAPS - 1) // 2
    matrix = interp[view_index]
    dest_tile = route_tile[view_index, :, 0].reshape(tile_count, blocks)
    dest_block = route_block[view_index].reshape(tile_count, blocks)
    tiles_iota = jnp.arange(tile_count, dtype=jnp.int32)
    one_hot = (dest_tile[:, :, None] == tiles_iota[None, None, :]).astype(jnp.int32)
    slot_rank = jnp.sum((jnp.cumsum(one_hot, axis=1) - one_hot) * one_hot, axis=2)
    slot_index = dest_tile * capacity + slot_rank
    my_slots = slot_index[my_tile]
    slots_iota = jnp.arange(tile_count * capacity, dtype=jnp.int32)
    block_iota = jnp.arange(blocks, dtype=jnp.int32)
    match_send = my_slots[None, :] == slots_iota[:, None]
    send_ok = jnp.any(match_send, axis=1)
    send_src = jnp.sum(jnp.where(match_send, block_iota[None, :], 0), axis=1)
    match_recv = (dest_tile == my_tile)[:, None, :] & (
        slot_rank[:, None, :] == jnp.arange(capacity, dtype=jnp.int32)[None, :, None]
    )
    recv_ok = jnp.any(match_recv, axis=2).reshape(-1)
    recv_off = jnp.sum(jnp.where(match_recv, dest_block[:, None, :], 0), axis=2).reshape(-1)
    zero_bf = jnp.zeros((), jnp.bfloat16)
    rounded_estimate = estimate.astype(jnp.bfloat16)
    interpolated = jnp.einsum(
        "bprj,jk->bprk", sharded_to_blocks(rounded_estimate), matrix, preferred_element_type=jnp.float32
    ).astype(jnp.bfloat16)
    outgoing = jnp.where(send_ok[:, None, None, None], interpolated[send_src], zero_bf)
    outgoing = outgoing.reshape(tile_count, capacity, planes, BR, BW)
    incoming = lax.all_to_all(outgoing, "tile", split_axis=0, concat_axis=0, tiled=True)
    incoming = incoming.reshape(tile_count * capacity, planes * BR * BW)
    landing = (recv_off[None, :] == block_iota[:, None]) & recv_ok[None, :]
    land_count = jnp.sum(landing.astype(jnp.float32), axis=1)
    summed = jnp.dot(landing.astype(jnp.bfloat16), incoming, preferred_element_type=jnp.float32)
    summed = (summed / jnp.maximum(land_count, 1.0)[:, None]).astype(jnp.bfloat16)
    joined_field = sharded_from_blocks(summed.reshape(blocks, planes, BR, BW), tile_rows, plane_width)
    plane_bands = lax.dynamic_slice_in_dim(psf_band, slab_index * planes, planes, 0)
    row_taps = row_psf[view_index][plane_bands]
    col_taps = col_psf[view_index][plane_bands]
    across = sharded_column_pass(joined_field, col_taps, False).astype(jnp.bfloat16)
    padded = with_halo(across, (("tile", 1),), radius)
    blurred = row_pass(padded, row_taps, False) + background[view_index]
    ratio_field = (raw_piece.astype(jnp.float32) / blurred).astype(jnp.bfloat16)
    padded_ratio = with_halo(ratio_field, (("tile", 1),), radius)
    rows_back = row_pass(padded_ratio, row_taps, True).astype(jnp.bfloat16)
    spread = sharded_column_pass(rows_back, col_taps, True).astype(jnp.bfloat16)
    returned_blocks = jnp.einsum(
        "bprj,kj->bprk", sharded_to_blocks(spread), matrix, preferred_element_type=jnp.float32
    ).astype(jnp.bfloat16)
    returning = jnp.where(recv_ok[:, None, None, None], returned_blocks[recv_off], zero_bf)
    returning = returning.reshape(tile_count, capacity, planes, BR, BW)
    arrived = lax.all_to_all(returning, "tile", split_axis=0, concat_axis=0, tiled=True)
    arrived = arrived.reshape(tile_count * capacity, planes, BR, BW)
    correction = arrived[my_slots]
    return estimate * sharded_from_blocks(correction.astype(jnp.float32), tile_rows, plane_width)


def local(
    initial_estimate,
    raw_views,
    route_tile,
    route_block,
    interp,
    row_kernel,
    col_kernel,
    psf_band,
    background,
):
    view_count = lax.axis_size("view")
    my_group = lax.axis_index("view")
    my_tile = lax.axis_index("tile")
    planes, tile_rows, plane_width = initial_estimate.shape
    tile_blocks = (tile_rows // BR) * (plane_width // BW)
    row_psf = (row_kernel / jnp.sum(row_kernel, axis=2, keepdims=True)).astype(jnp.bfloat16)
    col_psf = (col_kernel / jnp.sum(col_kernel, axis=2, keepdims=True)).astype(jnp.bfloat16)
    if view_count * tile_rows * plane_width * lax.axis_size("tile") > (1 << 22):
        estimate = initial_estimate
        for update_index in range(view_count):
            view_index = (my_group + update_index) % view_count
            own_piece = lax.dynamic_slice_in_dim(
                raw_views[0], (my_group - update_index) % view_count * planes, planes, 0
            )
            raw_piece = (
                own_piece if update_index == 0 else passed_along(own_piece, "view", -update_index)
            )
            estimate = sharded_update(
                estimate, raw_piece, view_index, my_group, route_tile, route_block,
                interp, row_psf, col_psf, psf_band, background,
            )
        return estimate
    pieces = []
    for update_index in range(view_count):
        own_piece = lax.dynamic_slice_in_dim(
            raw_views[0], (my_group - update_index) % view_count * planes, planes, 0
        )
        piece = own_piece if update_index == 0 else passed_along(own_piece, "view", -update_index)
        if pieces:
            piece, _ = lax.optimization_barrier((piece, pieces[-1]))
        else:
            estimate = lax.all_gather(initial_estimate, "tile", axis=1, tiled=True)
            piece, _ = lax.optimization_barrier((piece, estimate))
        pieces.append(lax.all_gather(piece, "tile", axis=1, tiled=True))
    plane_bands = lax.dynamic_slice_in_dim(psf_band, my_group * planes, planes, 0)
    for update_index in range(view_count):
        view_index = (my_group + update_index) % view_count
        matrix = interp[view_index]
        landing = route_tile[view_index, :, 0] * tile_blocks + route_block[view_index]
        row_taps = row_psf[view_index][plane_bands]
        col_taps = col_psf[view_index][plane_bands]
        level = background[view_index]
        estimate = jnp.stack(
            [
                kernel_update(
                    estimate[p],
                    pieces[update_index][p],
                    matrix,
                    landing,
                    row_taps[p],
                    col_taps[p],
                    level,
                )
                for p in range(planes)
            ]
        )
    return lax.dynamic_slice_in_dim(estimate, my_tile * tile_rows, tile_rows, 1)


def solution(mesh):
    return jax.shard_map(
        local,
        mesh=mesh,
        in_specs=(
            P("view", "tile", None),
            P("view", None, "tile", None),
            P(),
            P(),
            P(),
            P(),
            P(),
            P(),
            P(),
        ),
        out_specs=P("view", "tile", None),
        check_vma=False,
    )
```

profile of v0, /device:TPU:0, one launch (start us, length us, event | category | flops | bytes accessed | tf_op | source)
XLA Modules:
  0.0 208.6 jit_solution(5041300402463132612)
XLA Ops:
  7.4 1.8 dynamic-slice_bitcast_fusion.1
  9.2 3.9 %collective-permute-start = (bf16[1,32,2048]{2,1,0:T(8,128)(2,1)S(1)}, bf16[1,32,2048]{2,1,0:T(8,128)(2,1)S(1)}, u32[]{:S(2)}, u32[]{:S(2)}) collective-permute-start(bf16[1,32,2048]{2,1,0:T(8,128)(2,1)S(1)} %get-tuple-element.110), channel_id=1, source_target_pairs={{0,24},{8,0},{16,8},{24,16},{1,25},{9,1},{17,9},{25,17},{2,26},{10... | collective-permute-start | bytes 393224 | tf_op jit(solution)/shard_map/ppermute | solution.py:15
  14.2 0.9 divide_convert_fusion
  15.0 1.3 dynamic_slice.104
  18.4 0.9 divide_convert_fusion.1
  19.3 0.7 fusion.193
  30.7 0.7 fusion.191
  42.1 0.7 fusion.189
  53.5 0.7 fusion.187
  65.0 0.7 fusion.192
  67.7 0.7 fusion.190
  80.1 0.7 fusion.188
  81.1 10.0 %all-gather.8.cloned.1.call-done = bf16[1,256,2048]{2,1,0:T(8,128)(2,1)} async-done(((bf16[1,32,2048]{2,1,0:T(8,128)(2,1)}), bf16[1,256,2048]{2,1,0:T(8,128)(2,1)}) %all-gather.8.cloned.1.call-update) | async-done | bytes 1048592 | tf_op jit(solution)/shard_map/all_gather | solution.py:398
  91.2 0.7 fusion.186
  128.9 20.7 %all-gather.12.cloned.1.call-done = bf16[1,256,2048]{2,1,0:T(8,128)(2,1)} async-done(((bf16[1,32,2048]{2,1,0:T(8,128)(2,1)}), bf16[1,256,2048]{2,1,0:T(8,128)(2,1)}) %all-gather.12.cloned.1.call-update) | async-done | bytes 1048592 | tf_op jit(solution)/shard_map/all_gather | solution.py:398
  152.1 10.8 %shard_map.91.est_ref = f32[256,2048]{1,0:T(8,128)S(1)} custom-call(f32[256,2048]{1,0:T(8,128)} %bitcast.342, bf16[256,2048]{1,0:T(8,128)(2,1)S(1)} %bitcast.338, bf16[128,128]{1,0:T(8,128)(2,1)S(1)} %bitcast.333, bf16[128,128]{1,0:T(8,128)(2,1)S(1)} %bitcast.337, bf16[512,512]{1,0:T(8,128)(2,1)S(1)} %get-tuple-element.132.s_ref, ...), custom_call_target="tpu_custom_call" | custom-call | flops 2147483648 | bytes 5242880 | tf_op jit(solution)/shard_map/pallas_call | solution.py:171
  162.9 1.3 copy-done.5
  164.4 11.0 %shard_map.92.est_ref = f32[256,2048]{1,0:T(8,128)S(1)} custom-call(f32[256,2048]{1,0:T(8,128)} %copy-done.5, bf16[256,2048]{1,0:T(8,128)(2,1)S(1)} %bitcast.339, bf16[128,128]{1,0:T(8,128)(2,1)S(1)} %bitcast.332, bf16[128,128]{1,0:T(8,128)(2,1)S(1)} %bitcast.336, bf16[512,512]{1,0:T(8,128)(2,1)S(1)} %get-tuple-element.130.s_ref, ...), custom_call_target="tpu_custom_call" | custom-call | flops 2147483648 | bytes 5242880 | tf_op jit(solution)/shard_map/pallas_call | solution.py:171
  175.4 1.3 copy-done.6
  176.9 10.7 %shard_map.93.est_ref = f32[256,2048]{1,0:T(8,128)S(1)} custom-call(f32[256,2048]{1,0:T(8,128)} %copy-done.6, bf16[256,2048]{1,0:T(8,128)(2,1)S(1)} %bitcast.340, bf16[128,128]{1,0:T(8,128)(2,1)S(1)} %bitcast.331, bf16[128,128]{1,0:T(8,128)(2,1)S(1)} %bitcast.335, bf16[512,512]{1,0:T(8,128)(2,1)S(1)} %get-tuple-element.128.s_ref, ...), custom_call_target="tpu_custom_call" | custom-call | flops 2147483648 | bytes 5242880 | tf_op jit(solution)/shard_map/pallas_call | solution.py:171
  187.6 1.3 copy-done.4
  189.1 1.2 copy-done.3
  190.3 11.0 %shard_map.94 = f32[256,2048]{1,0:T(8,128)S(1)} custom-call(f32[256,2048]{1,0:T(8,128)} %copy-done.4, bf16[256,2048]{1,0:T(8,128)(2,1)S(1)} %bitcast.341, bf16[128,128]{1,0:T(8,128)(2,1)S(1)} %bitcast.330, bf16[128,128]{1,0:T(8,128)(2,1)S(1)} %bitcast.334, bf16[512,512]{1,0:T(8,128)(2,1)S(1)} %get-tuple-element.126.s_ref, ...), custom_call_target="tpu_custom_call" | custom-call | flops 2147483648 | bytes 5242880 | tf_op jit(solution)/shard_map/pallas_call | solution.py:171
  201.3 0.7 dynamic-slice_bitcast_fusion
  (131 shorter events, 12.6 us)
Async XLA Ops:
  6.5 61.1 %all-gather.6.cloned.1.call-start = ((), (), s32[]{:S(2)}) async-start(), calls=%async_computation | async-start | bytes 2359296 | tf_op jit(solution)/shard_map/all_gather | solution.py:396
  7.3 83.9 %all-gather.8.cloned.1.call-start = ((), (), s32[]{:S(2)}) async-start(), calls=%async_computation.1 | async-start | bytes 1179648 | tf_op jit(solution)/shard_map/all_gather | solution.py:398
  9.2 82.7 %copy-start.12 = (s32[4,512,1]{1,2,0:T(1,128)S(1)}, s32[4,512,1]{1,2,0:T(1,128)}, u32[]{:S(2)}) copy-start(s32[4,512,1]{1,2,0:T(1,128)} %param.11) | copy-start | bytes 24580
  9.2 82.9 %copy-start.13 = (s32[4,512]{1,0:T(4,128)S(1)}, s32[4,512]{1,0:T(4,128)}, u32[]{:S(2)}) copy-start(s32[4,512]{1,0:T(4,128)} %param.12) | copy-start | bytes 24580
  9.2 71.9 %collective-permute-start = (bf16[1,32,2048]{2,1,0:T(8,128)(2,1)S(1)}, bf16[1,32,2048]{2,1,0:T(8,128)(2,1)S(1)}, u32[]{:S(2)}, u32[]{:S(2)}) collective-permute-start(bf16[1,32,2048]{2,1,0:T(8,128)(2,1)S(1)} %get-tuple-element.110), channel_id=1, source_target_pairs={{0,24},{8,0},{16,8},{24,16},{1,25},{9,1},{17,9},{25,17},{2,26},{10... | collective-permute-start | bytes 393224 | tf_op jit(solution)/shard_map/ppermute | solution.py:15
  13.1 114.0 %collective-permute-start.1 = (bf16[1,32,2048]{2,1,0:T(8,128)(2,1)S(1)}, bf16[1,32,2048]{2,1,0:T(8,128)(2,1)S(1)}, u32[]{:S(2)}, u32[]{:S(2)}) collective-permute-start(bf16[1,32,2048]{2,1,0:T(8,128)(2,1)S(1)} %get-tuple-element.112), channel_id=1, source_target_pairs={{0,16},{8,24},{16,0},{24,8},{1,17},{9,25},{17,1},{25,9},{2,18},{10... | collective-permute-start | bytes 393224 | tf_op jit(solution)/shard_map/ppermute | solution.py:15
  13.6 115.3 %collective-permute-start.2 = (bf16[1,32,2048]{2,1,0:T(8,128)(2,1)S(1)}, bf16[1,32,2048]{2,1,0:T(8,128)(2,1)S(1)}, u32[]{:S(2)}, u32[]{:S(2)}) collective-permute-start(bf16[1,32,2048]{2,1,0:T(8,128)(2,1)S(1)} %get-tuple-element.109), channel_id=1, source_target_pairs={{0,8},{8,16},{16,24},{24,0},{1,9},{9,17},{17,25},{25,1},{2,10},{10... | collective-permute-start | bytes 393224 | tf_op jit(solution)/shard_map/ppermute | solution.py:15
  66.6 60.4 %copy-start.7 = (bf16[4,128,128]{2,1,0:T(8,128)(2,1)S(1)}, bf16[4,128,128]{2,1,0:T(8,128)(2,1)}, u32[]{:S(2)}) copy-start(bf16[4,128,128]{2,1,0:T(8,128)(2,1)} %param.13) | copy-start | bytes 393220
  67.7 59.4 %all-gather.10.cloned.1.call-start = ((), (), s32[]{:S(2)}) async-start(), calls=%async_computation.2 | async-start | bytes 1179648 | tf_op jit(solution)/shard_map/all_gather | solution.py:398
  78.9 71.2 %copy-start.11 = (f32[4]{0:T(128)S(1)}, f32[4]{0:T(128)}, u32[]{:S(2)}) copy-start(f32[4]{0:T(128)} %param.17) | copy-start | bytes 52
  81.1 10.0 %copy-start.10 = (bf16[1,32,2048]{2,1,0:T(8,128)(2,1)}, bf16[1,32,2048]{2,1,0:T(8,128)(2,1)S(1)}, u32[]{:S(2)}) copy-start(bf16[1,32,2048]{2,1,0:T(8,128)(2,1)S(1)} %collective-permute-done) | copy-start | bytes 393220
  91.1 58.5 %all-gather.12.cloned.1.call-start = ((), (), s32[]{:S(2)}) async-start(), calls=%async_computation.3 | async-start | bytes 1179648 | tf_op jit(solution)/shard_map/all_gather | solution.py:398
  127.0 0.7 copy-start.9
  127.7 61.2 %all-gather.14.cloned.1.call-start = ((), (), s32[]{:S(2)}) async-start(), calls=%async_computation.4 | async-start | bytes 1179648 | tf_op jit(solution)/shard_map/all_gather | solution.py:398
  128.9 20.7 %copy-start.8 = (bf16[1,32,2048]{2,1,0:T(8,128)(2,1)}, bf16[1,32,2048]{2,1,0:T(8,128)(2,1)S(1)}, u32[]{:S(2)}) copy-start(bf16[1,32,2048]{2,1,0:T(8,128)(2,1)S(1)} %collective-permute-done.2) | copy-start | bytes 393220
  150.8 1.3 copy-start
  152.1 12.3 %copy-start.1 = (bf16[1,256,2048]{2,1,0:T(8,128)(2,1)S(1)}, bf16[1,256,2048]{2,1,0:T(8,128)(2,1)}, u32[]{:S(2)}) copy-start(bf16[1,256,2048]{2,1,0:T(8,128)(2,1)} %all-gather.10.cloned.1.call-done) | copy-start | bytes 3145732
  162.9 1.3 copy-start.5
  164.4 12.5 %copy-start.2 = (bf16[1,256,2048]{2,1,0:T(8,128)(2,1)S(1)}, bf16[1,256,2048]{2,1,0:T(8,128)(2,1)}, u32[]{:S(2)}) copy-start(bf16[1,256,2048]{2,1,0:T(8,128)(2,1)} %all-gather.12.cloned.1.call-done) | copy-start | bytes 3145732
  175.4 1.3 copy-start.6
  187.6 1.3 copy-start.4
  189.1 1.2 copy-start.3
Sparse Core Ops, SparseCore 0:
  9.0 31.7 all-gather.5
  67.8 23.2 all-gather.7
  92.7 21.7 all-gather.9
  127.8 21.7 all-gather.11
  151.0 21.8 all-gather.13
where the time goes:
time: 210 us; the launch traced here: 209 us
  between operations  101 us (48%)
  Pallas kernels  43.5 us (21%)
  waiting for transfers between devices  31.5 us (15%)
  local copies, waits for them, and re-layouts  18.4 us (9%)
  other arithmetic  8.54 us (4%)
  starting transfers between devices  5.33 us (3%)
    pallas_call x4, Pallas kernels, kernel_update(): pl.pallas_call(plane_kernel, out_shape=jax.ShapeDtypeStruct((rows, plane_...  43.5 us
    all_gather x4, waiting for transfers between devices, local(): pieces.append(lax.all_gather(piece, 'tile', axis=1, tiled=True))  30.7 us
    unnamed x28, local copies, waits for them, and re-layouts  5.87 us
    slice x8, local copies, waits for them, and re-layouts, banded(): taps_in[tap_index].astype(jnp.float32)  5.82 us
    ppermute x3, starting transfers between devices, passed_along(): return lax.ppermute(x, axis, [(i, (i + by) % count) for i in range(count)])  4.99 us
    convert_element_type x32, other arithmetic, banded(): return result.astype(jnp.bfloat16)  4.71 us
  transfers between devices with their start and end apart: 8, of which 2 were waited for; matrix products, arithmetic and copies ran while one was open for 10% of the time, Pallas kernels for 16%

commit v1 on v0

--- a/solution.py
+++ b/solution.py
@@ -154,7 +154,49 @@
         out_ref[:, cols(c)] = est_ref[:, cols(c)] * joined[c]
 
 
-def kernel_update(estimate, raw_plane, matrix, landing, row_taps, col_taps, level):
+def band_kernel(row_ref, col_ref, a_ref, at_ref, bf_ref, bb_ref):
+    count, rows, _ = a_ref.shape
+    radius = (TAPS - 1) // 2
+    out_row = lax.broadcasted_iota(jnp.int32, (rows, rows), 0)
+    src_row = lax.broadcasted_iota(jnp.int32, (rows, rows), 1)
+    source_lane = lax.broadcasted_iota(jnp.int32, (BW, BW), 0)
+    target_lane = lax.broadcasted_iota(jnp.int32, (BW, BW), 1)
+
+    def build(diff, taps_ref, base):
+        result = jnp.zeros(diff.shape, jnp.float32)
+        for tap_index in range(TAPS):
+            result = jnp.where(diff == tap_index, taps_ref[base + tap_index], result)
+        return result.astype(jnp.bfloat16)
+
+    for i in range(count):
+        base = i * TAPS
+        a_ref[i] = build(src_row - out_row + radius, row_ref, base)
+        at_ref[i] = build(out_row - src_row + radius, row_ref, base)
+        for offset in (-1, 0, 1):
+            forward = source_lane + offset * BW - target_lane + radius
+            bf_ref[i, offset + 1] = build(forward, col_ref, base)
+            backward = target_lane - source_lane - offset * BW + radius
+            bb_ref[i, offset + 1] = build(backward, col_ref, base)
+
+
+def all_bands(row_taps, col_taps, rows):
+    count = row_taps.shape[0]
+    smem = pl.BlockSpec(memory_space=pltpu.SMEM)
+    vmem = pl.BlockSpec(memory_space=pltpu.VMEM)
+    return pl.pallas_call(
+        band_kernel,
+        out_shape=(
+            jax.ShapeDtypeStruct((count, rows, rows), jnp.bfloat16),
+            jax.ShapeDtypeStruct((count, rows, rows), jnp.bfloat16),
+            jax.ShapeDtypeStruct((count, 3, BW, BW), jnp.bfloat16),
+            jax.ShapeDtypeStruct((count, 3, BW, BW), jnp.bfloat16),
+        ),
+        in_specs=[smem, smem],
+        out_specs=(vmem, vmem, vmem, vmem),
+    )(row_taps.astype(jnp.float32).reshape(-1), col_taps.astype(jnp.float32).reshape(-1))
+
+
+def kernel_update(estimate, raw_plane, matrix, landing, bands, level):
     rows, plane_width = estimate.shape
     nt = rows // BR
     nc = plane_width // BW
@@ -166,7 +208,6 @@
     pick_mat = place[:, None] == spots[None, :]
     count = jnp.sum(sum_mat.astype(jnp.float32), axis=1)
     count = jnp.broadcast_to(jnp.maximum(count, 1.0)[:, None], (blocks, BW))
-    band = row_mat(row_taps, rows)
     vmem = pl.BlockSpec(memory_space=pltpu.VMEM)
     return pl.pallas_call(
         plane_kernel,
@@ -193,10 +234,10 @@
         sum_mat.astype(jnp.bfloat16),
         count,
         pick_mat.astype(jnp.bfloat16),
-        jnp.stack(column_mats(col_taps, False)),
-        jnp.stack(column_mats(col_taps, True)),
-        band,
-        band.T,
+        bands[2],
+        bands[3],
+        bands[0],
+        bands[1],
         jnp.reshape(level, (1,)).astype(jnp.float32),
     )
 
@@ -392,17 +433,19 @@
         piece = own_piece if update_index == 0 else passed_along(own_piece, "view", -update_index)
         if pieces:
             piece, _ = lax.optimization_barrier((piece, pieces[-1]))
-        else:
-            estimate = lax.all_gather(initial_estimate, "tile", axis=1, tiled=True)
-            piece, _ = lax.optimization_barrier((piece, estimate))
         pieces.append(lax.all_gather(piece, "tile", axis=1, tiled=True))
+    estimate = lax.all_gather(initial_estimate, "tile", axis=1, tiled=True)
     plane_bands = lax.dynamic_slice_in_dim(psf_band, my_group * planes, planes, 0)
+    views_in_order = (my_group + jnp.arange(view_count, dtype=jnp.int32)) % view_count
+    bands = all_bands(
+        row_psf[views_in_order][:, plane_bands].reshape(view_count * planes, TAPS),
+        col_psf[views_in_order][:, plane_bands].reshape(view_count * planes, TAPS),
+        tile_rows * lax.axis_size("tile"),
+    )
     for update_index in range(view_count):
         view_index = (my_group + update_index) % view_count
         matrix = interp[view_index]
         landing = route_tile[view_index, :, 0] * tile_blocks + route_block[view_index]
-        row_taps = row_psf[view_index][plane_bands]
-        col_taps = col_psf[view_index][plane_bands]
         level = background[view_index]
         estimate = jnp.stack(
             [
@@ -411,8 +454,7 @@
                     pieces[update_index][p],
                     matrix,
                     landing,
-                    row_taps[p],
-                    col_taps[p],
+                    [b[update_index * planes + p] for b in bands],
                     level,
                 )
                 for p in range(planes)

time: 210 us -> 183 us (0.87)
  between operations: 101 us -> 15.4 us
  waiting for transfers between devices: 31.5 us -> 74.5 us
  local copies, waits for them, and re-layouts: 18.4 us -> 31.7 us
  Pallas kernels: 43.5 us -> 48.6 us
  other arithmetic: 8.54 us -> 4.37 us
    all_gather x1, waiting for transfers between devices: 0.02 us -> 30.2 us  [local(): estimate = lax.all_gather(initial_estimate, 'tile', axis=1, tiled=True)]
    unnamed x28 -> x74, local copies, waits for them, and re-layouts: 5.87 us -> 13.6 us
    all_gather x4, waiting for transfers between devices: 30.7 us -> 37.4 us  [local(): pieces.append(lax.all_gather(piece, 'tile', axis=1, tiled=True))]
    squeeze x0 -> x4, local copies, waits for them, and re-layouts: none -> 6.34 us  [local(): b[update_index * planes + p]]
    ppermute x3, waiting for transfers between devices: 0.01 us -> 6.17 us  [passed_along(): return lax.ppermute(x, axis, [(i, (i + by) % count) for i in range(count)])]
    slice x8 -> x0, local copies, waits for them, and re-layouts: 5.82 us -> none  [banded(): taps_in[tap_index].astype(jnp.float32)]
    pallas_call x0 -> x1, Pallas kernels: none -> 5.05 us  [all_bands(): pl.pallas_call(band_kernel, out_shape=(jax.ShapeDtypeStruct((count, rows,...]
    convert_element_type x32 -> x1, other arithmetic: 4.71 us -> 0.03 us  [all_bands(): row_taps.astype(jnp.float32).reshape(-1)]
  transfers between devices with their start and end apart: 8 -> 8, of which waited for: 2 -> 6; matrix products, arithmetic and copies ran while one was open for 10% -> 11% of each run, Pallas kernels for 16% -> 21%
where the time goes in v1:
time: 183 us; the launch traced here: 182 us
  waiting for transfers between devices  74.5 us (41%)
  Pallas kernels  48.6 us (27%)
  local copies, waits for them, and re-layouts  31.7 us (17%)
  between operations  15.4 us (8%)
  starting transfers between devices  7.18 us (4%)
  other arithmetic  4.37 us (2%)
    pallas_call x4, Pallas kernels, kernel_update(): pl.pallas_call(plane_kernel, out_shape=jax.ShapeDtypeStruct((rows, plane_...  43.6 us
    all_gather x4, waiting for transfers between devices, local(): pieces.append(lax.all_gather(piece, 'tile', axis=1, tiled=True))  37.4 us
    all_gather x1, waiting for transfers between devices, local(): estimate = lax.all_gather(initial_estimate, 'tile', axis=1, tiled=True)  30.2 us
    unnamed x74, local copies, waits for them, and re-layouts  13.6 us
    ppermute x3, starting transfers between devices, passed_along(): return lax.ppermute(x, axis, [(i, (i + by) % count) for i in range(count)])  7.02 us
    squeeze x4, local copies, waits for them, and re-layouts, local(): b[update_index * planes + p]  6.34 us
    ppermute x3, waiting for transfers between devices, passed_along(): return lax.ppermute(x, axis, [(i, (i + by) % count) for i in range(count)])  6.17 us
    pallas_call x1, Pallas kernels, all_bands(): pl.pallas_call(band_kernel, out_shape=(jax.ShapeDtypeStruct((count, rows,...  5.05 us
  transfers between devices with their start and end apart: 8, of which 6 were waited for; matrix products, arithmetic and copies ran while one was open for 11% of the time, Pallas kernels for 21%

profile of v1, /device:TPU:0, one launch (start us, length us, event | category | flops | bytes accessed | tf_op | source)
XLA Modules:
  0.0 181.7 jit_solution(17012437345833434940)
XLA Ops:
  6.5 1.8 %dynamic-slice_bitcast_fusion.1 = (bf16[1,32,2048]{2,1,0:T(8,128)(2,1)S(1)}, bf16[1,32,2048]{2,1,0:T(8,128)(2,1)S(1)}, bf16[1,1,32,2048]{3,2,1,0:T(8,128)(2,1)}, bf16[1,32,2048]{2,1,0:T(8,128)(2,1)S(1)}) fusion(bf16[1,4,32,2048]{3,2,1,0:T(8,128)(2,1)} %param.10, s32[]{:T(128)S(6)} %select_n.218, s32[]{:T(128)S(6)} %select_n.206, s32[]{:T(128)S(6)} %select_n.198, ...), kind=kLoop, calls=%fused_computation.31 | loop fusion | bytes 1048592 | tf_op jit(solution)/shard_map/dynamic_slice | solution.py:430
  8.4 3.9 %collective-permute-start = (bf16[1,32,2048]{2,1,0:T(8,128)(2,1)S(1)}, bf16[1,32,2048]{2,1,0:T(8,128)(2,1)S(1)}, u32[]{:S(2)}, u32[]{:S(2)}) collective-permute-start(bf16[1,32,2048]{2,1,0:T(8,128)(2,1)S(1)} %get-tuple-element.58), channel_id=1, source_target_pairs={{0,24},{8,0},{16,8},{24,16},{1,25},{9,1},{17,9},{25,17},{2,26},{10... | collective-permute-start | bytes 393224 | tf_op jit(solution)/shard_map/ppermute | solution.py:15
  12.3 2.8 %collective-permute-done = bf16[1,32,2048]{2,1,0:T(8,128)(2,1)S(1)} collective-permute-done((bf16[1,32,2048]{2,1,0:T(8,128)(2,1)S(1)}, bf16[1,32,2048]{2,1,0:T(8,128)(2,1)S(1)}, u32[]{:S(2)}, u32[]{:S(2)}) %collective-permute-start) | collective-permute-done | bytes 131104 | tf_op jit(solution)/shard_map/ppermute | solution.py:15
  15.7 1.6 collective-permute-start.1
  17.4 3.4 %collective-permute-done.1 = bf16[1,32,2048]{2,1,0:T(8,128)(2,1)S(1)} collective-permute-done((bf16[1,32,2048]{2,1,0:T(8,128)(2,1)S(1)}, bf16[1,32,2048]{2,1,0:T(8,128)(2,1)S(1)}, u32[]{:S(2)}, u32[]{:S(2)}) %collective-permute-start.1) | collective-permute-done | bytes 131104 | tf_op jit(solution)/shard_map/ppermute | solution.py:15
  20.8 19.4 %all-gather.9.cloned.1.call-done = bf16[1,256,2048]{2,1,0:T(8,128)(2,1)} async-done(((bf16[1,32,2048]{2,1,0:T(8,128)(2,1)}), bf16[1,256,2048]{2,1,0:T(8,128)(2,1)}) %all-gather.9.cloned.1.call-update) | async-done | bytes 1048592 | tf_op jit(solution)/shard_map/all_gather | solution.py:436
  40.9 1.5 collective-permute-start.2
  50.5 5.0 %shard_map.91 = (bf16[4,256,256]{2,1,0:T(8,128)(2,1)}, bf16[4,256,256]{2,1,0:T(8,128)(2,1)}, bf16[4,3,128,128]{3,2,1,0:T(8,128)(2,1)}, bf16[4,3,128,128]{3,2,1,0:T(8,128)(2,1)}) custom-call(f32[68]{0:T(128)} %reshape.562.row_ref, f32[68]{0:T(128)} %reshape.563.col_ref), custom_call_target="tpu_custom_call" | custom-call | tf_op jit(solution)/shard_map/pallas_call | solution.py:186
  56.2 1.8 %slice_bitcast_fusion.8 = (bf16[3,128,128]{2,1,0:T(8,128)(2,1)}, bf16[3,128,128]{2,1,0:T(8,128)(2,1)}, bf16[3,128,128]{2,1,0:T(8,128)(2,1)}, bf16[3,128,128]{2,1,0:T(8,128)(2,1)}) fusion(bf16[4,3,128,128]{3,2,1,0:T(8,128)(2,1)} %get-tuple-element.13), kind=kLoop, calls=%fused_computation.40 | loop fusion | bytes 786432 | tf_op jit(solution)/shard_map/squeeze | solution.py:457
  58.0 1.8 slice_bitcast_fusion.9
  59.8 1.9 %slice_bitcast_fusion = (bf16[256,256]{1,0:T(8,128)(2,1)S(1)}, bf16[256,256]{1,0:T(8,128)(2,1)}, bf16[256,256]{1,0:T(8,128)(2,1)}, bf16[256,256]{1,0:T(8,128)(2,1)}) fusion(bf16[4,256,256]{2,1,0:T(8,128)(2,1)} %get-tuple-element.15), kind=kLoop, calls=%fused_computation.29 | loop fusion | bytes 1048576 | tf_op jit(solution)/shard_map/squeeze | solution.py:457
  67.8 1.1 fusion.10
  69.8 17.2 %all-gather.15.cloned.1.call-done = bf16[1,1,256,2048]{3,2,1,0:T(8,128)(2,1)} async-done(((bf16[1,1,32,2048]{3,2,1,0:T(8,128)(2,1)}), bf16[1,1,256,2048]{3,2,1,0:T(8,128)(2,1)}) %all-gather.15.cloned.1.call-update) | async-done | bytes 1048592 | tf_op jit(solution)/shard_map/all_gather | solution.py:436
  86.9 30.2 %all-gather.7.cloned.1.call-done = f32[1,256,2048]{2,1,0:T(8,128)} async-done(((f32[1,32,2048]{2,1,0:T(8,128)}), f32[1,256,2048]{2,1,0:T(8,128)}) %all-gather.7.cloned.1.call-update) | async-done | bytes 2097168 | tf_op jit(solution)/shard_map/all_gather | solution.py:437
  118.3 1.0 copy-done.1
  123.7 1.2 copy-done.22
  125.0 11.0 %shard_map.92.est_ref = f32[256,2048]{1,0:T(8,128)S(1)} custom-call(f32[256,2048]{1,0:T(8,128)} %bitcast.86, bf16[256,2048]{1,0:T(8,128)(2,1)S(1)} %bitcast.84, bf16[128,128]{1,0:T(8,128)(2,1)S(1)} %bitcast.77, bf16[128,128]{1,0:T(8,128)(2,1)S(1)} %bitcast.81, bf16[512,512]{1,0:T(8,128)(2,1)S(1)} %copy-done.1, f32[512,128]{1,0:T(8,128)S(1)} %broadcast_in_dim.10.cnt_ref, ...), custom_call_target="tpu_custom_call" | custom-call | flops 2147483648 | bytes 5242880 | tf_op jit(solution)/shard_map/pallas_call | solution.py:212
  136.0 1.3 copy-done.25
  137.6 10.9 %shard_map.93.est_ref = f32[256,2048]{1,0:T(8,128)S(1)} custom-call(f32[256,2048]{1,0:T(8,128)} %copy-done.25, bf16[256,2048]{1,0:T(8,128)(2,1)S(1)} %bitcast.82, bf16[128,128]{1,0:T(8,128)(2,1)S(1)} %bitcast.76, bf16[128,128]{1,0:T(8,128)(2,1)S(1)} %bitcast.80, bf16[512,512]{1,0:T(8,128)(2,1)S(1)} %get-tuple-element.78.s_ref, ...), custom_call_target="tpu_custom_call" | custom-call | flops 2147483648 | bytes 5242880 | tf_op jit(solution)/shard_map/pallas_call | solution.py:212
  148.6 1.3 copy-done.26
  150.1 10.9 %shard_map.94.est_ref = f32[256,2048]{1,0:T(8,128)S(1)} custom-call(f32[256,2048]{1,0:T(8,128)} %copy-done.26, bf16[256,2048]{1,0:T(8,128)(2,1)S(1)} %bitcast.83, bf16[128,128]{1,0:T(8,128)(2,1)S(1)} %bitcast.75, bf16[128,128]{1,0:T(8,128)(2,1)S(1)} %bitcast.79, bf16[512,512]{1,0:T(8,128)(2,1)S(1)} %get-tuple-element.76.s_ref, ...), custom_call_target="tpu_custom_call" | custom-call | flops 2147483648 | bytes 5242880 | tf_op jit(solution)/shard_map/pallas_call | solution.py:212
  161.0 1.3 copy-done.24
  162.5 1.2 copy-done.23
  163.8 10.7 %shard_map.95 = f32[256,2048]{1,0:T(8,128)S(1)} custom-call(f32[256,2048]{1,0:T(8,128)} %copy-done.24, bf16[256,2048]{1,0:T(8,128)(2,1)S(1)} %bitcast.85, bf16[128,128]{1,0:T(8,128)(2,1)S(1)} %bitcast.74, bf16[128,128]{1,0:T(8,128)(2,1)S(1)} %bitcast.78, bf16[512,512]{1,0:T(8,128)(2,1)S(1)} %get-tuple-element.74.s_ref, ...), custom_call_target="tpu_custom_call" | custom-call | flops 2147483648 | bytes 5242880 | tf_op jit(solution)/shard_map/pallas_call | solution.py:212
  (138 shorter events, 21.9 us)
Async XLA Ops:
  6.5 38.3 %copy-start.36 = (s32[4]{0:T(128)S(1)}, s32[4]{0:T(128)}, u32[]{:S(2)}) copy-start(s32[4]{0:T(128)} %param.16) | copy-start | bytes 52
  6.5 40.1 %copy-start.34 = (f32[4,4,17]{2,1,0:T(4,128)S(1)}, f32[4,4,17]{2,1,0:T(4,128)}, u32[]{:S(2)}) copy-start(f32[4,4,17]{2,1,0:T(4,128)} %param.14) | copy-start | bytes 3268
  6.5 40.8 %copy-start.35 = (f32[4,4,17]{2,1,0:T(4,128)S(1)}, f32[4,4,17]{2,1,0:T(4,128)}, u32[]{:S(2)}) copy-start(f32[4,4,17]{2,1,0:T(4,128)} %param.15) | copy-start | bytes 3268
  6.5 33.6 %all-gather.9.cloned.1.call-start = ((), (), s32[]{:S(2)}) async-start(), calls=%async_computation.1 | async-start | bytes 1179648 | tf_op jit(solution)/shard_map/all_gather | solution.py:436
  8.4 6.7 %collective-permute-start = (bf16[1,32,2048]{2,1,0:T(8,128)(2,1)S(1)}, bf16[1,32,2048]{2,1,0:T(8,128)(2,1)S(1)}, u32[]{:S(2)}, u32[]{:S(2)}) collective-permute-start(bf16[1,32,2048]{2,1,0:T(8,128)(2,1)S(1)} %get-tuple-element.58), channel_id=1, source_target_pairs={{0,24},{8,0},{16,8},{24,16},{1,25},{9,1},{17,9},{25,17},{2,26},{10... | collective-permute-start | bytes 393224 | tf_op jit(solution)/shard_map/ppermute | solution.py:15
  15.7 47.9 %all-gather.11.cloned.1.call-start = ((), (), s32[]{:S(2)}) async-start(), calls=%async_computation.2 | async-start | bytes 1179648 | tf_op jit(solution)/shard_map/all_gather | solution.py:436
  15.7 5.0 %collective-permute-start.1 = (bf16[1,32,2048]{2,1,0:T(8,128)(2,1)S(1)}, bf16[1,32,2048]{2,1,0:T(8,128)(2,1)S(1)}, u32[]{:S(2)}, u32[]{:S(2)}) collective-permute-start(bf16[1,32,2048]{2,1,0:T(8,128)(2,1)S(1)} %get-tuple-element.60), channel_id=1, source_target_pairs={{0,16},{8,24},{16,0},{24,8},{1,17},{9,25},{17,1},{25,9},{2,18},{10... | collective-permute-start | bytes 393224 | tf_op jit(solution)/shard_map/ppermute | solution.py:15
  20.8 19.4 %copy-start.30 = (bf16[1,32,2048]{2,1,0:T(8,128)(2,1)}, bf16[1,32,2048]{2,1,0:T(8,128)(2,1)S(1)}, u32[]{:S(2)}) copy-start(bf16[1,32,2048]{2,1,0:T(8,128)(2,1)S(1)} %collective-permute-done.1) | copy-start | bytes 393220
  40.2 46.8 %all-gather.15.cloned.1.call-start = ((), (), s32[]{:S(2)}) async-start(), calls=%async_computation.4 | async-start | bytes 1179648 | tf_op jit(solution)/shard_map/all_gather | solution.py:436
  40.9 76.2 %all-gather.7.cloned.1.call-start = ((), (), s32[]{:S(2)}) async-start(), calls=%async_computation | async-start | bytes 2359296 | tf_op jit(solution)/shard_map/all_gather | solution.py:437
  40.9 21.7 %collective-permute-start.2 = (bf16[1,32,2048]{2,1,0:T(8,128)(2,1)S(1)}, bf16[1,32,2048]{2,1,0:T(8,128)(2,1)S(1)}, u32[]{:S(2)}, u32[]{:S(2)}) collective-permute-start(bf16[1,32,2048]{2,1,0:T(8,128)(2,1)S(1)} %get-tuple-element.57), channel_id=1, source_target_pairs={{0,8},{8,16},{16,24},{24,0},{1,9},{9,17},{17,25},{25,1},{2,10},{10... | collective-permute-start | bytes 393224 | tf_op jit(solution)/shard_map/ppermute | solution.py:15
  42.5 119.9 %all-gather.13.cloned.1.call-start = ((), (), s32[]{:S(2)}) async-start(), calls=%async_computation.3 | async-start | bytes 1179648 | tf_op jit(solution)/shard_map/all_gather | solution.py:436
  47.3 16.3 %copy-start.28 = (bf16[4,128,128]{2,1,0:T(8,128)(2,1)S(1)}, bf16[4,128,128]{2,1,0:T(8,128)(2,1)}, u32[]{:S(2)}) copy-start(bf16[4,128,128]{2,1,0:T(8,128)(2,1)} %param.13) | copy-start | bytes 393220
  125.0 12.5 %copy-start.4 = (bf16[256,256]{1,0:T(8,128)(2,1)S(1)}, bf16[256,256]{1,0:T(8,128)(2,1)}, u32[]{:S(2)}) copy-start(bf16[256,256]{1,0:T(8,128)(2,1)} %get-tuple-element.51.at_ref) | copy-start | bytes 393220
  125.0 12.5 %copy-start.5 = (bf16[256,256]{1,0:T(8,128)(2,1)S(1)}, bf16[256,256]{1,0:T(8,128)(2,1)}, u32[]{:S(2)}) copy-start(bf16[256,256]{1,0:T(8,128)(2,1)} %get-tuple-element.55.a_ref) | copy-start | bytes 393220
  125.0 12.5 %copy-start.12 = (bf16[3,128,128]{2,1,0:T(8,128)(2,1)S(1)}, bf16[3,128,128]{2,1,0:T(8,128)(2,1)}, u32[]{:S(2)}) copy-start(bf16[3,128,128]{2,1,0:T(8,128)(2,1)} %get-tuple-element.63.bb_ref) | copy-start | bytes 294916
  125.0 12.5 %copy-start.13 = (bf16[3,128,128]{2,1,0:T(8,128)(2,1)S(1)}, bf16[3,128,128]{2,1,0:T(8,128)(2,1)}, u32[]{:S(2)}) copy-start(bf16[3,128,128]{2,1,0:T(8,128)(2,1)} %get-tuple-element.67.bf_ref) | copy-start | bytes 294916
  125.0 12.6 %copy-start.18 = (bf16[1,128,128]{1,2,0:T(8,128)(2,1)S(1)}, bf16[1,128,128]{1,2,0:T(8,128)(2,1)}, u32[]{:S(2)}) copy-start(bf16[1,128,128]{1,2,0:T(8,128)(2,1)} %copy.21) | copy-start | bytes 98308
  125.0 12.6 %copy-start.20 = (bf16[1,256,2048]{2,1,0:T(8,128)(2,1)S(1)}, bf16[1,256,2048]{2,1,0:T(8,128)(2,1)}, u32[]{:S(2)}) copy-start(bf16[1,256,2048]{2,1,0:T(8,128)(2,1)} %all-gather.9.cloned.1.call-done) | copy-start | bytes 3145732
  137.6 12.5 %copy-start.2 = (bf16[256,256]{1,0:T(8,128)(2,1)S(1)}, bf16[256,256]{1,0:T(8,128)(2,1)}, u32[]{:S(2)}) copy-start(bf16[256,256]{1,0:T(8,128)(2,1)} %get-tuple-element.50.at_ref) | copy-start | bytes 393220
  137.6 12.5 %copy-start.3 = (bf16[256,256]{1,0:T(8,128)(2,1)S(1)}, bf16[256,256]{1,0:T(8,128)(2,1)}, u32[]{:S(2)}) copy-start(bf16[256,256]{1,0:T(8,128)(2,1)} %get-tuple-element.54.a_ref) | copy-start | bytes 393220
  137.6 12.5 %copy-start.10 = (bf16[3,128,128]{2,1,0:T(8,128)(2,1)S(1)}, bf16[3,128,128]{2,1,0:T(8,128)(2,1)}, u32[]{:S(2)}) copy-start(bf16[3,128,128]{2,1,0:T(8,128)(2,1)} %get-tuple-element.62.bb_ref) | copy-start | bytes 294916
  137.6 12.5 %copy-start.11 = (bf16[3,128,128]{2,1,0:T(8,128)(2,1)S(1)}, bf16[3,128,128]{2,1,0:T(8,128)(2,1)}, u32[]{:S(2)}) copy-start(bf16[3,128,128]{2,1,0:T(8,128)(2,1)} %get-tuple-element.66.bf_ref) | copy-start | bytes 294916
  137.6 12.5 %copy-start.17 = (bf16[1,128,128]{1,2,0:T(8,128)(2,1)S(1)}, bf16[1,128,128]{1,2,0:T(8,128)(2,1)}, u32[]{:S(2)}) copy-start(bf16[1,128,128]{1,2,0:T(8,128)(2,1)} %copy.24) | copy-start | bytes 98308
  (21 other events, 93.0 us)
Sparse Core Ops, SparseCore 0:
  15.8 24.2 all-gather.8
  41.7 21.7 all-gather.10
  65.2 21.7 all-gather.14
  88.4 28.7 all-gather.6
  118.6 21.5 all-gather.12

commit v2 on v1

--- a/solution.py
+++ b/solution.py
@@ -431,10 +431,15 @@
             raw_views[0], (my_group - update_index) % view_count * planes, planes, 0
         )
         piece = own_piece if update_index == 0 else passed_along(own_piece, "view", -update_index)
-        if pieces:
-            piece, _ = lax.optimization_barrier((piece, pieces[-1]))
-        pieces.append(lax.all_gather(piece, "tile", axis=1, tiled=True))
-    estimate = lax.all_gather(initial_estimate, "tile", axis=1, tiled=True)
+        pieces.append(piece)
+    pieces = lax.all_gather(jnp.stack(pieces), "tile", axis=2, tiled=True)
+    tile_count = lax.axis_size("tile")
+    arrived = [initial_estimate] + [
+        passed_along(initial_estimate, "tile", shift) for shift in range(1, tile_count)
+    ]
+    source_order = (my_tile - jnp.arange(tile_count, dtype=jnp.int32)) % tile_count
+    estimate = jnp.take(jnp.stack(arrived), source_order, axis=0)
+    estimate = jnp.swapaxes(estimate, 0, 1).reshape(planes, tile_count * tile_rows, plane_width)
     plane_bands = lax.dynamic_slice_in_dim(psf_band, my_group * planes, planes, 0)
     views_in_order = (my_group + jnp.arange(view_count, dtype=jnp.int32)) % view_count
     bands = all_bands(

time: 183 us -> 161 us (0.88)
  the two profiles are of different devices: /device:TPU:0 before, /device:TPU:9 now
where the time goes in v2:
time: 161 us; the launch traced here: 160 us
  Pallas kernels  48.4 us (30%)
  local copies, waits for them, and re-layouts  40.8 us (25%)
  waiting for transfers between devices  32.4 us (20%)
  between operations  15.9 us (10%)
  starting transfers between devices  12.3 us (8%)
  other arithmetic  10.6 us (7%)
    pallas_call x4, Pallas kernels, kernel_update(): pl.pallas_call(plane_kernel, out_shape=jax.ShapeDtypeStruct((rows, plane_...  43.4 us
    ppermute x10, waiting for transfers between devices, passed_along(): return lax.ppermute(x, axis, [(i, (i + by) % count) for i in range(count)])  32.3 us
    unnamed x63, local copies, waits for them, and re-layouts  14.8 us
    ppermute x10, starting transfers between devices, passed_along(): return lax.ppermute(x, axis, [(i, (i + by) % count) for i in range(count)])  12.3 us
    squeeze x4, local copies, waits for them, and re-layouts, local(): b[update_index * planes + p]  6.21 us
    pallas_call x1, Pallas kernels, all_bands(): pl.pallas_call(band_kernel, out_shape=(jax.ShapeDtypeStruct((count, rows,...  5 us
    gather x1, local copies, waits for them, and re-layouts, local(): estimate = jnp.take(jnp.stack(arrived), source_order, axis=0)  3.74 us
    dynamic_slice x5, local copies, waits for them, and re-layouts, local(): matrix = interp[view_index]  3.65 us
  transfers between devices with their start and end apart: 11, of which 3 were waited for; matrix products, arithmetic and copies ran while one was open for 27% of the time, Pallas kernels for 3%

profile of v2, /device:TPU:9, one launch (start us, length us, event | category | flops | bytes accessed | tf_op | source)
XLA Modules:
  0.0 160.3 jit_solution(13250614848547982625)
XLA Ops:
  6.5 1.9 %collective-permute-start = (f32[1,32,2048]{2,1,0:T(8,128)}, f32[1,32,2048]{2,1,0:T(8,128)}, u32[]{:S(2)}, u32[]{:S(2)}) collective-permute-start(f32[1,32,2048]{2,1,0:T(8,128)} %param.9), channel_id=1, source_target_pairs={{0,1},{1,2},{2,3},{3,4},{4,5},{5,6},{6,7},{7,0},{8,9},{9,10},{10,1... | collective-permute-start | bytes 786440 | tf_op jit(solution)/shard_map/ppermute | solution.py:15
  22.1 1.4 collective-permute-start.3
  30.1 5.0 %shard_map.91 = (bf16[4,256,256]{2,1,0:T(8,128)(2,1)}, bf16[4,256,256]{2,1,0:T(8,128)(2,1)}, bf16[4,3,128,128]{3,2,1,0:T(8,128)(2,1)}, bf16[4,3,128,128]{3,2,1,0:T(8,128)(2,1)}) custom-call(f32[68]{0:T(128)} %reshape.621.row_ref, f32[68]{0:T(128)} %reshape.622.col_ref), custom_call_target="tpu_custom_call" | custom-call | tf_op jit(solution)/shard_map/pallas_call | solution.py:186
  35.9 1.8 %slice_bitcast_fusion.13 = (bf16[3,128,128]{2,1,0:T(8,128)(2,1)}, bf16[3,128,128]{2,1,0:T(8,128)(2,1)}, bf16[3,128,128]{2,1,0:T(8,128)(2,1)}, bf16[3,128,128]{2,1,0:T(8,128)(2,1)}) fusion(bf16[4,3,128,128]{3,2,1,0:T(8,128)(2,1)} %get-tuple-element.9), kind=kLoop, calls=%fused_computation.56 | loop fusion | bytes 786432 | tf_op jit(solution)/shard_map/squeeze | solution.py:462
  37.7 1.8 %slice_bitcast_fusion.12 = (bf16[3,128,128]{2,1,0:T(8,128)(2,1)}, bf16[3,128,128]{2,1,0:T(8,128)(2,1)}, bf16[3,128,128]{2,1,0:T(8,128)(2,1)}, bf16[3,128,128]{2,1,0:T(8,128)(2,1)}) fusion(bf16[4,3,128,128]{3,2,1,0:T(8,128)(2,1)} %get-tuple-element.10), kind=kLoop, calls=%fused_computation.55 | loop fusion | bytes 786432 | tf_op jit(solution)/shard_map/squeeze | solution.py:462
  39.5 1.8 %slice_bitcast_fusion.5 = (bf16[256,256]{1,0:T(8,128)(2,1)S(1)}, bf16[256,256]{1,0:T(8,128)(2,1)}, bf16[256,256]{1,0:T(8,128)(2,1)}, bf16[256,256]{1,0:T(8,128)(2,1)}) fusion(bf16[4,256,256]{2,1,0:T(8,128)(2,1)} %get-tuple-element.11), kind=kLoop, calls=%fused_computation.45 | loop fusion | bytes 1048576 | tf_op jit(solution)/shard_map/squeeze | solution.py:462
  43.8 1.7 %bitcast_dynamic-update-slice_fusion.7 = f32[8,1,32,2048]{3,2,1,0:T(8,128)} fusion(f32[1,32,2048]{2,1,0:T(8,128)} %param.9), kind=kLoop, calls=%fused_computation.42 | loop fusion | bytes 524288
  51.2 1.7 %bitcast_dynamic-update-slice_fusion.6 = f32[8,1,32,2048]{3,2,1,0:T(8,128)} fusion(f32[8,1,32,2048]{3,2,1,0:T(8,128)} %bitcast_dynamic-update-slice_fusion.7, f32[1,32,2048]{2,1,0:T(8,128)} %collective-permute-done), kind=kLoop, calls=%fused_computation.41 | loop fusion | bytes 524288
  54.2 1.7 %bitcast_dynamic-update-slice_fusion.5 = f32[8,1,32,2048]{3,2,1,0:T(8,128)} fusion(f32[8,1,32,2048]{3,2,1,0:T(8,128)} %bitcast_dynamic-update-slice_fusion.6, f32[1,32,2048]{2,1,0:T(8,128)} %collective-permute-done.1), kind=kLoop, calls=%fused_computation.40 | loop fusion | bytes 524288
  55.8 1.7 %bitcast_dynamic-update-slice_fusion.4 = f32[8,1,32,2048]{3,2,1,0:T(8,128)} fusion(f32[8,1,32,2048]{3,2,1,0:T(8,128)} %bitcast_dynamic-update-slice_fusion.5, f32[1,32,2048]{2,1,0:T(8,128)} %collective-permute-done.2), kind=kLoop, calls=%fused_computation.39 | loop fusion | bytes 524288
  57.5 20.1 %collective-permute-done.3 = f32[1,32,2048]{2,1,0:T(8,128)} collective-permute-done((f32[1,32,2048]{2,1,0:T(8,128)}, f32[1,32,2048]{2,1,0:T(8,128)}, u32[]{:S(2)}, u32[]{:S(2)}) %collective-permute-start.3) | collective-permute-done | bytes 262176 | tf_op jit(solution)/shard_map/ppermute | solution.py:15
  77.6 1.7 %bitcast_dynamic-update-slice_fusion.3 = f32[8,1,32,2048]{3,2,1,0:T(8,128)} fusion(f32[8,1,32,2048]{3,2,1,0:T(8,128)} %bitcast_dynamic-update-slice_fusion.4, f32[1,32,2048]{2,1,0:T(8,128)} %collective-permute-done.3), kind=kLoop, calls=%fused_computation.38 | loop fusion | bytes 524288
  79.2 1.7 %bitcast_dynamic-update-slice_fusion.2 = f32[8,1,32,2048]{3,2,1,0:T(8,128)} fusion(f32[8,1,32,2048]{3,2,1,0:T(8,128)} %bitcast_dynamic-update-slice_fusion.3, f32[1,32,2048]{2,1,0:T(8,128)} %collective-permute-done.4), kind=kLoop, calls=%fused_computation.37 | loop fusion | bytes 524288
  80.9 12.1 %collective-permute-done.5 = f32[1,32,2048]{2,1,0:T(8,128)S(1)} collective-permute-done((f32[1,32,2048]{2,1,0:T(8,128)}, f32[1,32,2048]{2,1,0:T(8,128)S(1)}, u32[]{:S(2)}, u32[]{:S(2)}) %collective-permute-start.5) | collective-permute-done | bytes 262176 | tf_op jit(solution)/shard_map/ppermute | solution.py:15
  94.6 3.7 %gather_fusion = f32[8,32,2048]{2,1,0:T(8,128)} fusion(f32[8,32,2048]{2,1,0:T(8,128)} %bitcast.111, s32[1024]{0:T(1024)} %pad_clamp_fusion.1), kind=kCustom, calls=%fused_computation | custom fusion | bytes 4194336 | tf_op jit(solution)/shard_map/jit(_take)/gather | solution.py:441
  98.4 3.1 %bitcast_select_fusion.est_ref = f32[256,2048]{1,0:T(8,128)} fusion(f32[8,32,2048]{2,1,0:T(8,128)} %gather_fusion, pred[256]{0:T(512)(128)(4,1)S(1)} %copy-done.26), kind=kLoop, calls=%fused_computation.5 | loop fusion | flops 524288 | bytes 4194560 | tf_op jit(solution)/shard_map/jit(_take)/select_n | solution.py:441
  101.5 2.9 %slice_bitcast_fusion = (bf16[256,2048]{1,0:T(8,128)(2,1)S(1)}, bf16[256,2048]{1,0:T(8,128)(2,1)S(1)}, bf16[256,2048]{1,0:T(8,128)(2,1)S(1)}, bf16[256,2048]{1,0:T(8,128)(2,1)S(1)}) fusion(bf16[4,1,256,2048]{3,2,1,0:T(8,128)(2,1)} %all-gather.2.cloned.1.call-done), kind=kLoop, calls=%fused_computation.10 | loop fusion | bytes 8388608 | tf_op jit(solution)/shard_map/squeeze;squeeze | solution.py:459
  104.7 10.8 %shard_map.92.est_ref = f32[256,2048]{1,0:T(8,128)S(1)} custom-call(f32[256,2048]{1,0:T(8,128)} %bitcast_select_fusion.est_ref, bf16[256,2048]{1,0:T(8,128)(2,1)S(1)} %get-tuple-element.46.raw_ref, bf16[128,128]{1,0:T(8,128)(2,1)S(1)} %bitcast.106, bf16[128,128]{1,0:T(8,128)(2,1)S(1)} %bitcast.110, bf16[512,512]{1,0:T(8,128)(2,1)S(1)} %copy-done.1, ...), custom_call_target="tpu_custom_call" | custom-call | flops 2147483648 | bytes 5242880 | tf_op jit(solution)/shard_map/pallas_call | solution.py:212
  115.5 1.3 copy-done.21
  117.1 11.0 %shard_map.93.est_ref = f32[256,2048]{1,0:T(8,128)S(1)} custom-call(f32[256,2048]{1,0:T(8,128)} %copy-done.21, bf16[256,2048]{1,0:T(8,128)(2,1)S(1)} %get-tuple-element.45.raw_ref, bf16[128,128]{1,0:T(8,128)(2,1)S(1)} %bitcast.105, bf16[128,128]{1,0:T(8,128)(2,1)S(1)} %bitcast.109, bf16[512,512]{1,0:T(8,128)(2,1)S(1)} %get-tuple-element.76.s_ref, ...), custom_call_target="tpu_custom_call" | custom-call | flops 2147483648 | bytes 5242880 | tf_op jit(solution)/shard_map/pallas_call | solution.py:212
  128.1 1.3 copy-done.22
  129.6 10.8 %shard_map.94.est_ref = f32[256,2048]{1,0:T(8,128)S(1)} custom-call(f32[256,2048]{1,0:T(8,128)} %copy-done.22, bf16[256,2048]{1,0:T(8,128)(2,1)S(1)} %get-tuple-element.44.raw_ref, bf16[128,128]{1,0:T(8,128)(2,1)S(1)} %bitcast.104, bf16[128,128]{1,0:T(8,128)(2,1)S(1)} %bitcast.108, bf16[512,512]{1,0:T(8,128)(2,1)S(1)} %get-tuple-element.74.s_ref, ...), custom_call_target="tpu_custom_call" | custom-call | flops 2147483648 | bytes 5242880 | tf_op jit(solution)/shard_map/pallas_call | solution.py:212
  140.5 1.3 copy-done.20
  142.0 10.8 %shard_map.95 = f32[256,2048]{1,0:T(8,128)S(1)} custom-call(f32[256,2048]{1,0:T(8,128)} %copy-done.20, bf16[256,2048]{1,0:T(8,128)(2,1)S(1)} %get-tuple-element.43.raw_ref, bf16[128,128]{1,0:T(8,128)(2,1)S(1)} %bitcast.103, bf16[128,128]{1,0:T(8,128)(2,1)S(1)} %bitcast.107, bf16[512,512]{1,0:T(8,128)(2,1)S(1)} %get-tuple-element.72.s_ref, ...), custom_call_target="tpu_custom_call" | custom-call | flops 2147483648 | bytes 5242880 | tf_op jit(solution)/shard_map/pallas_call | solution.py:212
  (139 shorter events, 31.4 us)
Async XLA Ops:
  6.5 18.7 %copy-start.27 = (s32[4]{0:T(128)S(1)}, s32[4]{0:T(128)}, u32[]{:S(2)}) copy-start(s32[4]{0:T(128)} %param.16) | copy-start | bytes 52
  6.5 95.0 %all-gather.2.cloned.1.call-start = ((), (), s32[]{:S(2)}) async-start(), calls=%async_computation | async-start | bytes 4718592 | tf_op jit(solution)/shard_map/all_gather | solution.py:435
  6.5 43.5 %collective-permute-start = (f32[1,32,2048]{2,1,0:T(8,128)}, f32[1,32,2048]{2,1,0:T(8,128)}, u32[]{:S(2)}, u32[]{:S(2)}) collective-permute-start(f32[1,32,2048]{2,1,0:T(8,128)} %param.9), channel_id=1, source_target_pairs={{0,1},{1,2},{2,3},{3,4},{4,5},{5,6},{6,7},{7,0},{8,9},{9,10},{10,1... | collective-permute-start | bytes 786440 | tf_op jit(solution)/shard_map/ppermute | solution.py:15
  8.4 44.5 %collective-permute-start.1 = (f32[1,32,2048]{2,1,0:T(8,128)}, f32[1,32,2048]{2,1,0:T(8,128)}, u32[]{:S(2)}, u32[]{:S(2)}) collective-permute-start(f32[1,32,2048]{2,1,0:T(8,128)} %param.9), channel_id=1, source_target_pairs={{0,2},{1,3},{2,4},{3,5},{4,6},{5,7},{6,0},{7,1},{8,10},{9,11},{10,... | collective-permute-start | bytes 786440 | tf_op jit(solution)/shard_map/ppermute | solution.py:15
  10.8 10.4 %collective-permute-start.9 = (bf16[1,32,2048]{2,1,0:T(8,128)(2,1)S(1)}, bf16[1,32,2048]{2,1,0:T(8,128)(2,1)S(1)}, u32[]{:S(2)}, u32[]{:S(2)}) collective-permute-start(bf16[1,32,2048]{2,1,0:T(8,128)(2,1)S(1)} %get-tuple-element.57), channel_id=1, source_target_pairs={{0,8},{8,16},{16,24},{24,0},{1,9},{9,17},{17,25},{25,1},{2,10},{10... | collective-permute-start | bytes 393224 | tf_op jit(solution)/shard_map/ppermute | solution.py:15
  12.1 10.0 %collective-permute-start.8 = (bf16[1,32,2048]{2,1,0:T(8,128)(2,1)S(1)}, bf16[1,32,2048]{2,1,0:T(8,128)(2,1)S(1)}, u32[]{:S(2)}, u32[]{:S(2)}) collective-permute-start(bf16[1,32,2048]{2,1,0:T(8,128)(2,1)S(1)} %get-tuple-element.58), channel_id=1, source_target_pairs={{0,16},{8,24},{16,0},{24,8},{1,17},{9,25},{17,1},{25,9},{2,18},{10... | collective-permute-start | bytes 393224 | tf_op jit(solution)/shard_map/ppermute | solution.py:15
  13.3 10.2 %collective-permute-start.7 = (bf16[1,32,2048]{2,1,0:T(8,128)(2,1)S(1)}, bf16[1,32,2048]{2,1,0:T(8,128)(2,1)S(1)}, u32[]{:S(2)}, u32[]{:S(2)}) collective-permute-start(bf16[1,32,2048]{2,1,0:T(8,128)(2,1)S(1)} %get-tuple-element.56), channel_id=1, source_target_pairs={{0,24},{8,0},{16,8},{24,16},{1,25},{9,1},{17,9},{25,17},{2,26},{10... | collective-permute-start | bytes 393224 | tf_op jit(solution)/shard_map/ppermute | solution.py:15
  21.2 34.6 %collective-permute-start.2 = (f32[1,32,2048]{2,1,0:T(8,128)}, f32[1,32,2048]{2,1,0:T(8,128)}, u32[]{:S(2)}, u32[]{:S(2)}) collective-permute-start(f32[1,32,2048]{2,1,0:T(8,128)} %param.9), channel_id=1, source_target_pairs={{0,3},{1,4},{2,5},{3,6},{4,7},{5,0},{6,1},{7,2},{8,11},{9,12},{10,... | collective-permute-start | bytes 786440 | tf_op jit(solution)/shard_map/ppermute | solution.py:15
  22.1 55.5 %collective-permute-start.3 = (f32[1,32,2048]{2,1,0:T(8,128)}, f32[1,32,2048]{2,1,0:T(8,128)}, u32[]{:S(2)}, u32[]{:S(2)}) collective-permute-start(f32[1,32,2048]{2,1,0:T(8,128)} %param.9), channel_id=1, source_target_pairs={{0,4},{1,5},{2,6},{3,7},{4,0},{5,1},{6,2},{7,3},{8,12},{9,13},{10,... | collective-permute-start | bytes 786440 | tf_op jit(solution)/shard_map/ppermute | solution.py:15
  23.5 55.7 %collective-permute-start.4 = (f32[1,32,2048]{2,1,0:T(8,128)}, f32[1,32,2048]{2,1,0:T(8,128)}, u32[]{:S(2)}, u32[]{:S(2)}) collective-permute-start(f32[1,32,2048]{2,1,0:T(8,128)} %param.9), channel_id=1, source_target_pairs={{0,5},{1,6},{2,7},{3,0},{4,1},{5,2},{6,3},{7,4},{8,13},{9,14},{10,... | collective-permute-start | bytes 786440 | tf_op jit(solution)/shard_map/ppermute | solution.py:15
  50.0 43.0 %collective-permute-start.5 = (f32[1,32,2048]{2,1,0:T(8,128)}, f32[1,32,2048]{2,1,0:T(8,128)S(1)}, u32[]{:S(2)}, u32[]{:S(2)}) collective-permute-start(f32[1,32,2048]{2,1,0:T(8,128)} %param.9), channel_id=1, source_target_pairs={{0,6},{1,7},{2,0},{3,1},{4,2},{5,3},{6,4},{7,5},{8,14},{9,15},{10,... | collective-permute-start | bytes 786440 | tf_op jit(solution)/shard_map/ppermute | solution.py:15
  52.9 41.0 %collective-permute-start.6 = (f32[1,32,2048]{2,1,0:T(8,128)}, f32[1,32,2048]{2,1,0:T(8,128)S(1)}, u32[]{:S(2)}, u32[]{:S(2)}) collective-permute-start(f32[1,32,2048]{2,1,0:T(8,128)} %param.9), channel_id=1, source_target_pairs={{0,7},{1,0},{2,1},{3,2},{4,3},{5,4},{6,5},{7,6},{8,15},{9,8},{10,9... | collective-permute-start | bytes 786440 | tf_op jit(solution)/shard_map/ppermute | solution.py:15
  104.6 12.3 %copy-start.4 = (bf16[256,256]{1,0:T(8,128)(2,1)S(1)}, bf16[256,256]{1,0:T(8,128)(2,1)}, u32[]{:S(2)}) copy-start(bf16[256,256]{1,0:T(8,128)(2,1)} %get-tuple-element.53.a_ref) | copy-start | bytes 393220
  104.6 12.3 %copy-start.5 = (bf16[256,256]{1,0:T(8,128)(2,1)S(1)}, bf16[256,256]{1,0:T(8,128)(2,1)}, u32[]{:S(2)}) copy-start(bf16[256,256]{1,0:T(8,128)(2,1)} %get-tuple-element.49.at_ref) | copy-start | bytes 393220
  104.6 12.3 %copy-start.12 = (bf16[3,128,128]{2,1,0:T(8,128)(2,1)S(1)}, bf16[3,128,128]{2,1,0:T(8,128)(2,1)}, u32[]{:S(2)}) copy-start(bf16[3,128,128]{2,1,0:T(8,128)(2,1)} %get-tuple-element.65.bf_ref) | copy-start | bytes 294916
  104.7 12.3 %copy-start.13 = (bf16[3,128,128]{2,1,0:T(8,128)(2,1)S(1)}, bf16[3,128,128]{2,1,0:T(8,128)(2,1)}, u32[]{:S(2)}) copy-start(bf16[3,128,128]{2,1,0:T(8,128)(2,1)} %get-tuple-element.61.bb_ref) | copy-start | bytes 294916
  117.0 12.5 %copy-start.2 = (bf16[256,256]{1,0:T(8,128)(2,1)S(1)}, bf16[256,256]{1,0:T(8,128)(2,1)}, u32[]{:S(2)}) copy-start(bf16[256,256]{1,0:T(8,128)(2,1)} %get-tuple-element.52.a_ref) | copy-start | bytes 393220
  117.0 12.5 %copy-start.3 = (bf16[256,256]{1,0:T(8,128)(2,1)S(1)}, bf16[256,256]{1,0:T(8,128)(2,1)}, u32[]{:S(2)}) copy-start(bf16[256,256]{1,0:T(8,128)(2,1)} %get-tuple-element.48.at_ref) | copy-start | bytes 393220
  117.0 12.5 %copy-start.10 = (bf16[3,128,128]{2,1,0:T(8,128)(2,1)S(1)}, bf16[3,128,128]{2,1,0:T(8,128)(2,1)}, u32[]{:S(2)}) copy-start(bf16[3,128,128]{2,1,0:T(8,128)(2,1)} %get-tuple-element.64.bf_ref) | copy-start | bytes 294916
  117.0 12.5 %copy-start.11 = (bf16[3,128,128]{2,1,0:T(8,128)(2,1)S(1)}, bf16[3,128,128]{2,1,0:T(8,128)(2,1)}, u32[]{:S(2)}) copy-start(bf16[3,128,128]{2,1,0:T(8,128)(2,1)} %get-tuple-element.60.bb_ref) | copy-start | bytes 294916
  117.0 12.5 %copy-start.17 = (bf16[1,128,128]{1,2,0:T(8,128)(2,1)S(1)}, bf16[1,128,128]{1,2,0:T(8,128)(2,1)}, u32[]{:S(2)}) copy-start(bf16[1,128,128]{1,2,0:T(8,128)(2,1)} %copy.24) | copy-start | bytes 98308
  129.6 12.3 %copy-start.8 = (bf16[3,128,128]{2,1,0:T(8,128)(2,1)S(1)}, bf16[3,128,128]{2,1,0:T(8,128)(2,1)}, u32[]{:S(2)}) copy-start(bf16[3,128,128]{2,1,0:T(8,128)(2,1)} %get-tuple-element.63.bf_ref) | copy-start | bytes 294916
  129.6 12.3 %copy-start.9 = (bf16[3,128,128]{2,1,0:T(8,128)(2,1)S(1)}, bf16[3,128,128]{2,1,0:T(8,128)(2,1)}, u32[]{:S(2)}) copy-start(bf16[3,128,128]{2,1,0:T(8,128)(2,1)} %get-tuple-element.59.bb_ref) | copy-start | bytes 294916
  129.6 12.3 %copy-start.16 = (bf16[1,128,128]{1,2,0:T(8,128)(2,1)S(1)}, bf16[1,128,128]{1,2,0:T(8,128)(2,1)}, u32[]{:S(2)}) copy-start(bf16[1,128,128]{1,2,0:T(8,128)(2,1)} %copy.27) | copy-start | bytes 98308
  (15 other events, 57.6 us)
Sparse Core Ops, SparseCore 0:
  25.3 69.5 all-gather.1

commit v3 on v2

--- a/solution.py
+++ b/solution.py
@@ -100,9 +100,17 @@
     return estimate * from_blocks(correction, rows, plane_width).astype(jnp.float32)
 
 
-def plane_kernel(est_ref, raw_ref, m_ref, mt_ref, s_ref, cnt_ref, g_ref, bf_ref, bb_ref, a_ref,
-                 at_ref, bg_ref, out_ref, work, joined, across, ratio):
-    rows, plane_width = est_ref.shape
+def plane_kernel(offs_ref, bg_ref, raw_ref, m_ref, mt_ref, s_ref, cnt_ref, g_ref, bf_ref, bb_ref,
+                 a_ref, at_ref, *rest):
+    *piece_refs, out_ref, est_whole, work, joined, across, ratio = rest
+    rows, plane_width = out_ref.shape
+    if len(piece_refs) == 1:
+        est_ref = piece_refs[0]
+    else:
+        est_ref = est_whole
+        for k, piece in enumerate(piece_refs):
+            piece_rows = piece.shape[0]
+            est_ref[pl.ds(pl.multiple_of(offs_ref[k], BR), piece_rows), :] = piece[...]
     nt = rows // BR
     nc = plane_width // BW
     f32 = jnp.float32
@@ -196,8 +204,8 @@
     )(row_taps.astype(jnp.float32).reshape(-1), col_taps.astype(jnp.float32).reshape(-1))
 
 
-def kernel_update(estimate, raw_plane, matrix, landing, bands, level):
-    rows, plane_width = estimate.shape
+def kernel_update(est_pieces, offsets, raw_all, raw_index, matrix, landing, bands, level):
+    rows, plane_width = raw_all.shape[-2:]
     nt = rows // BR
     nc = plane_width // BW
     blocks = nt * nc
@@ -209,12 +217,16 @@
     count = jnp.sum(sum_mat.astype(jnp.float32), axis=1)
     count = jnp.broadcast_to(jnp.maximum(count, 1.0)[:, None], (blocks, BW))
     vmem = pl.BlockSpec(memory_space=pltpu.VMEM)
+    smem = pl.BlockSpec(memory_space=pltpu.SMEM)
+    raw_spec = pl.BlockSpec((None, None, rows, plane_width), lambda i: raw_index + (0, 0))
     return pl.pallas_call(
         plane_kernel,
+        grid=(1,),
         out_shape=jax.ShapeDtypeStruct((rows, plane_width), jnp.float32),
-        in_specs=[vmem] * 11 + [pl.BlockSpec(memory_space=pltpu.SMEM)],
+        in_specs=[smem, smem, raw_spec] + [vmem] * (9 + len(est_pieces)),
         out_specs=vmem,
         scratch_shapes=[
+            pltpu.VMEM((rows, plane_width), jnp.float32),
             pltpu.VMEM((nc, rows, BW), jnp.float32),
             pltpu.VMEM((nc, rows, BW), jnp.float32),
             pltpu.VMEM((rows, plane_width), jnp.bfloat16),
@@ -227,8 +239,9 @@
             transcendentals=0,
         ),
     )(
-        estimate,
-        raw_plane,
+        offsets,
+        jnp.reshape(level, (1,)).astype(jnp.float32),
+        raw_all,
         matrix,
         matrix.T,
         sum_mat.astype(jnp.bfloat16),
@@ -238,7 +251,7 @@
         bands[3],
         bands[0],
         bands[1],
-        jnp.reshape(level, (1,)).astype(jnp.float32),
+        *est_pieces,
     )
 
 
@@ -437,9 +450,8 @@
     arrived = [initial_estimate] + [
         passed_along(initial_estimate, "tile", shift) for shift in range(1, tile_count)
     ]
-    source_order = (my_tile - jnp.arange(tile_count, dtype=jnp.int32)) % tile_count
-    estimate = jnp.take(jnp.stack(arrived), source_order, axis=0)
-    estimate = jnp.swapaxes(estimate, 0, 1).reshape(planes, tile_count * tile_rows, plane_width)
+    offsets = (my_tile - jnp.arange(tile_count, dtype=jnp.int32)) % tile_count * tile_rows
+    whole_plane = jnp.zeros((1,), jnp.int32)
     plane_bands = lax.dynamic_slice_in_dim(psf_band, my_group * planes, planes, 0)
     views_in_order = (my_group + jnp.arange(view_count, dtype=jnp.int32)) % view_count
     bands = all_bands(
@@ -455,8 +467,10 @@
         estimate = jnp.stack(
             [
                 kernel_update(
-                    estimate[p],
-                    pieces[update_index][p],
+                    [piece[p] for piece in arrived] if update_index == 0 else [estimate[p]],
+                    offsets if update_index == 0 else whole_plane,
+                    pieces,
+                    (update_index, p),
                     matrix,
                     landing,
                     [b[update_index * planes + p] for b in bands],

time: 161 us -> 160 us (level)
  the two profiles are of different devices: /device:TPU:9 before, /device:TPU:25 now
where the time goes in v3:
time: 160 us
  waiting for transfers between devices  52.6 us (33%)
  Pallas kernels  47.8 us (30%)
  local copies, waits for them, and re-layouts  26.7 us (17%)
  between operations  15.9 us (10%)
  starting transfers between devices  11.4 us (7%)
  other arithmetic  5.12 us (3%)
    ppermute x10, waiting for transfers between devices, passed_along(): return lax.ppermute(x, axis, [(i, (i + by) % count) for i in range(count)])  51.1 us
    pallas_call x4, Pallas kernels, kernel_update(): pl.pallas_call(plane_kernel, grid=(1,), out_shape=jax.ShapeDtypeStruct((r...  42.7 us
    ppermute x10, starting transfers between devices, passed_along(): return lax.ppermute(x, axis, [(i, (i + by) % count) for i in range(count)])  11.4 us
    dynamic_slice x5, local copies, waits for them, and re-layouts, local(): matrix = interp[view_index]  6.51 us
    squeeze x4, local copies, waits for them, and re-layouts, local(): b[update_index * planes + p]  6.24 us
    unnamed x62, local copies, waits for them, and re-layouts  5.2 us
    pallas_call x1, Pallas kernels, all_bands(): pl.pallas_call(band_kernel, out_shape=(jax.ShapeDtypeStruct((count, rows,...  5.06 us
  transfers between devices with their start and end apart: 11, of which 6 were waited for; matrix products, arithmetic and copies ran while one was open for 14% of the time, Pallas kernels for 3%

profile of v3, /device:TPU:25, one launch (start us, length us, event | category | flops | bytes accessed | tf_op | source)
XLA Modules:
  0.0 159.5 jit_solution(2298637917932055800)
XLA Ops:
  7.8 2.2 %collective-permute-start = (bf16[1,32,2048]{2,1,0:T(8,128)(2,1)S(1)}, bf16[1,32,2048]{2,1,0:T(8,128)(2,1)S(1)}, u32[]{:S(2)}, u32[]{:S(2)}) collective-permute-start(bf16[1,32,2048]{2,1,0:T(8,128)(2,1)S(1)} %get-tuple-element.52), channel_id=1, source_target_pairs={{0,24},{8,0},{16,8},{24,16},{1,25},{9,1},{17,9},{25,17},{2,26},{10... | collective-permute-start | bytes 393224 | tf_op jit(solution)/shard_map/ppermute | solution.py:15
  10.6 1.7 %collective-permute-done = bf16[1,32,2048]{2,1,0:T(8,128)(2,1)S(1)} collective-permute-done((bf16[1,32,2048]{2,1,0:T(8,128)(2,1)S(1)}, bf16[1,32,2048]{2,1,0:T(8,128)(2,1)S(1)}, u32[]{:S(2)}, u32[]{:S(2)}) %collective-permute-start) | collective-permute-done | bytes 131104 | tf_op jit(solution)/shard_map/ppermute | solution.py:15
  12.3 2.2 %collective-permute-done.1 = bf16[1,32,2048]{2,1,0:T(8,128)(2,1)S(1)} collective-permute-done((bf16[1,32,2048]{2,1,0:T(8,128)(2,1)S(1)}, bf16[1,32,2048]{2,1,0:T(8,128)(2,1)S(1)}, u32[]{:S(2)}, u32[]{:S(2)}) %collective-permute-start.1) | collective-permute-done | bytes 131104 | tf_op jit(solution)/shard_map/ppermute | solution.py:15
  14.5 1.4 collective-permute-done.2
  16.8 2.7 %collective-permute-start.3 = (f32[1,32,2048]{2,1,0:T(8,128)}, f32[1,32,2048]{2,1,0:T(8,128)}, u32[]{:S(2)}, u32[]{:S(2)}) collective-permute-start(f32[1,32,2048]{2,1,0:T(8,128)} %param.9), channel_id=1, source_target_pairs={{0,1},{1,2},{2,3},{3,4},{4,5},{5,6},{6,7},{7,0},{8,9},{9,10},{10,1... | collective-permute-start | bytes 786440 | tf_op jit(solution)/shard_map/ppermute | solution.py:15
  19.5 1.3 collective-permute-start.4
  22.2 2.0 %collective-permute-start.7 = (f32[1,32,2048]{2,1,0:T(8,128)}, f32[1,32,2048]{2,1,0:T(8,128)}, u32[]{:S(2)}, u32[]{:S(2)}) collective-permute-start(f32[1,32,2048]{2,1,0:T(8,128)} %param.9), channel_id=1, source_target_pairs={{0,5},{1,6},{2,7},{3,0},{4,1},{5,2},{6,3},{7,4},{8,13},{9,14},{10,... | collective-permute-start | bytes 786440 | tf_op jit(solution)/shard_map/ppermute | solution.py:15
  30.8 5.1 %shard_map.91 = (bf16[4,256,256]{2,1,0:T(8,128)(2,1)}, bf16[4,256,256]{2,1,0:T(8,128)(2,1)}, bf16[4,3,128,128]{3,2,1,0:T(8,128)(2,1)}, bf16[4,3,128,128]{3,2,1,0:T(8,128)(2,1)}) custom-call(f32[68]{0:T(128)} %reshape.563.row_ref, f32[68]{0:T(128)} %reshape.564.col_ref), custom_call_target="tpu_custom_call" | custom-call | tf_op jit(solution)/shard_map/pallas_call | solution.py:194
  37.8 1.8 %slice_bitcast_fusion.8 = (bf16[3,128,128]{2,1,0:T(8,128)(2,1)}, bf16[3,128,128]{2,1,0:T(8,128)(2,1)}, bf16[3,128,128]{2,1,0:T(8,128)(2,1)}, bf16[3,128,128]{2,1,0:T(8,128)(2,1)}) fusion(bf16[4,3,128,128]{3,2,1,0:T(8,128)(2,1)} %get-tuple-element.10), kind=kLoop, calls=%fused_computation.41 | loop fusion | bytes 786432 | tf_op jit(solution)/shard_map/squeeze | solution.py:476
  39.6 1.8 %slice_bitcast_fusion.9 = (bf16[3,128,128]{2,1,0:T(8,128)(2,1)}, bf16[3,128,128]{2,1,0:T(8,128)(2,1)}, bf16[3,128,128]{2,1,0:T(8,128)(2,1)}, bf16[3,128,128]{2,1,0:T(8,128)(2,1)}) fusion(bf16[4,3,128,128]{3,2,1,0:T(8,128)(2,1)} %get-tuple-element.9), kind=kLoop, calls=%fused_computation.42 | loop fusion | bytes 786432 | tf_op jit(solution)/shard_map/squeeze | solution.py:476
  41.4 1.9 %slice_bitcast_fusion = (bf16[256,256]{1,0:T(8,128)(2,1)}, bf16[256,256]{1,0:T(8,128)(2,1)}, bf16[256,256]{1,0:T(8,128)(2,1)S(1)}, bf16[256,256]{1,0:T(8,128)(2,1)S(1)}) fusion(bf16[4,256,256]{2,1,0:T(8,128)(2,1)} %get-tuple-element.12), kind=kLoop, calls=%fused_computation.30 | loop fusion | bytes 1048576 | tf_op jit(solution)/shard_map/squeeze | solution.py:476
  46.8 1.5 copy.24
  48.2 1.5 copy.22
  49.7 1.5 copy.20
  51.1 1.5 copy.18
  52.6 1.5 fusion.50
  54.1 1.2 fusion.10
  55.2 44.5 %collective-permute-done.6 = f32[1,32,2048]{2,1,0:T(8,128)} collective-permute-done((f32[1,32,2048]{2,1,0:T(8,128)}, f32[1,32,2048]{2,1,0:T(8,128)}, u32[]{:S(2)}, u32[]{:S(2)}) %collective-permute-start.6) | collective-permute-done | bytes 262176 | tf_op jit(solution)/shard_map/ppermute | solution.py:15
  99.8 1.2 collective-permute-done.7
  101.0 1.5 all-gather.2.cloned.1.call-done.raw_ref
  108.5 11.2 %shard_map.92.rest_0_ = f32[256,2048]{1,0:T(8,128)S(1)} custom-call(s32[8]{0:T(128)S(1)} %fusion.46.offs_ref, f32[1]{0:T(128)} %get-tuple-element.75.bg_ref, bf16[4,1,256,2048]{3,2,1,0:T(8,128)(2,1)} %all-gather.2.cloned.1.call-done.raw_ref, bf16[128,128]{1,0:T(8,128)(2,1)S(1)} %bitcast.83, bf16[128,128]{1,0:T(8,128)(2,1)S(1)} %bitcast.87, ...), custom_call_target="tpu_custom_call" | custom-call | flops 2147483648 | bytes 5242880 | tf_op jit(solution)/shard_map/pallas_call | solution.py:222
  119.9 10.7 %shard_map.93.rest_0_ = f32[256,2048]{1,0:T(8,128)S(1)} custom-call(s32[1]{0:T(128)} %constant.150.clone.1.offs_ref, f32[1]{0:T(128)} %get-tuple-element.78.bg_ref, bf16[4,1,256,2048]{3,2,1,0:T(8,128)(2,1)} %all-gather.2.cloned.1.call-done.raw_ref, bf16[128,128]{1,0:T(8,128)(2,1)S(1)} %bitcast.82, bf16[128,128]{1,0:T(8,128)(2,1)S(1)} %bitcast.86, ...), custom_call_target="tpu_custom_call" | custom-call | flops 2147483648 | bytes 5242880 | tf_op jit(solution)/shard_map/pallas_call | solution.py:222
  130.8 10.5 %shard_map.94.rest_0_ = f32[256,2048]{1,0:T(8,128)S(1)} custom-call(s32[1]{0:T(128)} %constant.150.clone.1.offs_ref, f32[1]{0:T(128)} %get-tuple-element.76.bg_ref, bf16[4,1,256,2048]{3,2,1,0:T(8,128)(2,1)} %all-gather.2.cloned.1.call-done.raw_ref, bf16[128,128]{1,0:T(8,128)(2,1)S(1)} %bitcast.81, bf16[128,128]{1,0:T(8,128)(2,1)S(1)} %bitcast.85, ...), custom_call_target="tpu_custom_call" | custom-call | flops 2147483648 | bytes 5242880 | tf_op jit(solution)/shard_map/pallas_call | solution.py:222
  141.6 10.4 %shard_map.95 = f32[256,2048]{1,0:T(8,128)S(1)} custom-call(s32[1]{0:T(128)} %constant.150.clone.1.offs_ref, f32[1]{0:T(128)} %get-tuple-element.77.bg_ref, bf16[4,1,256,2048]{3,2,1,0:T(8,128)(2,1)} %all-gather.2.cloned.1.call-done.raw_ref, bf16[128,128]{1,0:T(8,128)(2,1)S(1)} %bitcast.80, bf16[128,128]{1,0:T(8,128)(2,1)S(1)} %bitcast.84, ...), custom_call_target="tpu_custom_call" | custom-call | flops 2147483648 | bytes 5242880 | tf_op jit(solution)/shard_map/pallas_call | solution.py:222
  (130 shorter events, 21.0 us)
Async XLA Ops:
  6.5 17.7 %copy-start.26 = (s32[4,512,1]{1,2,0:T(1,128)S(1)}, s32[4,512,1]{1,2,0:T(1,128)}, u32[]{:S(2)}) copy-start(s32[4,512,1]{1,2,0:T(1,128)} %param.11) | copy-start | bytes 24580
  6.5 17.8 %copy-start.27 = (s32[4,512]{1,0:T(4,128)S(1)}, s32[4,512]{1,0:T(4,128)}, u32[]{:S(2)}) copy-start(s32[4,512]{1,0:T(4,128)} %param.12) | copy-start | bytes 24580
  6.5 18.4 %copy-start.30 = (s32[4]{0:T(128)S(1)}, s32[4]{0:T(128)}, u32[]{:S(2)}) copy-start(s32[4]{0:T(128)} %param.16) | copy-start | bytes 52
  6.5 20.4 %copy-start.28 = (f32[4,4,17]{2,1,0:T(4,128)S(1)}, f32[4,4,17]{2,1,0:T(4,128)}, u32[]{:S(2)}) copy-start(f32[4,4,17]{2,1,0:T(4,128)} %param.14) | copy-start | bytes 3268
  6.5 21.1 %copy-start.29 = (f32[4,4,17]{2,1,0:T(4,128)S(1)}, f32[4,4,17]{2,1,0:T(4,128)}, u32[]{:S(2)}) copy-start(f32[4,4,17]{2,1,0:T(4,128)} %param.15) | copy-start | bytes 3268
  6.5 96.0 %all-gather.2.cloned.1.call-start = ((), (), s32[]{:S(2)}) async-start(), calls=%async_computation | async-start | bytes 4718592 | tf_op jit(solution)/shard_map/all_gather | solution.py:448
  7.8 4.5 %collective-permute-start = (bf16[1,32,2048]{2,1,0:T(8,128)(2,1)S(1)}, bf16[1,32,2048]{2,1,0:T(8,128)(2,1)S(1)}, u32[]{:S(2)}, u32[]{:S(2)}) collective-permute-start(bf16[1,32,2048]{2,1,0:T(8,128)(2,1)S(1)} %get-tuple-element.52), channel_id=1, source_target_pairs={{0,24},{8,0},{16,8},{24,16},{1,25},{9,1},{17,9},{25,17},{2,26},{10... | collective-permute-start | bytes 393224 | tf_op jit(solution)/shard_map/ppermute | solution.py:15
  10.0 4.5 %collective-permute-start.1 = (bf16[1,32,2048]{2,1,0:T(8,128)(2,1)S(1)}, bf16[1,32,2048]{2,1,0:T(8,128)(2,1)S(1)}, u32[]{:S(2)}, u32[]{:S(2)}) collective-permute-start(bf16[1,32,2048]{2,1,0:T(8,128)(2,1)S(1)} %get-tuple-element.54), channel_id=1, source_target_pairs={{0,16},{8,24},{16,0},{24,8},{1,17},{9,25},{17,1},{25,9},{2,18},{10... | collective-permute-start | bytes 393224 | tf_op jit(solution)/shard_map/ppermute | solution.py:15
  10.3 5.6 %collective-permute-start.2 = (bf16[1,32,2048]{2,1,0:T(8,128)(2,1)S(1)}, bf16[1,32,2048]{2,1,0:T(8,128)(2,1)S(1)}, u32[]{:S(2)}, u32[]{:S(2)}) collective-permute-start(bf16[1,32,2048]{2,1,0:T(8,128)(2,1)S(1)} %get-tuple-element.53), channel_id=1, source_target_pairs={{0,8},{8,16},{16,24},{24,0},{1,9},{9,17},{17,25},{25,1},{2,10},{10... | collective-permute-start | bytes 393224 | tf_op jit(solution)/shard_map/ppermute | solution.py:15
  16.8 28.8 %collective-permute-start.3 = (f32[1,32,2048]{2,1,0:T(8,128)}, f32[1,32,2048]{2,1,0:T(8,128)}, u32[]{:S(2)}, u32[]{:S(2)}) collective-permute-start(f32[1,32,2048]{2,1,0:T(8,128)} %param.9), channel_id=1, source_target_pairs={{0,1},{1,2},{2,3},{3,4},{4,5},{5,6},{6,7},{7,0},{8,9},{9,10},{10,1... | collective-permute-start | bytes 786440 | tf_op jit(solution)/shard_map/ppermute | solution.py:15
  19.5 27.2 %collective-permute-start.4 = (f32[1,32,2048]{2,1,0:T(8,128)}, f32[1,32,2048]{2,1,0:T(8,128)}, u32[]{:S(2)}, u32[]{:S(2)}) collective-permute-start(f32[1,32,2048]{2,1,0:T(8,128)} %param.9), channel_id=1, source_target_pairs={{0,2},{1,3},{2,4},{3,5},{4,6},{5,7},{6,0},{7,1},{8,10},{9,11},{10,... | collective-permute-start | bytes 786440 | tf_op jit(solution)/shard_map/ppermute | solution.py:15
  20.8 34.4 %collective-permute-start.5 = (f32[1,32,2048]{2,1,0:T(8,128)}, f32[1,32,2048]{2,1,0:T(8,128)}, u32[]{:S(2)}, u32[]{:S(2)}) collective-permute-start(f32[1,32,2048]{2,1,0:T(8,128)} %param.9), channel_id=1, source_target_pairs={{0,3},{1,4},{2,5},{3,6},{4,7},{5,0},{6,1},{7,2},{8,11},{9,12},{10,... | collective-permute-start | bytes 786440 | tf_op jit(solution)/shard_map/ppermute | solution.py:15
  21.3 78.5 %collective-permute-start.6 = (f32[1,32,2048]{2,1,0:T(8,128)}, f32[1,32,2048]{2,1,0:T(8,128)}, u32[]{:S(2)}, u32[]{:S(2)}) collective-permute-start(f32[1,32,2048]{2,1,0:T(8,128)} %param.9), channel_id=1, source_target_pairs={{0,4},{1,5},{2,6},{3,7},{4,0},{5,1},{6,2},{7,3},{8,12},{9,13},{10,... | collective-permute-start | bytes 786440 | tf_op jit(solution)/shard_map/ppermute | solution.py:15
  22.2 78.8 %collective-permute-start.7 = (f32[1,32,2048]{2,1,0:T(8,128)}, f32[1,32,2048]{2,1,0:T(8,128)}, u32[]{:S(2)}, u32[]{:S(2)}) collective-permute-start(f32[1,32,2048]{2,1,0:T(8,128)} %param.9), channel_id=1, source_target_pairs={{0,5},{1,6},{2,7},{3,0},{4,1},{5,2},{6,3},{7,4},{8,13},{9,14},{10,... | collective-permute-start | bytes 786440 | tf_op jit(solution)/shard_map/ppermute | solution.py:15
  45.6 55.4 %collective-permute-start.8 = (f32[1,32,2048]{2,1,0:T(8,128)}, f32[1,32,2048]{2,1,0:T(8,128)}, u32[]{:S(2)}, u32[]{:S(2)}) collective-permute-start(f32[1,32,2048]{2,1,0:T(8,128)} %param.9), channel_id=1, source_target_pairs={{0,6},{1,7},{2,0},{3,1},{4,2},{5,3},{6,4},{7,5},{8,14},{9,15},{10,... | collective-permute-start | bytes 786440 | tf_op jit(solution)/shard_map/ppermute | solution.py:15
  46.8 54.3 %collective-permute-start.9 = (f32[1,32,2048]{2,1,0:T(8,128)}, f32[1,32,2048]{2,1,0:T(8,128)}, u32[]{:S(2)}, u32[]{:S(2)}) collective-permute-start(f32[1,32,2048]{2,1,0:T(8,128)} %param.9), channel_id=1, source_target_pairs={{0,7},{1,0},{2,1},{3,2},{4,3},{5,4},{6,5},{7,6},{8,15},{9,8},{10,9... | collective-permute-start | bytes 786440 | tf_op jit(solution)/shard_map/ppermute | solution.py:15
  108.5 11.2 %copy-start.25 = (f32[512]{0:T(512)S(1)}, f32[512]{0:T(512)}, u32[]{:S(2)}) copy-start(f32[512]{0:T(512)} %broadcast_maximum_fusion.1) | copy-start | bytes 6148
  108.5 11.4 %copy-start.3 = (bf16[256,256]{1,0:T(8,128)(2,1)S(1)}, bf16[256,256]{1,0:T(8,128)(2,1)}, u32[]{:S(2)}) copy-start(bf16[256,256]{1,0:T(8,128)(2,1)} %get-tuple-element.44.at_ref) | copy-start | bytes 393220
  108.5 11.4 %copy-start.4 = (bf16[256,256]{1,0:T(8,128)(2,1)S(1)}, bf16[256,256]{1,0:T(8,128)(2,1)}, u32[]{:S(2)}) copy-start(bf16[256,256]{1,0:T(8,128)(2,1)} %get-tuple-element.48.a_ref) | copy-start | bytes 393220
  108.5 11.4 %copy-start.11 = (bf16[3,128,128]{2,1,0:T(8,128)(2,1)S(1)}, bf16[3,128,128]{2,1,0:T(8,128)(2,1)}, u32[]{:S(2)}) copy-start(bf16[3,128,128]{2,1,0:T(8,128)(2,1)} %get-tuple-element.56.bb_ref) | copy-start | bytes 294916
  108.5 11.4 %copy-start.12 = (bf16[3,128,128]{2,1,0:T(8,128)(2,1)S(1)}, bf16[3,128,128]{2,1,0:T(8,128)(2,1)}, u32[]{:S(2)}) copy-start(bf16[3,128,128]{2,1,0:T(8,128)(2,1)} %get-tuple-element.60.bf_ref) | copy-start | bytes 294916
  108.5 11.4 %copy-start.17 = (bf16[1,128,128]{2,1,0:T(8,128)(2,1)S(1)}, bf16[1,128,128]{2,1,0:T(8,128)(2,1)}, u32[]{:S(2)}) copy-start(bf16[1,128,128]{2,1,0:T(8,128)(2,1)} %get-tuple-element.66) | copy-start | bytes 98308
  108.5 11.4 %copy-start.21 = (bf16[1,128,128]{1,2,0:T(8,128)(2,1)S(1)}, bf16[1,128,128]{1,2,0:T(8,128)(2,1)}, u32[]{:S(2)}) copy-start(bf16[1,128,128]{1,2,0:T(8,128)(2,1)} %copy.22) | copy-start | bytes 98308
  119.9 10.9 %copy-start.2 = (bf16[256,256]{1,0:T(8,128)(2,1)S(1)}, bf16[256,256]{1,0:T(8,128)(2,1)}, u32[]{:S(2)}) copy-start(bf16[256,256]{1,0:T(8,128)(2,1)} %get-tuple-element.49.a_ref) | copy-start | bytes 393220
  (18 other events, 123.6 us)
Sparse Core Ops, SparseCore 0:
  16.9 85.5 all-gather.1

commit v4 on v3

--- a/solution.py
+++ b/solution.py
@@ -445,12 +445,17 @@
         )
         piece = own_piece if update_index == 0 else passed_along(own_piece, "view", -update_index)
         pieces.append(piece)
-    pieces = lax.all_gather(jnp.stack(pieces), "tile", axis=2, tiled=True)
+    first_raw = lax.all_gather(jnp.stack(pieces[:1]), "tile", axis=2, tiled=True)
+    later_raw = lax.all_gather(jnp.stack(pieces[1:]), "tile", axis=2, tiled=True)
     tile_count = lax.axis_size("tile")
-    arrived = [initial_estimate] + [
-        passed_along(initial_estimate, "tile", shift) for shift in range(1, tile_count)
+    along = [initial_estimate] + [
+        passed_along(initial_estimate, "tile", shift) for shift in range(2, tile_count, 2)
     ]
-    offsets = (my_tile - jnp.arange(tile_count, dtype=jnp.int32)) % tile_count * tile_rows
+    partner = [(i, i ^ 1) for i in range(tile_count)]
+    arrived = along + [lax.ppermute(piece, "tile", partner) for piece in along]
+    sources = [(my_tile - shift) % tile_count for shift in range(0, tile_count, 2)]
+    sources = sources + [(source ^ 1) for source in sources]
+    offsets = jnp.stack(sources).astype(jnp.int32) * tile_rows
     whole_plane = jnp.zeros((1,), jnp.int32)
     plane_bands = lax.dynamic_slice_in_dim(psf_band, my_group * planes, planes, 0)
     views_in_order = (my_group + jnp.arange(view_count, dtype=jnp.int32)) % view_count
@@ -469,8 +474,8 @@
                 kernel_update(
                     [piece[p] for piece in arrived] if update_index == 0 else [estimate[p]],
                     offsets if update_index == 0 else whole_plane,
-                    pieces,
-                    (update_index, p),
+                    first_raw if update_index == 0 else later_raw,
+                    (0 if update_index == 0 else update_index - 1, p),
                     matrix,
                     landing,
                     [b[update_index * planes + p] for b in bands],

time: 160 us -> 132 us (0.82)
  the two profiles are of different devices: /device:TPU:25 before, /device:TPU:0 now
where the time goes in v4:
time: 132 us; the launch traced here: 131 us
  Pallas kernels  48.6 us (37%)
  local copies, waits for them, and re-layouts  34.9 us (26%)
  between operations  15.7 us (12%)
  waiting for transfers between devices  14.3 us (11%)
  starting transfers between devices  11.7 us (9%)
  other arithmetic  5.79 us (4%)
    pallas_call x4, Pallas kernels, kernel_update(): pl.pallas_call(plane_kernel, grid=(1,), out_shape=jax.ShapeDtypeStruct((r...  43.6 us
    unnamed x74, local copies, waits for them, and re-layouts  16.2 us
    all_gather x1, waiting for transfers between devices, local(): lax.all_gather(jnp.stack(pieces[1:]), 'tile', axis=2, tiled=True)  11.3 us
    ppermute x6, starting transfers between devices, passed_along(): return lax.ppermute(x, axis, [(i, (i + by) % count) for i in range(count)])  10.6 us
    squeeze x4, local copies, waits for them, and re-layouts, local(): b[update_index * planes + p]  6.25 us
    pallas_call x1, Pallas kernels, all_bands(): pl.pallas_call(band_kernel, out_shape=(jax.ShapeDtypeStruct((count, rows,...  5.01 us
    ppermute x6, waiting for transfers between devices, passed_along(): return lax.ppermute(x, axis, [(i, (i + by) % count) for i in range(count)])  2.92 us
    dynamic_slice x5, local copies, waits for them, and re-layouts, local(): matrix = interp[view_index]  2.89 us
  transfers between devices with their start and end apart: 12, of which 3 were waited for; matrix products, arithmetic and copies ran while one was open for 16% of the time, Pallas kernels for 13%

profile of v4, /device:TPU:0, one launch (start us, length us, event | category | flops | bytes accessed | tf_op | source)
XLA Modules:
  0.0 131.0 jit_solution(10721603372665212787)
XLA Ops:
  6.5 1.8 %constant_dynamic-slice_fusion.5 = (bf16[1,1,32,2048]{3,2,1,0:T(8,128)(2,1)}, bf16[1,32,2048]{2,1,0:T(8,128)(2,1)S(1)}, bf16[1,32,2048]{2,1,0:T(8,128)(2,1)S(1)}, bf16[1,32,2048]{2,1,0:T(8,128)(2,1)S(1)}) fusion(bf16[1,4,32,2048]{3,2,1,0:T(8,128)(2,1)} %param.10, s32[]{:T(128)S(6)} %select_n.240, s32[]{:T(128)S(6)} %select_n.218, s32[]{:T(128)S(6)} %select_n.216, ...), kind=kLoop, calls=%fused_computation.58 | loop fusion | bytes 1048592 | tf_op jit(solution)/shard_map/dynamic_slice | solution.py:443
  8.4 3.1 %collective-permute-start.3 = (f32[1,32,2048]{2,1,0:T(8,128)}, f32[1,32,2048]{2,1,0:T(8,128)}, u32[]{:S(2)}, u32[]{:S(2)}) collective-permute-start(f32[1,32,2048]{2,1,0:T(8,128)} %param.9), channel_id=1, source_target_pairs={{0,2},{1,3},{2,4},{3,5},{4,6},{5,7},{6,0},{7,1},{8,10},{9,11},{10,... | collective-permute-start | bytes 786440 | tf_op jit(solution)/shard_map/ppermute | solution.py:15
  11.5 2.6 %collective-permute-start.4 = (f32[1,32,2048]{2,1,0:T(8,128)}, f32[1,32,2048]{2,1,0:T(8,128)}, u32[]{:S(2)}, u32[]{:S(2)}) collective-permute-start(f32[1,32,2048]{2,1,0:T(8,128)} %param.9), channel_id=1, source_target_pairs={{0,4},{1,5},{2,6},{3,7},{4,0},{5,1},{6,2},{7,3},{8,12},{9,13},{10,... | collective-permute-start | bytes 786440 | tf_op jit(solution)/shard_map/ppermute | solution.py:15
  14.1 2.4 %collective-permute-start = (bf16[1,32,2048]{2,1,0:T(8,128)(2,1)S(1)}, bf16[1,32,2048]{2,1,0:T(8,128)(2,1)S(1)}, u32[]{:S(2)}, u32[]{:S(2)}) collective-permute-start(bf16[1,32,2048]{2,1,0:T(8,128)(2,1)S(1)} %get-tuple-element.53), channel_id=1, source_target_pairs={{0,24},{8,0},{16,8},{24,16},{1,25},{9,1},{17,9},{25,17},{2,26},{10... | collective-permute-start | bytes 393224 | tf_op jit(solution)/shard_map/ppermute | solution.py:15
  20.2 1.3 %collective-permute-start.5 = (f32[1,32,2048]{2,1,0:T(8,128)}, f32[1,32,2048]{2,1,0:T(8,128)}, u32[]{:S(2)}, u32[]{:S(2)}) collective-permute-start(f32[1,32,2048]{2,1,0:T(8,128)} %param.9), channel_id=1, source_target_pairs={{0,6},{1,7},{2,0},{3,1},{4,2},{5,3},{6,4},{7,5},{8,14},{9,15},{10,... | collective-permute-start | bytes 786440 | tf_op jit(solution)/shard_map/ppermute | solution.py:15
  21.6 2.3 %collective-permute-done.1 = bf16[1,32,2048]{2,1,0:T(8,128)(2,1)S(1)} collective-permute-done((bf16[1,32,2048]{2,1,0:T(8,128)(2,1)S(1)}, bf16[1,32,2048]{2,1,0:T(8,128)(2,1)S(1)}, u32[]{:S(2)}, u32[]{:S(2)}) %collective-permute-start.1) | collective-permute-done | bytes 131104 | tf_op jit(solution)/shard_map/ppermute | solution.py:15
  30.8 5.0 %shard_map.91 = (bf16[4,256,256]{2,1,0:T(8,128)(2,1)}, bf16[4,256,256]{2,1,0:T(8,128)(2,1)}, bf16[4,3,128,128]{3,2,1,0:T(8,128)(2,1)}, bf16[4,3,128,128]{3,2,1,0:T(8,128)(2,1)}) custom-call(f32[68]{0:T(128)} %reshape.563.row_ref, f32[68]{0:T(128)} %reshape.564.col_ref), custom_call_target="tpu_custom_call" | custom-call | tf_op jit(solution)/shard_map/pallas_call | solution.py:194
  37.9 1.8 %slice_bitcast_fusion.8 = (bf16[3,128,128]{2,1,0:T(8,128)(2,1)}, bf16[3,128,128]{2,1,0:T(8,128)(2,1)}, bf16[3,128,128]{2,1,0:T(8,128)(2,1)}, bf16[3,128,128]{2,1,0:T(8,128)(2,1)}) fusion(bf16[4,3,128,128]{3,2,1,0:T(8,128)(2,1)} %get-tuple-element.10), kind=kLoop, calls=%fused_computation.41 | loop fusion | bytes 786432 | tf_op jit(solution)/shard_map/squeeze | solution.py:481
  39.7 1.8 %slice_bitcast_fusion.9 = (bf16[3,128,128]{2,1,0:T(8,128)(2,1)}, bf16[3,128,128]{2,1,0:T(8,128)(2,1)}, bf16[3,128,128]{2,1,0:T(8,128)(2,1)}, bf16[3,128,128]{2,1,0:T(8,128)(2,1)}) fusion(bf16[4,3,128,128]{3,2,1,0:T(8,128)(2,1)} %get-tuple-element.9), kind=kLoop, calls=%fused_computation.42 | loop fusion | bytes 786432 | tf_op jit(solution)/shard_map/squeeze | solution.py:481
  41.5 1.9 %slice_bitcast_fusion = (bf16[256,256]{1,0:T(8,128)(2,1)}, bf16[256,256]{1,0:T(8,128)(2,1)}, bf16[256,256]{1,0:T(8,128)(2,1)S(1)}, bf16[256,256]{1,0:T(8,128)(2,1)S(1)}) fusion(bf16[4,256,256]{2,1,0:T(8,128)(2,1)} %get-tuple-element.12), kind=kLoop, calls=%fused_computation.30 | loop fusion | bytes 1048576 | tf_op jit(solution)/shard_map/squeeze | solution.py:481
  44.2 1.1 fusion.13
  51.8 1.0 copy-done.4
  52.9 1.1 copy-done.5
  54.7 0.9 copy-done.23
  55.6 0.9 copy-done.24
  59.1 1.2 copy-done.28
  60.3 0.9 copy-done.29
  61.3 12.3 %shard_map.92.rest_0_ = f32[256,2048]{1,0:T(8,128)} custom-call(s32[8]{0:T(128)S(1)} %broadcast_multiply_fusion.offs_ref, f32[1]{0:T(128)} %get-tuple-element.75.bg_ref, bf16[1,1,256,2048]{3,2,1,0:T(8,128)(2,1)S(1)} %copy-done.28, bf16[128,128]{1,0:T(8,128)(2,1)S(1)} %bitcast.94, bf16[128,128]{1,0:T(8,128)(2,1)S(1)} %bitcast.95, ...), custom_call_target="tpu_custom_call" | custom-call | flops 2147483648 | bytes 5242880 | tf_op jit(solution)/shard_map/pallas_call | solution.py:222
  73.5 11.3 %all-gather.3.cloned.1.call-done.raw_ref = bf16[3,1,256,2048]{3,2,1,0:T(8,128)(2,1)} async-done(((bf16[3,1,32,2048]{3,2,1,0:T(8,128)(2,1)}), bf16[3,1,256,2048]{3,2,1,0:T(8,128)(2,1)}) %all-gather.3.cloned.1.call-update) | async-done | bytes 3145744 | tf_op jit(solution)/shard_map/all_gather | solution.py:449
  85.0 1.6 %copy-done = f32[256,2048]{1,0:T(8,128)S(1)} copy-done((f32[256,2048]{1,0:T(8,128)S(1)}, f32[256,2048]{1,0:T(8,128)}, u32[]{:S(2)}) %copy-start) | copy-done | bytes 2097176
  87.4 0.9 copy-done.3
  91.7 10.3 %shard_map.93.rest_0_ = f32[256,2048]{1,0:T(8,128)S(1)} custom-call(s32[1]{0:T(128)} %constant.162.clone.1.offs_ref, f32[1]{0:T(128)} %get-tuple-element.78.bg_ref, bf16[3,1,256,2048]{3,2,1,0:T(8,128)(2,1)} %all-gather.3.cloned.1.call-done.raw_ref, bf16[128,128]{1,0:T(8,128)(2,1)S(1)} %bitcast.90, bf16[128,128]{1,0:T(8,128)(2,1)S(1)} %bitcast.93, ...), custom_call_target="tpu_custom_call" | custom-call | flops 2147483648 | bytes 5242880 | tf_op jit(solution)/shard_map/pallas_call | solution.py:222
  102.3 10.6 %shard_map.94.rest_0_ = f32[256,2048]{1,0:T(8,128)S(1)} custom-call(s32[1]{0:T(128)} %constant.162.clone.1.offs_ref, f32[1]{0:T(128)} %get-tuple-element.76.bg_ref, bf16[3,1,256,2048]{3,2,1,0:T(8,128)(2,1)} %all-gather.3.cloned.1.call-done.raw_ref, bf16[128,128]{1,0:T(8,128)(2,1)S(1)} %bitcast.89, bf16[128,128]{1,0:T(8,128)(2,1)S(1)} %bitcast.92, ...), custom_call_target="tpu_custom_call" | custom-call | flops 2147483648 | bytes 5242880 | tf_op jit(solution)/shard_map/pallas_call | solution.py:222
  113.0 10.4 %shard_map.95 = f32[256,2048]{1,0:T(8,128)S(1)} custom-call(s32[1]{0:T(128)} %constant.162.clone.1.offs_ref, f32[1]{0:T(128)} %get-tuple-element.77.bg_ref, bf16[3,1,256,2048]{3,2,1,0:T(8,128)(2,1)} %all-gather.3.cloned.1.call-done.raw_ref, bf16[128,128]{1,0:T(8,128)(2,1)S(1)} %bitcast.88, bf16[128,128]{1,0:T(8,128)(2,1)S(1)} %bitcast.91, ...), custom_call_target="tpu_custom_call" | custom-call | flops 2147483648 | bytes 5242880 | tf_op jit(solution)/shard_map/pallas_call | solution.py:222
  (146 shorter events, 26.6 us)
Async XLA Ops:
  6.5 18.6 %copy-start.36 = (s32[4]{0:T(128)S(1)}, s32[4]{0:T(128)}, u32[]{:S(2)}) copy-start(s32[4]{0:T(128)} %param.16) | copy-start | bytes 52
  6.5 20.4 %copy-start.34 = (f32[4,4,17]{2,1,0:T(4,128)S(1)}, f32[4,4,17]{2,1,0:T(4,128)}, u32[]{:S(2)}) copy-start(f32[4,4,17]{2,1,0:T(4,128)} %param.14) | copy-start | bytes 3268
  6.5 21.1 %copy-start.35 = (f32[4,4,17]{2,1,0:T(4,128)S(1)}, f32[4,4,17]{2,1,0:T(4,128)}, u32[]{:S(2)}) copy-start(f32[4,4,17]{2,1,0:T(4,128)} %param.15) | copy-start | bytes 3268
  6.5 44.4 %all-gather.5.cloned.1.call-start = ((), (), s32[]{:S(2)}) async-start(), calls=%async_computation.1 | async-start | bytes 1179648 | tf_op jit(solution)/shard_map/all_gather | solution.py:448
  8.4 76.4 %all-gather.3.cloned.1.call-start = ((), (), s32[]{:S(2)}) async-start(), calls=%async_computation | async-start | bytes 3538944 | tf_op jit(solution)/shard_map/all_gather | solution.py:449
  8.4 37.5 %collective-permute-start.3 = (f32[1,32,2048]{2,1,0:T(8,128)}, f32[1,32,2048]{2,1,0:T(8,128)}, u32[]{:S(2)}, u32[]{:S(2)}) collective-permute-start(f32[1,32,2048]{2,1,0:T(8,128)} %param.9), channel_id=1, source_target_pairs={{0,2},{1,3},{2,4},{3,5},{4,6},{5,7},{6,0},{7,1},{8,10},{9,11},{10,... | collective-permute-start | bytes 786440 | tf_op jit(solution)/shard_map/ppermute | solution.py:15
  11.5 35.0 %collective-permute-start.4 = (f32[1,32,2048]{2,1,0:T(8,128)}, f32[1,32,2048]{2,1,0:T(8,128)}, u32[]{:S(2)}, u32[]{:S(2)}) collective-permute-start(f32[1,32,2048]{2,1,0:T(8,128)} %param.9), channel_id=1, source_target_pairs={{0,4},{1,5},{2,6},{3,7},{4,0},{5,1},{6,2},{7,3},{8,12},{9,13},{10,... | collective-permute-start | bytes 786440 | tf_op jit(solution)/shard_map/ppermute | solution.py:15
  14.1 6.1 %collective-permute-start = (bf16[1,32,2048]{2,1,0:T(8,128)(2,1)S(1)}, bf16[1,32,2048]{2,1,0:T(8,128)(2,1)S(1)}, u32[]{:S(2)}, u32[]{:S(2)}) collective-permute-start(bf16[1,32,2048]{2,1,0:T(8,128)(2,1)S(1)} %get-tuple-element.53), channel_id=1, source_target_pairs={{0,24},{8,0},{16,8},{24,16},{1,25},{9,1},{17,9},{25,17},{2,26},{10... | collective-permute-start | bytes 393224 | tf_op jit(solution)/shard_map/ppermute | solution.py:15
  16.6 7.3 %collective-permute-start.1 = (bf16[1,32,2048]{2,1,0:T(8,128)(2,1)S(1)}, bf16[1,32,2048]{2,1,0:T(8,128)(2,1)S(1)}, u32[]{:S(2)}, u32[]{:S(2)}) collective-permute-start(bf16[1,32,2048]{2,1,0:T(8,128)(2,1)S(1)} %get-tuple-element.52), channel_id=1, source_target_pairs={{0,16},{8,24},{16,0},{24,8},{1,17},{9,25},{17,1},{25,9},{2,18},{10... | collective-permute-start | bytes 393224 | tf_op jit(solution)/shard_map/ppermute | solution.py:15
  17.1 6.8 %collective-permute-start.2 = (bf16[1,32,2048]{2,1,0:T(8,128)(2,1)S(1)}, bf16[1,32,2048]{2,1,0:T(8,128)(2,1)S(1)}, u32[]{:S(2)}, u32[]{:S(2)}) collective-permute-start(bf16[1,32,2048]{2,1,0:T(8,128)(2,1)S(1)} %get-tuple-element.54), channel_id=1, source_target_pairs={{0,8},{8,16},{16,24},{24,0},{1,9},{9,17},{17,25},{25,1},{2,10},{10... | collective-permute-start | bytes 393224 | tf_op jit(solution)/shard_map/ppermute | solution.py:15
  20.2 26.4 %collective-permute-start.5 = (f32[1,32,2048]{2,1,0:T(8,128)}, f32[1,32,2048]{2,1,0:T(8,128)}, u32[]{:S(2)}, u32[]{:S(2)}) collective-permute-start(f32[1,32,2048]{2,1,0:T(8,128)} %param.9), channel_id=1, source_target_pairs={{0,6},{1,7},{2,0},{3,1},{4,2},{5,3},{6,4},{7,5},{8,14},{9,15},{10,... | collective-permute-start | bytes 786440 | tf_op jit(solution)/shard_map/ppermute | solution.py:15
  23.9 27.0 %collective-permute-start.6 = (f32[1,32,2048]{2,1,0:T(8,128)}, f32[1,32,2048]{2,1,0:T(8,128)}, u32[]{:S(2)}, u32[]{:S(2)}) collective-permute-start(f32[1,32,2048]{2,1,0:T(8,128)} %param.9), channel_id=1, source_target_pairs={{0,1},{1,0},{2,3},{3,2},{4,5},{5,4},{6,7},{7,6},{8,9},{9,8},{10,11... | collective-permute-start | bytes 786440 | tf_op jit(solution)/shard_map/ppermute | solution.py:455
  45.9 5.0 %collective-permute-start.7 = (f32[1,32,2048]{2,1,0:T(8,128)}, f32[1,32,2048]{2,1,0:T(8,128)}, u32[]{:S(2)}, u32[]{:S(2)}) collective-permute-start(f32[1,32,2048]{2,1,0:T(8,128)} %collective-permute-done.3), channel_id=1, source_target_pairs={{0,1},{1,0},{2,3},{3,2},{4,5},{5,4},{6,7},{7,6},{8,9},{9,8},{10,11... | collective-permute-start | bytes 786440 | tf_op jit(solution)/shard_map/ppermute | solution.py:455
  46.5 4.5 %collective-permute-start.8 = (f32[1,32,2048]{2,1,0:T(8,128)}, f32[1,32,2048]{2,1,0:T(8,128)}, u32[]{:S(2)}, u32[]{:S(2)}) collective-permute-start(f32[1,32,2048]{2,1,0:T(8,128)} %collective-permute-done.4), channel_id=1, source_target_pairs={{0,1},{1,0},{2,3},{3,2},{4,5},{5,4},{6,7},{7,6},{8,9},{9,8},{10,11... | collective-permute-start | bytes 786440 | tf_op jit(solution)/shard_map/ppermute | solution.py:455
  46.6 4.4 %collective-permute-start.9 = (f32[1,32,2048]{2,1,0:T(8,128)}, f32[1,32,2048]{2,1,0:T(8,128)}, u32[]{:S(2)}, u32[]{:S(2)}) collective-permute-start(f32[1,32,2048]{2,1,0:T(8,128)} %collective-permute-done.5), channel_id=1, source_target_pairs={{0,1},{1,0},{2,3},{3,2},{4,5},{5,4},{6,7},{7,6},{8,9},{9,8},{10,11... | collective-permute-start | bytes 786440 | tf_op jit(solution)/shard_map/ppermute | solution.py:455
  61.3 23.6 %copy-start.32 = (f32[512]{0:T(512)S(1)}, f32[512]{0:T(512)}, u32[]{:S(2)}) copy-start(f32[512]{0:T(512)} %broadcast_maximum_fusion.1) | copy-start | bytes 6148
  91.7 10.5 %copy-start.8 = (bf16[3,128,128]{2,1,0:T(8,128)(2,1)S(1)}, bf16[3,128,128]{2,1,0:T(8,128)(2,1)}, u32[]{:S(2)}) copy-start(bf16[3,128,128]{2,1,0:T(8,128)(2,1)} %get-tuple-element.57.bb_ref) | copy-start | bytes 294916
  91.7 10.5 %copy-start.9 = (bf16[3,128,128]{2,1,0:T(8,128)(2,1)S(1)}, bf16[3,128,128]{2,1,0:T(8,128)(2,1)}, u32[]{:S(2)}) copy-start(bf16[3,128,128]{2,1,0:T(8,128)(2,1)} %get-tuple-element.61.bf_ref) | copy-start | bytes 294916
  91.7 10.5 %copy-start.15 = (bf16[1,128,128]{2,1,0:T(8,128)(2,1)S(1)}, bf16[1,128,128]{2,1,0:T(8,128)(2,1)}, u32[]{:S(2)}) copy-start(bf16[1,128,128]{2,1,0:T(8,128)(2,1)} %copy-done.14) | copy-start | bytes 98308
  91.7 10.5 %copy-start.19 = (bf16[1,128,128]{1,2,0:T(8,128)(2,1)S(1)}, bf16[1,128,128]{1,2,0:T(8,128)(2,1)}, u32[]{:S(2)}) copy-start(bf16[1,128,128]{1,2,0:T(8,128)(2,1)} %copy.20) | copy-start | bytes 98308
  102.2 10.8 %copy-start.6 = (bf16[3,128,128]{2,1,0:T(8,128)(2,1)S(1)}, bf16[3,128,128]{2,1,0:T(8,128)(2,1)}, u32[]{:S(2)}) copy-start(bf16[3,128,128]{2,1,0:T(8,128)(2,1)} %get-tuple-element.58.bb_ref) | copy-start | bytes 294916
  102.2 10.8 %copy-start.7 = (bf16[3,128,128]{2,1,0:T(8,128)(2,1)S(1)}, bf16[3,128,128]{2,1,0:T(8,128)(2,1)}, u32[]{:S(2)}) copy-start(bf16[3,128,128]{2,1,0:T(8,128)(2,1)} %get-tuple-element.62.bf_ref) | copy-start | bytes 294916
  102.2 10.8 %copy-start.13 = (bf16[1,128,128]{2,1,0:T(8,128)(2,1)S(1)}, bf16[1,128,128]{2,1,0:T(8,128)(2,1)}, u32[]{:S(2)}) copy-start(bf16[1,128,128]{2,1,0:T(8,128)(2,1)} %copy-done.12) | copy-start | bytes 98308
  102.2 10.8 %copy-start.18 = (bf16[1,128,128]{1,2,0:T(8,128)(2,1)S(1)}, bf16[1,128,128]{1,2,0:T(8,128)(2,1)}, u32[]{:S(2)}) copy-start(bf16[1,128,128]{1,2,0:T(8,128)(2,1)} %copy.18) | copy-start | bytes 98308
  (25 other events, 55.3 us)
Sparse Core Ops, SparseCore 0:
  9.0 35.4 all-gather.4
  46.0 38.7 all-gather.2

commit v5 on v4

--- a/solution.py
+++ b/solution.py
@@ -1,3 +1,5 @@
+import functools
+
 import jax
 import jax.numpy as jnp
 from jax import lax
@@ -100,17 +102,21 @@
     return estimate * from_blocks(correction, rows, plane_width).astype(jnp.float32)
 
 
-def plane_kernel(offs_ref, bg_ref, raw_ref, m_ref, mt_ref, s_ref, cnt_ref, g_ref, bf_ref, bb_ref,
-                 a_ref, at_ref, *rest):
-    *piece_refs, out_ref, est_whole, work, joined, across, ratio = rest
+def plane_kernel(est_count, offs_ref, roffs_ref, bg_ref, m_ref, mt_ref, s_ref, cnt_ref, g_ref,
+                 bf_ref, bb_ref, a_ref, at_ref, *rest):
+    *piece_refs, out_ref, est_whole, raw_whole, work, joined, across, ratio = rest
     rows, plane_width = out_ref.shape
-    if len(piece_refs) == 1:
-        est_ref = piece_refs[0]
-    else:
-        est_ref = est_whole
-        for k, piece in enumerate(piece_refs):
+
+    def assemble(refs, offsets_ref, whole):
+        if len(refs) == 1:
+            return refs[0]
+        for k, piece in enumerate(refs):
             piece_rows = piece.shape[0]
-            est_ref[pl.ds(pl.multiple_of(offs_ref[k], BR), piece_rows), :] = piece[...]
+            whole[pl.ds(pl.multiple_of(offsets_ref[k], 2 * BR), piece_rows), :] = piece[...]
+        return whole
+
+    est_ref = assemble(piece_refs[:est_count], offs_ref, est_whole)
+    raw_ref = assemble(piece_refs[est_count:], roffs_ref, raw_whole)
     nt = rows // BR
     nc = plane_width // BW
     f32 = jnp.float32
@@ -204,8 +210,8 @@
     )(row_taps.astype(jnp.float32).reshape(-1), col_taps.astype(jnp.float32).reshape(-1))
 
 
-def kernel_update(est_pieces, offsets, raw_all, raw_index, matrix, landing, bands, level):
-    rows, plane_width = raw_all.shape[-2:]
+def kernel_update(est_pieces, offsets, raw_pieces, raw_offsets, matrix, landing, bands, level):
+    rows, plane_width = raw_pieces[0][0].shape[-2] * len(raw_pieces), raw_pieces[0][0].shape[-1]
     nt = rows // BR
     nc = plane_width // BW
     blocks = nt * nc
@@ -218,15 +224,19 @@
     count = jnp.broadcast_to(jnp.maximum(count, 1.0)[:, None], (blocks, BW))
     vmem = pl.BlockSpec(memory_space=pltpu.VMEM)
     smem = pl.BlockSpec(memory_space=pltpu.SMEM)
-    raw_spec = pl.BlockSpec((None, None, rows, plane_width), lambda i: raw_index + (0, 0))
+    raw_specs = [
+        pl.BlockSpec((None, None) + array.shape[2:], lambda i, at=at: at + (0, 0))
+        for array, at in raw_pieces
+    ]
     return pl.pallas_call(
-        plane_kernel,
+        functools.partial(plane_kernel, len(est_pieces)),
         grid=(1,),
         out_shape=jax.ShapeDtypeStruct((rows, plane_width), jnp.float32),
-        in_specs=[smem, smem, raw_spec] + [vmem] * (9 + len(est_pieces)),
+        in_specs=[smem, smem, smem] + [vmem] * (9 + len(est_pieces)) + raw_specs,
         out_specs=vmem,
         scratch_shapes=[
             pltpu.VMEM((rows, plane_width), jnp.float32),
+            pltpu.VMEM((rows, plane_width), jnp.bfloat16),
             pltpu.VMEM((nc, rows, BW), jnp.float32),
             pltpu.VMEM((nc, rows, BW), jnp.float32),
             pltpu.VMEM((rows, plane_width), jnp.bfloat16),
@@ -240,8 +250,8 @@
         ),
     )(
         offsets,
+        raw_offsets,
         jnp.reshape(level, (1,)).astype(jnp.float32),
-        raw_all,
         matrix,
         matrix.T,
         sum_mat.astype(jnp.bfloat16),
@@ -252,6 +262,7 @@
         bands[0],
         bands[1],
         *est_pieces,
+        *[array for array, _ in raw_pieces],
     )
 
 
@@ -446,7 +457,7 @@
         piece = own_piece if update_index == 0 else passed_along(own_piece, "view", -update_index)
         pieces.append(piece)
     first_raw = lax.all_gather(jnp.stack(pieces[:1]), "tile", axis=2, tiled=True)
-    later_raw = lax.all_gather(jnp.stack(pieces[1:]), "tile", axis=2, tiled=True)
+    second_raw = lax.all_gather(jnp.stack(pieces[1:2]), "tile", axis=2, tiled=True)
     tile_count = lax.axis_size("tile")
     along = [initial_estimate] + [
         passed_along(initial_estimate, "tile", shift) for shift in range(2, tile_count, 2)
@@ -456,6 +467,11 @@
     sources = [(my_tile - shift) % tile_count for shift in range(0, tile_count, 2)]
     sources = sources + [(source ^ 1) for source in sources]
     offsets = jnp.stack(sources).astype(jnp.int32) * tile_rows
+    late_raw, _ = lax.optimization_barrier((jnp.stack(pieces[2:]), arrived))
+    late_along = [late_raw] + [
+        passed_along(late_raw, "tile", shift) for shift in range(2, tile_count, 2)
+    ]
+    late_arrived = late_along + [lax.ppermute(piece, "tile", partner) for piece in late_along]
     whole_plane = jnp.zeros((1,), jnp.int32)
     plane_bands = lax.dynamic_slice_in_dim(psf_band, my_group * planes, planes, 0)
     views_in_order = (my_group + jnp.arange(view_count, dtype=jnp.int32)) % view_count
@@ -464,6 +480,11 @@
         col_psf[views_in_order][:, plane_bands].reshape(view_count * planes, TAPS),
         tile_rows * lax.axis_size("tile"),
     )
+    def raw_source(update_index, p):
+        if update_index < 2:
+            return [((first_raw, second_raw)[update_index], (0, p))]
+        return [(piece, (update_index - 2, p)) for piece in late_arrived]
+
     for update_index in range(view_count):
         view_index = (my_group + update_index) % view_count
         matrix = interp[view_index]
@@ -474,8 +495,8 @@
                 kernel_update(
                     [piece[p] for piece in arrived] if update_index == 0 else [estimate[p]],
                     offsets if update_index == 0 else whole_plane,
-                    first_raw if update_index == 0 else later_raw,
-                    (0 if update_index == 0 else update_index - 1, p),
+                    raw_source(update_index, p),
+                    whole_plane if update_index < 2 else offsets,
                     matrix,
                     landing,
                     [b[update_index * planes + p] for b in bands],

time: 132 us -> 168 us (1.27)
  the two profiles are of different devices: /device:TPU:0 before, /device:TPU:9 now
where the time goes in v5:
time: 168 us; the launch traced here: 166 us
  local copies, waits for them, and re-layouts  50.4 us (30%)
  Pallas kernels  49.1 us (29%)
  starting transfers between devices  31.2 us (19%)
  between operations  15.9 us (9%)
  waiting for transfers between devices  11.3 us (7%)
  other arithmetic  8.1 us (5%)
    pallas_call x4, Pallas kernels, kernel_update(): pl.pallas_call(functools.partial(plane_kernel, len(est_pieces)), grid=(1,...  44.1 us
    unnamed x110, local copies, waits for them, and re-layouts  30.4 us
    ppermute x4, starting transfers between devices, local(): lax.ppermute(piece, 'tile', partner)  18.5 us
    ppermute x9, waiting for transfers between devices, passed_along(): return lax.ppermute(x, axis, [(i, (i + by) % count) for i in range(count)])  11.3 us
    ppermute x9, starting transfers between devices, passed_along(): return lax.ppermute(x, axis, [(i, (i + by) % count) for i in range(count)])  9.46 us
    squeeze x4, local copies, waits for them, and re-layouts, local(): b[update_index * planes + p]  6.31 us
    pallas_call x1, Pallas kernels, all_bands(): pl.pallas_call(band_kernel, out_shape=(jax.ShapeDtypeStruct((count, rows,...  4.99 us
  transfers between devices with their start and end apart: 19, of which 5 were waited for; matrix products, arithmetic and copies ran while one was open for 16% of the time, Pallas kernels for 16%

profile of v5, /device:TPU:9, one launch (start us, length us, event | category | flops | bytes accessed | tf_op | source)
XLA Modules:
  0.0 166.0 jit_solution(12466210206333299923)
XLA Ops:
  8.8 1.5 collective-permute-start.2
  10.3 1.5 collective-permute-start.3
  11.8 1.8 %dynamic-slice_bitcast_fusion.2 = (bf16[1,32,2048]{2,1,0:T(8,128)(2,1)S(1)}, bf16[1,32,2048]{2,1,0:T(8,128)(2,1)S(1)}, bf16[1,1,32,2048]{3,2,1,0:T(8,128)(2,1)}, bf16[1,32,2048]{2,1,0:T(8,128)(2,1)S(1)}) fusion(bf16[1,4,32,2048]{3,2,1,0:T(8,128)(2,1)} %param.10, s32[]{:T(128)S(6)} %select_n.240, s32[]{:T(128)S(6)} %select_n.238, s32[]{:T(128)S(6)} %select_n.234, ...), kind=kLoop, calls=%fused_computation.31 | loop fusion | bytes 1048592 | tf_op jit(solution)/shard_map/dynamic_slice | solution.py:454
  13.7 2.2 %collective-permute-start.7 = (bf16[1,32,2048]{2,1,0:T(8,128)(2,1)S(1)}, bf16[1,32,2048]{2,1,0:T(8,128)(2,1)S(1)}, u32[]{:S(2)}, u32[]{:S(2)}) collective-permute-start(bf16[1,32,2048]{2,1,0:T(8,128)(2,1)S(1)} %get-tuple-element.46), channel_id=1, source_target_pairs={{0,24},{8,0},{16,8},{24,16},{1,25},{9,1},{17,9},{25,17},{2,26},{10... | collective-permute-start | bytes 393224 | tf_op jit(solution)/shard_map/ppermute | solution.py:17
  26.6 5.0 %shard_map.91 = (bf16[4,256,256]{2,1,0:T(8,128)(2,1)}, bf16[4,256,256]{2,1,0:T(8,128)(2,1)}, bf16[4,3,128,128]{3,2,1,0:T(8,128)(2,1)}, bf16[4,3,128,128]{3,2,1,0:T(8,128)(2,1)}) custom-call(f32[68]{0:T(128)} %reshape.563.row_ref, f32[68]{0:T(128)} %reshape.564.col_ref), custom_call_target="tpu_custom_call" | custom-call | tf_op jit(solution)/shard_map/pallas_call | solution.py:200
  31.6 1.9 %slice_bitcast_fusion.8 = (bf16[3,128,128]{2,1,0:T(8,128)(2,1)}, bf16[3,128,128]{2,1,0:T(8,128)(2,1)}, bf16[3,128,128]{2,1,0:T(8,128)(2,1)}, bf16[3,128,128]{2,1,0:T(8,128)(2,1)}) fusion(bf16[4,3,128,128]{3,2,1,0:T(8,128)(2,1)} %get-tuple-element.11), kind=kLoop, calls=%fused_computation.41 | loop fusion | bytes 786432 | tf_op jit(solution)/shard_map/squeeze | solution.py:502
  33.5 1.8 %slice_bitcast_fusion.9 = (bf16[3,128,128]{2,1,0:T(8,128)(2,1)}, bf16[3,128,128]{2,1,0:T(8,128)(2,1)}, bf16[3,128,128]{2,1,0:T(8,128)(2,1)}, bf16[3,128,128]{2,1,0:T(8,128)(2,1)}) fusion(bf16[4,3,128,128]{3,2,1,0:T(8,128)(2,1)} %get-tuple-element.10), kind=kLoop, calls=%fused_computation.42 | loop fusion | bytes 786432 | tf_op jit(solution)/shard_map/squeeze | solution.py:502
  35.3 1.8 %slice_bitcast_fusion = (bf16[256,256]{1,0:T(8,128)(2,1)}, bf16[256,256]{1,0:T(8,128)(2,1)}, bf16[256,256]{1,0:T(8,128)(2,1)}, bf16[256,256]{1,0:T(8,128)(2,1)S(1)}) fusion(bf16[4,256,256]{2,1,0:T(8,128)(2,1)} %get-tuple-element.13), kind=kLoop, calls=%fused_computation.33 | loop fusion | bytes 1048576 | tf_op jit(solution)/shard_map/squeeze | solution.py:502
  43.5 2.4 %collective-permute-done.8 = bf16[1,32,2048]{2,1,0:T(8,128)(2,1)S(1)} collective-permute-done((bf16[1,32,2048]{2,1,0:T(8,128)(2,1)S(1)}, bf16[1,32,2048]{2,1,0:T(8,128)(2,1)S(1)}, u32[]{:S(2)}, u32[]{:S(2)}) %collective-permute-start.8) | collective-permute-done | bytes 131104 | tf_op jit(solution)/shard_map/ppermute | solution.py:17
  48.2 2.3 %collective-permute-done.9 = bf16[1,32,2048]{2,1,0:T(8,128)(2,1)S(1)} collective-permute-done((bf16[1,32,2048]{2,1,0:T(8,128)(2,1)S(1)}, bf16[1,32,2048]{2,1,0:T(8,128)(2,1)S(1)}, u32[]{:S(2)}, u32[]{:S(2)}) %collective-permute-start.9) | collective-permute-done | bytes 131104 | tf_op jit(solution)/shard_map/ppermute | solution.py:17
  53.5 3.2 %collective-permute-start.11 = (bf16[2,1,32,2048]{3,2,1,0:T(8,128)(2,1)S(1)}, bf16[2,1,32,2048]{3,2,1,0:T(8,128)(2,1)S(1)}, u32[]{:S(2)}, u32[]{:S(2)}) collective-permute-start(bf16[2,1,32,2048]{3,2,1,0:T(8,128)(2,1)S(1)} %pad_maximum_fusion.rest_1_), channel_id=1, source_target_pairs={{0,4},{1,5},{2,6},{3,7},{4,0},{5,1},{6,2},{7,3},{8,12},{9,13},{10,... | collective-permute-start | bytes 786440 | tf_op jit(solution)/shard_map/ppermute | solution.py:17
  59.5 1.5 fusion.48
  61.3 2.9 %collective-permute-start.13 = (bf16[2,1,32,2048]{3,2,1,0:T(8,128)(2,1)S(1)}, bf16[2,1,32,2048]{3,2,1,0:T(8,128)(2,1)S(1)}, u32[]{:S(2)}, u32[]{:S(2)}) collective-permute-start(bf16[2,1,32,2048]{3,2,1,0:T(8,128)(2,1)S(1)} %pad_maximum_fusion.rest_1_), channel_id=1, source_target_pairs={{0,1},{1,0},{2,3},{3,2},{4,5},{5,4},{6,7},{7,6},{8,9},{9,8},{10,11... | collective-permute-start | bytes 786440 | tf_op jit(solution)/shard_map/ppermute | solution.py:474
  64.2 1.8 %collective-permute-done.10.rest_2_ = bf16[2,1,32,2048]{3,2,1,0:T(8,128)(2,1)S(1)} collective-permute-done((bf16[2,1,32,2048]{3,2,1,0:T(8,128)(2,1)S(1)}, bf16[2,1,32,2048]{3,2,1,0:T(8,128)(2,1)S(1)}, u32[]{:S(2)}, u32[]{:S(2)}) %collective-permute-start.10) | collective-permute-done | bytes 262176 | tf_op jit(solution)/shard_map/ppermute | solution.py:17
  66.0 13.4 %collective-permute-start.14 = (bf16[2,1,32,2048]{3,2,1,0:T(8,128)(2,1)S(1)}, bf16[2,1,32,2048]{3,2,1,0:T(8,128)(2,1)}, u32[]{:S(2)}, u32[]{:S(2)}) collective-permute-start(bf16[2,1,32,2048]{3,2,1,0:T(8,128)(2,1)S(1)} %collective-permute-done.10.rest_2_), channel_id=1, source_target_pairs={{0,1},{1,0},{2,3},{3,2},{4,5},{5,4},{6,7},{7,6},{8,9},{9,8},{10,11... | collective-permute-start | bytes 786440 | tf_op jit(solution)/shard_map/ppermute | solution.py:474
  79.3 3.3 %collective-permute-done.11.rest_3_ = bf16[2,1,32,2048]{3,2,1,0:T(8,128)(2,1)S(1)} collective-permute-done((bf16[2,1,32,2048]{3,2,1,0:T(8,128)(2,1)S(1)}, bf16[2,1,32,2048]{3,2,1,0:T(8,128)(2,1)S(1)}, u32[]{:S(2)}, u32[]{:S(2)}) %collective-permute-start.11) | collective-permute-done | bytes 262176 | tf_op jit(solution)/shard_map/ppermute | solution.py:17
  82.6 1.4 collective-permute-start.15
  84.0 1.5 collective-permute-done.12.rest_4_
  102.5 11.2 %shard_map.92.rest_0_ = f32[256,2048]{1,0:T(8,128)} custom-call(s32[8]{0:T(128)S(1)} %broadcast_multiply_fusion.offs_ref.roffs_ref, s32[1]{0:T(128)} %constant.162.clone.1.roffs_ref.offs_ref, f32[1]{0:T(128)} %get-tuple-element.77.bg_ref, bf16[128,128]{1,0:T(8,128)(2,1)S(1)} %bitcast.93, bf16[128,128]{1,0:T(8,128)(2,1)S(1)} %bitcast.95, ...), custom_call_target="tpu_custom_call" | custom-call | flops 2147483648 | bytes 5242880 | tf_op jit(solution)/shard_map/pallas_call | solution.py:231
  122.3 11.0 %shard_map.93.rest_0_ = f32[256,2048]{1,0:T(8,128)S(1)} custom-call(s32[1]{0:T(128)} %constant.162.clone.1.roffs_ref.offs_ref, s32[1]{0:T(128)} %constant.162.clone.1.roffs_ref.offs_ref, f32[1]{0:T(128)} %get-tuple-element.80.bg_ref, bf16[128,128]{1,0:T(8,128)(2,1)S(1)} %bitcast.92, bf16[128,128]{1,0:T(8,128)(2,1)S(1)} %bitcast.94, ...), custom_call_target="tpu_custom_call" | custom-call | flops 2147483648 | bytes 5242880 | tf_op jit(solution)/shard_map/pallas_call | solution.py:231
  133.4 1.3 copy-done.1
  135.0 10.8 %shard_map.94.rest_0_ = f32[256,2048]{1,0:T(8,128)S(1)} custom-call(s32[1]{0:T(128)} %constant.162.clone.1.roffs_ref.offs_ref, s32[8]{0:T(128)S(1)} %broadcast_multiply_fusion.offs_ref.roffs_ref, f32[1]{0:T(128)} %get-tuple-element.78.bg_ref, bf16[128,128]{1,0:T(8,128)(2,1)S(1)} %bitcast.89, bf16[128,128]{1,0:T(8,128)(2,1)S(1)} %bitcast.91, ...), custom_call_target="tpu_custom_call" | custom-call | flops 2147483648 | bytes 5242880 | tf_op jit(solution)/shard_map/pallas_call | solution.py:231
  145.8 1.3 copy-done
  147.3 11.1 %shard_map.95 = f32[256,2048]{1,0:T(8,128)S(1)} custom-call(s32[1]{0:T(128)} %constant.162.clone.1.roffs_ref.offs_ref, s32[8]{0:T(128)S(1)} %broadcast_multiply_fusion.offs_ref.roffs_ref, f32[1]{0:T(128)} %get-tuple-element.79.bg_ref, bf16[128,128]{1,0:T(8,128)(2,1)S(1)} %bitcast.88, bf16[128,128]{1,0:T(8,128)(2,1)S(1)} %bitcast.90, ...), custom_call_target="tpu_custom_call" | custom-call | flops 2147483648 | bytes 5242880 | tf_op jit(solution)/shard_map/pallas_call | solution.py:231
  (196 shorter events, 52.4 us)
Async XLA Ops:
  6.5 79.8 %all-gather.4.cloned.1.call-start = ((), (), s32[]{:S(2)}) async-start(), calls=%async_computation | async-start | bytes 1179648 | tf_op jit(solution)/shard_map/all_gather | solution.py:459
  6.5 39.3 %collective-permute-start = (f32[1,32,2048]{2,1,0:T(8,128)}, f32[1,32,2048]{2,1,0:T(8,128)S(1)}, u32[]{:S(2)}, u32[]{:S(2)}) collective-permute-start(f32[1,32,2048]{2,1,0:T(8,128)} %param.9), channel_id=1, source_target_pairs={{0,2},{1,3},{2,4},{3,5},{4,6},{5,7},{6,0},{7,1},{8,10},{9,11},{10,... | collective-permute-start | bytes 786440 | tf_op jit(solution)/shard_map/ppermute | solution.py:17
  7.8 39.2 %collective-permute-start.1 = (f32[1,32,2048]{2,1,0:T(8,128)}, f32[1,32,2048]{2,1,0:T(8,128)S(1)}, u32[]{:S(2)}, u32[]{:S(2)}) collective-permute-start(f32[1,32,2048]{2,1,0:T(8,128)} %param.9), channel_id=1, source_target_pairs={{0,4},{1,5},{2,6},{3,7},{4,0},{5,1},{6,2},{7,3},{8,12},{9,13},{10,... | collective-permute-start | bytes 786440 | tf_op jit(solution)/shard_map/ppermute | solution.py:17
  8.8 38.3 %collective-permute-start.2 = (f32[1,32,2048]{2,1,0:T(8,128)}, f32[1,32,2048]{2,1,0:T(8,128)S(1)}, u32[]{:S(2)}, u32[]{:S(2)}) collective-permute-start(f32[1,32,2048]{2,1,0:T(8,128)} %param.9), channel_id=1, source_target_pairs={{0,6},{1,7},{2,0},{3,1},{4,2},{5,3},{6,4},{7,5},{8,14},{9,15},{10,... | collective-permute-start | bytes 786440 | tf_op jit(solution)/shard_map/ppermute | solution.py:17
  10.3 40.3 %collective-permute-start.3 = (f32[1,32,2048]{2,1,0:T(8,128)}, f32[1,32,2048]{2,1,0:T(8,128)S(1)}, u32[]{:S(2)}, u32[]{:S(2)}) collective-permute-start(f32[1,32,2048]{2,1,0:T(8,128)} %param.9), channel_id=1, source_target_pairs={{0,1},{1,0},{2,3},{3,2},{4,5},{5,4},{6,7},{7,6},{8,9},{9,8},{10,11... | collective-permute-start | bytes 786440 | tf_op jit(solution)/shard_map/ppermute | solution.py:466
  13.6 100.1 %all-gather.6.cloned.1.call-start = ((), (), s32[]{:S(2)}) async-start(), calls=%async_computation.1 | async-start | bytes 1179648 | tf_op jit(solution)/shard_map/all_gather | solution.py:460
  13.7 27.3 %collective-permute-start.7 = (bf16[1,32,2048]{2,1,0:T(8,128)(2,1)S(1)}, bf16[1,32,2048]{2,1,0:T(8,128)(2,1)S(1)}, u32[]{:S(2)}, u32[]{:S(2)}) collective-permute-start(bf16[1,32,2048]{2,1,0:T(8,128)(2,1)S(1)} %get-tuple-element.46), channel_id=1, source_target_pairs={{0,24},{8,0},{16,8},{24,16},{1,25},{9,1},{17,9},{25,17},{2,26},{10... | collective-permute-start | bytes 393224 | tf_op jit(solution)/shard_map/ppermute | solution.py:17
  37.9 18.7 %copy-start.51 = (bf16[4,128,128]{2,1,0:T(8,128)(2,1)S(1)}, bf16[4,128,128]{2,1,0:T(8,128)(2,1)}, u32[]{:S(2)}) copy-start(bf16[4,128,128]{2,1,0:T(8,128)(2,1)} %param.13) | copy-start | bytes 393220
  41.0 4.9 %collective-permute-start.8 = (bf16[1,32,2048]{2,1,0:T(8,128)(2,1)S(1)}, bf16[1,32,2048]{2,1,0:T(8,128)(2,1)S(1)}, u32[]{:S(2)}, u32[]{:S(2)}) collective-permute-start(bf16[1,32,2048]{2,1,0:T(8,128)(2,1)S(1)} %get-tuple-element.45), channel_id=1, source_target_pairs={{0,16},{8,24},{16,0},{24,8},{1,17},{9,25},{17,1},{25,9},{2,18},{10... | collective-permute-start | bytes 393224 | tf_op jit(solution)/shard_map/ppermute | solution.py:17
  45.9 4.7 %collective-permute-start.9 = (bf16[1,32,2048]{2,1,0:T(8,128)(2,1)S(1)}, bf16[1,32,2048]{2,1,0:T(8,128)(2,1)S(1)}, u32[]{:S(2)}, u32[]{:S(2)}) collective-permute-start(bf16[1,32,2048]{2,1,0:T(8,128)(2,1)S(1)} %get-tuple-element.48), channel_id=1, source_target_pairs={{0,8},{8,16},{16,24},{24,0},{1,9},{9,17},{17,25},{25,1},{2,10},{10... | collective-permute-start | bytes 393224 | tf_op jit(solution)/shard_map/ppermute | solution.py:17
  45.9 13.7 %copy-start.36 = (f32[1,32,2048]{2,1,0:T(8,128)}, f32[1,32,2048]{2,1,0:T(8,128)S(1)}, u32[]{:S(2)}) copy-start(f32[1,32,2048]{2,1,0:T(8,128)S(1)} %collective-permute-done) | copy-start | bytes 786436
  45.9 5.5 %collective-permute-start.4 = (f32[1,32,2048]{2,1,0:T(8,128)S(1)}, f32[1,32,2048]{2,1,0:T(8,128)S(1)}, u32[]{:S(2)}, u32[]{:S(2)}) collective-permute-start(f32[1,32,2048]{2,1,0:T(8,128)S(1)} %collective-permute-done), channel_id=1, source_target_pairs={{0,1},{1,0},{2,3},{3,2},{4,5},{5,4},{6,7},{7,6},{8,9},{9,8},{10,11... | collective-permute-start | bytes 786440 | tf_op jit(solution)/shard_map/ppermute | solution.py:466
  47.1 5.0 %collective-permute-start.5 = (f32[1,32,2048]{2,1,0:T(8,128)S(1)}, f32[1,32,2048]{2,1,0:T(8,128)S(1)}, u32[]{:S(2)}, u32[]{:S(2)}) collective-permute-start(f32[1,32,2048]{2,1,0:T(8,128)S(1)} %collective-permute-done.1), channel_id=1, source_target_pairs={{0,1},{1,0},{2,3},{3,2},{4,5},{5,4},{6,7},{7,6},{8,9},{9,8},{10,11... | collective-permute-start | bytes 786440 | tf_op jit(solution)/shard_map/ppermute | solution.py:466
  47.2 5.6 %collective-permute-start.6 = (f32[1,32,2048]{2,1,0:T(8,128)S(1)}, f32[1,32,2048]{2,1,0:T(8,128)S(1)}, u32[]{:S(2)}, u32[]{:S(2)}) collective-permute-start(f32[1,32,2048]{2,1,0:T(8,128)S(1)} %collective-permute-done.2), channel_id=1, source_target_pairs={{0,1},{1,0},{2,3},{3,2},{4,5},{5,4},{6,7},{7,6},{8,9},{9,8},{10,11... | collective-permute-start | bytes 786440 | tf_op jit(solution)/shard_map/ppermute | solution.py:466
  53.5 12.5 %collective-permute-start.10 = (bf16[2,1,32,2048]{3,2,1,0:T(8,128)(2,1)S(1)}, bf16[2,1,32,2048]{3,2,1,0:T(8,128)(2,1)S(1)}, u32[]{:S(2)}, u32[]{:S(2)}) collective-permute-start(bf16[2,1,32,2048]{3,2,1,0:T(8,128)(2,1)S(1)} %pad_maximum_fusion.rest_1_), channel_id=1, source_target_pairs={{0,2},{1,3},{2,4},{3,5},{4,6},{5,7},{6,0},{7,1},{8,10},{9,11},{10,... | collective-permute-start | bytes 786440 | tf_op jit(solution)/shard_map/ppermute | solution.py:17
  53.5 29.2 %collective-permute-start.11 = (bf16[2,1,32,2048]{3,2,1,0:T(8,128)(2,1)S(1)}, bf16[2,1,32,2048]{3,2,1,0:T(8,128)(2,1)S(1)}, u32[]{:S(2)}, u32[]{:S(2)}) collective-permute-start(bf16[2,1,32,2048]{3,2,1,0:T(8,128)(2,1)S(1)} %pad_maximum_fusion.rest_1_), channel_id=1, source_target_pairs={{0,4},{1,5},{2,6},{3,7},{4,0},{5,1},{6,2},{7,3},{8,12},{9,13},{10,... | collective-permute-start | bytes 786440 | tf_op jit(solution)/shard_map/ppermute | solution.py:17
  56.6 28.8 %collective-permute-start.12 = (bf16[2,1,32,2048]{3,2,1,0:T(8,128)(2,1)S(1)}, bf16[2,1,32,2048]{3,2,1,0:T(8,128)(2,1)S(1)}, u32[]{:S(2)}, u32[]{:S(2)}) collective-permute-start(bf16[2,1,32,2048]{3,2,1,0:T(8,128)(2,1)S(1)} %pad_maximum_fusion.rest_1_), channel_id=1, source_target_pairs={{0,6},{1,7},{2,0},{3,1},{4,2},{5,3},{6,4},{7,5},{8,14},{9,15},{10,... | collective-permute-start | bytes 786440 | tf_op jit(solution)/shard_map/ppermute | solution.py:17
  61.3 73.4 %collective-permute-start.13 = (bf16[2,1,32,2048]{3,2,1,0:T(8,128)(2,1)S(1)}, bf16[2,1,32,2048]{3,2,1,0:T(8,128)(2,1)S(1)}, u32[]{:S(2)}, u32[]{:S(2)}) collective-permute-start(bf16[2,1,32,2048]{3,2,1,0:T(8,128)(2,1)S(1)} %pad_maximum_fusion.rest_1_), channel_id=1, source_target_pairs={{0,1},{1,0},{2,3},{3,2},{4,5},{5,4},{6,7},{7,6},{8,9},{9,8},{10,11... | collective-permute-start | bytes 786440 | tf_op jit(solution)/shard_map/ppermute | solution.py:474
  66.0 68.7 %collective-permute-start.14 = (bf16[2,1,32,2048]{3,2,1,0:T(8,128)(2,1)S(1)}, bf16[2,1,32,2048]{3,2,1,0:T(8,128)(2,1)}, u32[]{:S(2)}, u32[]{:S(2)}) collective-permute-start(bf16[2,1,32,2048]{3,2,1,0:T(8,128)(2,1)S(1)} %collective-permute-done.10.rest_2_), channel_id=1, source_target_pairs={{0,1},{1,0},{2,3},{3,2},{4,5},{5,4},{6,7},{7,6},{8,9},{9,8},{10,11... | collective-permute-start | bytes 786440 | tf_op jit(solution)/shard_map/ppermute | solution.py:474
  82.6 52.1 %collective-permute-start.15 = (bf16[2,1,32,2048]{3,2,1,0:T(8,128)(2,1)S(1)}, bf16[2,1,32,2048]{3,2,1,0:T(8,128)(2,1)}, u32[]{:S(2)}, u32[]{:S(2)}) collective-permute-start(bf16[2,1,32,2048]{3,2,1,0:T(8,128)(2,1)S(1)} %collective-permute-done.11.rest_3_), channel_id=1, source_target_pairs={{0,1},{1,0},{2,3},{3,2},{4,5},{5,4},{6,7},{7,6},{8,9},{9,8},{10,11... | collective-permute-start | bytes 786440 | tf_op jit(solution)/shard_map/ppermute | solution.py:474
  85.5 49.2 %collective-permute-start.16 = (bf16[2,1,32,2048]{3,2,1,0:T(8,128)(2,1)S(1)}, bf16[2,1,32,2048]{3,2,1,0:T(8,128)(2,1)}, u32[]{:S(2)}, u32[]{:S(2)}) collective-permute-start(bf16[2,1,32,2048]{3,2,1,0:T(8,128)(2,1)S(1)} %collective-permute-done.12.rest_4_), channel_id=1, source_target_pairs={{0,1},{1,0},{2,3},{3,2},{4,5},{5,4},{6,7},{7,6},{8,9},{9,8},{10,11... | collective-permute-start | bytes 786440 | tf_op jit(solution)/shard_map/ppermute | solution.py:474
  122.3 12.6 %copy-start.12 = (bf16[3,128,128]{2,1,0:T(8,128)(2,1)S(1)}, bf16[3,128,128]{2,1,0:T(8,128)(2,1)}, u32[]{:S(2)}) copy-start(bf16[3,128,128]{2,1,0:T(8,128)(2,1)} %get-tuple-element.63.bf_ref) | copy-start | bytes 294916
  122.3 12.6 %copy-start.16 = (bf16[1,128,128]{2,1,0:T(8,128)(2,1)S(1)}, bf16[1,128,128]{2,1,0:T(8,128)(2,1)}, u32[]{:S(2)}) copy-start(bf16[1,128,128]{2,1,0:T(8,128)(2,1)} %copy-done.15) | copy-start | bytes 98308
  122.3 12.6 %copy-start.18 = (bf16[1,128,128]{1,2,0:T(8,128)(2,1)S(1)}, bf16[1,128,128]{1,2,0:T(8,128)(2,1)}, u32[]{:S(2)}) copy-start(bf16[1,128,128]{1,2,0:T(8,128)(2,1)} %copy.20) | copy-start | bytes 98308
  (50 other events, 201.7 us)
Sparse Core Ops, SparseCore 0:
  13.8 27.4 all-gather.3
  42.9 31.1 all-gather.5

commit v6 on v4

--- a/solution.py
+++ b/solution.py
@@ -216,15 +216,30 @@
     pick_mat = place[:, None] == spots[None, :]
     count = jnp.sum(sum_mat.astype(jnp.float32), axis=1)
     count = jnp.broadcast_to(jnp.maximum(count, 1.0)[:, None], (blocks, BW))
-    vmem = pl.BlockSpec(memory_space=pltpu.VMEM)
     smem = pl.BlockSpec(memory_space=pltpu.SMEM)
+    operands = [
+        matrix,
+        matrix.T,
+        sum_mat.astype(jnp.bfloat16),
+        count,
+        pick_mat.astype(jnp.bfloat16),
+        bands[2],
+        bands[3],
+        bands[0],
+        bands[1],
+        *est_pieces,
+    ]
+
+    def whole(x):
+        return pl.BlockSpec(x.shape, lambda i, dims=len(x.shape): (0,) * dims)
+
     raw_spec = pl.BlockSpec((None, None, rows, plane_width), lambda i: raw_index + (0, 0))
     return pl.pallas_call(
         plane_kernel,
         grid=(1,),
         out_shape=jax.ShapeDtypeStruct((rows, plane_width), jnp.float32),
-        in_specs=[smem, smem, raw_spec] + [vmem] * (9 + len(est_pieces)),
-        out_specs=vmem,
+        in_specs=[smem, smem, raw_spec] + [whole(x) for x in operands],
+        out_specs=whole(jax.ShapeDtypeStruct((rows, plane_width), jnp.float32)),
         scratch_shapes=[
             pltpu.VMEM((rows, plane_width), jnp.float32),
             pltpu.VMEM((nc, rows, BW), jnp.float32),
@@ -238,21 +253,7 @@
             bytes_accessed=rows * plane_width * 10,
             transcendentals=0,
         ),
-    )(
-        offsets,
-        jnp.reshape(level, (1,)).astype(jnp.float32),
-        raw_all,
-        matrix,
-        matrix.T,
-        sum_mat.astype(jnp.bfloat16),
-        count,
-        pick_mat.astype(jnp.bfloat16),
-        bands[2],
-        bands[3],
-        bands[0],
-        bands[1],
-        *est_pieces,
-    )
+    )(offsets, jnp.reshape(level, (1,)).astype(jnp.float32), raw_all, *operands)
 
 
 def with_halo(cells, sides, width):

time: 132 us -> 132 us (level)
  no operation moved by 1% of the time
where the time goes in v6:
time: 132 us; the launch traced here: 131 us
  Pallas kernels  48.6 us (37%)
  local copies, waits for them, and re-layouts  34.9 us (26%)
  between operations  15.7 us (12%)
  waiting for transfers between devices  14.3 us (11%)
  starting transfers between devices  11.7 us (9%)
  other arithmetic  5.79 us (4%)
    pallas_call x4, Pallas kernels, kernel_update(): pl.pallas_call(plane_kernel, grid=(1,), out_shape=jax.ShapeDtypeStruct((r...  43.6 us
    unnamed x74, local copies, waits for them, and re-layouts  16.2 us
    all_gather x1, waiting for transfers between devices, local(): lax.all_gather(jnp.stack(pieces[1:]), 'tile', axis=2, tiled=True)  11.3 us
    ppermute x6, starting transfers between devices, passed_along(): return lax.ppermute(x, axis, [(i, (i + by) % count) for i in range(count)])  10.6 us
    squeeze x4, local copies, waits for them, and re-layouts, local(): b[update_index * planes + p]  6.25 us
    pallas_call x1, Pallas kernels, all_bands(): pl.pallas_call(band_kernel, out_shape=(jax.ShapeDtypeStruct((count, rows,...  5.01 us
    ppermute x6, waiting for transfers between devices, passed_along(): return lax.ppermute(x, axis, [(i, (i + by) % count) for i in range(count)])  2.92 us
    dynamic_slice x5, local copies, waits for them, and re-layouts, local(): matrix = interp[view_index]  2.89 us
  transfers between devices with their start and end apart: 12, of which 3 were waited for; matrix products, arithmetic and copies ran while one was open for 16% of the time, Pallas kernels for 13%

profile of v6, /device:TPU:0, one launch (start us, length us, event | category | flops | bytes accessed | tf_op | source)
XLA Modules:
  0.0 131.0 jit_solution(10721603372665212787)
XLA Ops:
  6.5 1.8 %constant_dynamic-slice_fusion.5 = (bf16[1,1,32,2048]{3,2,1,0:T(8,128)(2,1)}, bf16[1,32,2048]{2,1,0:T(8,128)(2,1)S(1)}, bf16[1,32,2048]{2,1,0:T(8,128)(2,1)S(1)}, bf16[1,32,2048]{2,1,0:T(8,128)(2,1)S(1)}) fusion(bf16[1,4,32,2048]{3,2,1,0:T(8,128)(2,1)} %param.10, s32[]{:T(128)S(6)} %select_n.240, s32[]{:T(128)S(6)} %select_n.218, s32[]{:T(128)S(6)} %select_n.216, ...), kind=kLoop, calls=%fused_computation.58 | loop fusion | bytes 1048592 | tf_op jit(solution)/shard_map/dynamic_slice | solution.py:444
  8.4 3.1 %collective-permute-start.3 = (f32[1,32,2048]{2,1,0:T(8,128)}, f32[1,32,2048]{2,1,0:T(8,128)}, u32[]{:S(2)}, u32[]{:S(2)}) collective-permute-start(f32[1,32,2048]{2,1,0:T(8,128)} %param.9), channel_id=1, source_target_pairs={{0,2},{1,3},{2,4},{3,5},{4,6},{5,7},{6,0},{7,1},{8,10},{9,11},{10,... | collective-permute-start | bytes 786440 | tf_op jit(solution)/shard_map/ppermute | solution.py:15
  11.5 2.6 %collective-permute-start.4 = (f32[1,32,2048]{2,1,0:T(8,128)}, f32[1,32,2048]{2,1,0:T(8,128)}, u32[]{:S(2)}, u32[]{:S(2)}) collective-permute-start(f32[1,32,2048]{2,1,0:T(8,128)} %param.9), channel_id=1, source_target_pairs={{0,4},{1,5},{2,6},{3,7},{4,0},{5,1},{6,2},{7,3},{8,12},{9,13},{10,... | collective-permute-start | bytes 786440 | tf_op jit(solution)/shard_map/ppermute | solution.py:15
  14.1 2.4 %collective-permute-start = (bf16[1,32,2048]{2,1,0:T(8,128)(2,1)S(1)}, bf16[1,32,2048]{2,1,0:T(8,128)(2,1)S(1)}, u32[]{:S(2)}, u32[]{:S(2)}) collective-permute-start(bf16[1,32,2048]{2,1,0:T(8,128)(2,1)S(1)} %get-tuple-element.53), channel_id=1, source_target_pairs={{0,24},{8,0},{16,8},{24,16},{1,25},{9,1},{17,9},{25,17},{2,26},{10... | collective-permute-start | bytes 393224 | tf_op jit(solution)/shard_map/ppermute | solution.py:15
  20.2 1.3 %collective-permute-start.5 = (f32[1,32,2048]{2,1,0:T(8,128)}, f32[1,32,2048]{2,1,0:T(8,128)}, u32[]{:S(2)}, u32[]{:S(2)}) collective-permute-start(f32[1,32,2048]{2,1,0:T(8,128)} %param.9), channel_id=1, source_target_pairs={{0,6},{1,7},{2,0},{3,1},{4,2},{5,3},{6,4},{7,5},{8,14},{9,15},{10,... | collective-permute-start | bytes 786440 | tf_op jit(solution)/shard_map/ppermute | solution.py:15
  21.6 2.3 %collective-permute-done.1 = bf16[1,32,2048]{2,1,0:T(8,128)(2,1)S(1)} collective-permute-done((bf16[1,32,2048]{2,1,0:T(8,128)(2,1)S(1)}, bf16[1,32,2048]{2,1,0:T(8,128)(2,1)S(1)}, u32[]{:S(2)}, u32[]{:S(2)}) %collective-permute-start.1) | collective-permute-done | bytes 131104 | tf_op jit(solution)/shard_map/ppermute | solution.py:15
  30.8 5.0 %shard_map.91 = (bf16[4,256,256]{2,1,0:T(8,128)(2,1)}, bf16[4,256,256]{2,1,0:T(8,128)(2,1)}, bf16[4,3,128,128]{3,2,1,0:T(8,128)(2,1)}, bf16[4,3,128,128]{3,2,1,0:T(8,128)(2,1)}) custom-call(f32[68]{0:T(128)} %reshape.563.row_ref, f32[68]{0:T(128)} %reshape.564.col_ref), custom_call_target="tpu_custom_call" | custom-call | tf_op jit(solution)/shard_map/pallas_call | solution.py:194
  37.9 1.8 %slice_bitcast_fusion.8 = (bf16[3,128,128]{2,1,0:T(8,128)(2,1)}, bf16[3,128,128]{2,1,0:T(8,128)(2,1)}, bf16[3,128,128]{2,1,0:T(8,128)(2,1)}, bf16[3,128,128]{2,1,0:T(8,128)(2,1)}) fusion(bf16[4,3,128,128]{3,2,1,0:T(8,128)(2,1)} %get-tuple-element.10), kind=kLoop, calls=%fused_computation.41 | loop fusion | bytes 786432 | tf_op jit(solution)/shard_map/squeeze | solution.py:482
  39.7 1.8 %slice_bitcast_fusion.9 = (bf16[3,128,128]{2,1,0:T(8,128)(2,1)}, bf16[3,128,128]{2,1,0:T(8,128)(2,1)}, bf16[3,128,128]{2,1,0:T(8,128)(2,1)}, bf16[3,128,128]{2,1,0:T(8,128)(2,1)}) fusion(bf16[4,3,128,128]{3,2,1,0:T(8,128)(2,1)} %get-tuple-element.9), kind=kLoop, calls=%fused_computation.42 | loop fusion | bytes 786432 | tf_op jit(solution)/shard_map/squeeze | solution.py:482
  41.5 1.9 %slice_bitcast_fusion = (bf16[256,256]{1,0:T(8,128)(2,1)}, bf16[256,256]{1,0:T(8,128)(2,1)}, bf16[256,256]{1,0:T(8,128)(2,1)S(1)}, bf16[256,256]{1,0:T(8,128)(2,1)S(1)}) fusion(bf16[4,256,256]{2,1,0:T(8,128)(2,1)} %get-tuple-element.12), kind=kLoop, calls=%fused_computation.30 | loop fusion | bytes 1048576 | tf_op jit(solution)/shard_map/squeeze | solution.py:482
  44.2 1.1 fusion.13
  51.8 1.0 copy-done.4
  52.9 1.1 copy-done.5
  54.7 0.9 copy-done.23
  55.6 0.9 copy-done.24
  59.1 1.2 copy-done.28
  60.3 0.9 copy-done.29
  61.3 12.3 %shard_map.92.rest_0_ = f32[256,2048]{1,0:T(8,128)} custom-call(s32[8]{0:T(128)S(1)} %broadcast_multiply_fusion.offs_ref, f32[1]{0:T(128)} %get-tuple-element.75.bg_ref, bf16[1,1,256,2048]{3,2,1,0:T(8,128)(2,1)S(1)} %copy-done.28, bf16[128,128]{1,0:T(8,128)(2,1)S(1)} %bitcast.94, bf16[128,128]{1,0:T(8,128)(2,1)S(1)} %bitcast.95, ...), custom_call_target="tpu_custom_call" | custom-call | flops 2147483648 | bytes 5242880 | tf_op jit(solution)/shard_map/pallas_call | solution.py:237
  73.5 11.3 %all-gather.3.cloned.1.call-done.raw_ref = bf16[3,1,256,2048]{3,2,1,0:T(8,128)(2,1)} async-done(((bf16[3,1,32,2048]{3,2,1,0:T(8,128)(2,1)}), bf16[3,1,256,2048]{3,2,1,0:T(8,128)(2,1)}) %all-gather.3.cloned.1.call-update) | async-done | bytes 3145744 | tf_op jit(solution)/shard_map/all_gather | solution.py:450
  85.0 1.6 %copy-done = f32[256,2048]{1,0:T(8,128)S(1)} copy-done((f32[256,2048]{1,0:T(8,128)S(1)}, f32[256,2048]{1,0:T(8,128)}, u32[]{:S(2)}) %copy-start) | copy-done | bytes 2097176
  87.4 0.9 copy-done.3
  91.7 10.3 %shard_map.93.rest_0_ = f32[256,2048]{1,0:T(8,128)S(1)} custom-call(s32[1]{0:T(128)} %constant.162.clone.1.offs_ref, f32[1]{0:T(128)} %get-tuple-element.78.bg_ref, bf16[3,1,256,2048]{3,2,1,0:T(8,128)(2,1)} %all-gather.3.cloned.1.call-done.raw_ref, bf16[128,128]{1,0:T(8,128)(2,1)S(1)} %bitcast.90, bf16[128,128]{1,0:T(8,128)(2,1)S(1)} %bitcast.93, ...), custom_call_target="tpu_custom_call" | custom-call | flops 2147483648 | bytes 5242880 | tf_op jit(solution)/shard_map/pallas_call | solution.py:237
  102.3 10.6 %shard_map.94.rest_0_ = f32[256,2048]{1,0:T(8,128)S(1)} custom-call(s32[1]{0:T(128)} %constant.162.clone.1.offs_ref, f32[1]{0:T(128)} %get-tuple-element.76.bg_ref, bf16[3,1,256,2048]{3,2,1,0:T(8,128)(2,1)} %all-gather.3.cloned.1.call-done.raw_ref, bf16[128,128]{1,0:T(8,128)(2,1)S(1)} %bitcast.89, bf16[128,128]{1,0:T(8,128)(2,1)S(1)} %bitcast.92, ...), custom_call_target="tpu_custom_call" | custom-call | flops 2147483648 | bytes 5242880 | tf_op jit(solution)/shard_map/pallas_call | solution.py:237
  113.0 10.4 %shard_map.95 = f32[256,2048]{1,0:T(8,128)S(1)} custom-call(s32[1]{0:T(128)} %constant.162.clone.1.offs_ref, f32[1]{0:T(128)} %get-tuple-element.77.bg_ref, bf16[3,1,256,2048]{3,2,1,0:T(8,128)(2,1)} %all-gather.3.cloned.1.call-done.raw_ref, bf16[128,128]{1,0:T(8,128)(2,1)S(1)} %bitcast.88, bf16[128,128]{1,0:T(8,128)(2,1)S(1)} %bitcast.91, ...), custom_call_target="tpu_custom_call" | custom-call | flops 2147483648 | bytes 5242880 | tf_op jit(solution)/shard_map/pallas_call | solution.py:237
  (146 shorter events, 26.6 us)
Async XLA Ops:
  6.5 18.6 %copy-start.36 = (s32[4]{0:T(128)S(1)}, s32[4]{0:T(128)}, u32[]{:S(2)}) copy-start(s32[4]{0:T(128)} %param.16) | copy-start | bytes 52
  6.5 20.4 %copy-start.34 = (f32[4,4,17]{2,1,0:T(4,128)S(1)}, f32[4,4,17]{2,1,0:T(4,128)}, u32[]{:S(2)}) copy-start(f32[4,4,17]{2,1,0:T(4,128)} %param.14) | copy-start | bytes 3268
  6.5 21.1 %copy-start.35 = (f32[4,4,17]{2,1,0:T(4,128)S(1)}, f32[4,4,17]{2,1,0:T(4,128)}, u32[]{:S(2)}) copy-start(f32[4,4,17]{2,1,0:T(4,128)} %param.15) | copy-start | bytes 3268
  6.5 44.4 %all-gather.5.cloned.1.call-start = ((), (), s32[]{:S(2)}) async-start(), calls=%async_computation.1 | async-start | bytes 1179648 | tf_op jit(solution)/shard_map/all_gather | solution.py:449
  8.4 76.4 %all-gather.3.cloned.1.call-start = ((), (), s32[]{:S(2)}) async-start(), calls=%async_computation | async-start | bytes 3538944 | tf_op jit(solution)/shard_map/all_gather | solution.py:450
  8.4 37.5 %collective-permute-start.3 = (f32[1,32,2048]{2,1,0:T(8,128)}, f32[1,32,2048]{2,1,0:T(8,128)}, u32[]{:S(2)}, u32[]{:S(2)}) collective-permute-start(f32[1,32,2048]{2,1,0:T(8,128)} %param.9), channel_id=1, source_target_pairs={{0,2},{1,3},{2,4},{3,5},{4,6},{5,7},{6,0},{7,1},{8,10},{9,11},{10,... | collective-permute-start | bytes 786440 | tf_op jit(solution)/shard_map/ppermute | solution.py:15
  11.5 35.0 %collective-permute-start.4 = (f32[1,32,2048]{2,1,0:T(8,128)}, f32[1,32,2048]{2,1,0:T(8,128)}, u32[]{:S(2)}, u32[]{:S(2)}) collective-permute-start(f32[1,32,2048]{2,1,0:T(8,128)} %param.9), channel_id=1, source_target_pairs={{0,4},{1,5},{2,6},{3,7},{4,0},{5,1},{6,2},{7,3},{8,12},{9,13},{10,... | collective-permute-start | bytes 786440 | tf_op jit(solution)/shard_map/ppermute | solution.py:15
  14.1 6.1 %collective-permute-start = (bf16[1,32,2048]{2,1,0:T(8,128)(2,1)S(1)}, bf16[1,32,2048]{2,1,0:T(8,128)(2,1)S(1)}, u32[]{:S(2)}, u32[]{:S(2)}) collective-permute-start(bf16[1,32,2048]{2,1,0:T(8,128)(2,1)S(1)} %get-tuple-element.53), channel_id=1, source_target_pairs={{0,24},{8,0},{16,8},{24,16},{1,25},{9,1},{17,9},{25,17},{2,26},{10... | collective-permute-start | bytes 393224 | tf_op jit(solution)/shard_map/ppermute | solution.py:15
  16.6 7.3 %collective-permute-start.1 = (bf16[1,32,2048]{2,1,0:T(8,128)(2,1)S(1)}, bf16[1,32,2048]{2,1,0:T(8,128)(2,1)S(1)}, u32[]{:S(2)}, u32[]{:S(2)}) collective-permute-start(bf16[1,32,2048]{2,1,0:T(8,128)(2,1)S(1)} %get-tuple-element.52), channel_id=1, source_target_pairs={{0,16},{8,24},{16,0},{24,8},{1,17},{9,25},{17,1},{25,9},{2,18},{10... | collective-permute-start | bytes 393224 | tf_op jit(solution)/shard_map/ppermute | solution.py:15
  17.1 6.8 %collective-permute-start.2 = (bf16[1,32,2048]{2,1,0:T(8,128)(2,1)S(1)}, bf16[1,32,2048]{2,1,0:T(8,128)(2,1)S(1)}, u32[]{:S(2)}, u32[]{:S(2)}) collective-permute-start(bf16[1,32,2048]{2,1,0:T(8,128)(2,1)S(1)} %get-tuple-element.54), channel_id=1, source_target_pairs={{0,8},{8,16},{16,24},{24,0},{1,9},{9,17},{17,25},{25,1},{2,10},{10... | collective-permute-start | bytes 393224 | tf_op jit(solution)/shard_map/ppermute | solution.py:15
  20.2 26.4 %collective-permute-start.5 = (f32[1,32,2048]{2,1,0:T(8,128)}, f32[1,32,2048]{2,1,0:T(8,128)}, u32[]{:S(2)}, u32[]{:S(2)}) collective-permute-start(f32[1,32,2048]{2,1,0:T(8,128)} %param.9), channel_id=1, source_target_pairs={{0,6},{1,7},{2,0},{3,1},{4,2},{5,3},{6,4},{7,5},{8,14},{9,15},{10,... | collective-permute-start | bytes 786440 | tf_op jit(solution)/shard_map/ppermute | solution.py:15
  23.9 27.0 %collective-permute-start.6 = (f32[1,32,2048]{2,1,0:T(8,128)}, f32[1,32,2048]{2,1,0:T(8,128)}, u32[]{:S(2)}, u32[]{:S(2)}) collective-permute-start(f32[1,32,2048]{2,1,0:T(8,128)} %param.9), channel_id=1, source_target_pairs={{0,1},{1,0},{2,3},{3,2},{4,5},{5,4},{6,7},{7,6},{8,9},{9,8},{10,11... | collective-permute-start | bytes 786440 | tf_op jit(solution)/shard_map/ppermute | solution.py:456
  45.9 5.0 %collective-permute-start.7 = (f32[1,32,2048]{2,1,0:T(8,128)}, f32[1,32,2048]{2,1,0:T(8,128)}, u32[]{:S(2)}, u32[]{:S(2)}) collective-permute-start(f32[1,32,2048]{2,1,0:T(8,128)} %collective-permute-done.3), channel_id=1, source_target_pairs={{0,1},{1,0},{2,3},{3,2},{4,5},{5,4},{6,7},{7,6},{8,9},{9,8},{10,11... | collective-permute-start | bytes 786440 | tf_op jit(solution)/shard_map/ppermute | solution.py:456
  46.5 4.5 %collective-permute-start.8 = (f32[1,32,2048]{2,1,0:T(8,128)}, f32[1,32,2048]{2,1,0:T(8,128)}, u32[]{:S(2)}, u32[]{:S(2)}) collective-permute-start(f32[1,32,2048]{2,1,0:T(8,128)} %collective-permute-done.4), channel_id=1, source_target_pairs={{0,1},{1,0},{2,3},{3,2},{4,5},{5,4},{6,7},{7,6},{8,9},{9,8},{10,11... | collective-permute-start | bytes 786440 | tf_op jit(solution)/shard_map/ppermute | solution.py:456
  46.6 4.4 %collective-permute-start.9 = (f32[1,32,2048]{2,1,0:T(8,128)}, f32[1,32,2048]{2,1,0:T(8,128)}, u32[]{:S(2)}, u32[]{:S(2)}) collective-permute-start(f32[1,32,2048]{2,1,0:T(8,128)} %collective-permute-done.5), channel_id=1, source_target_pairs={{0,1},{1,0},{2,3},{3,2},{4,5},{5,4},{6,7},{7,6},{8,9},{9,8},{10,11... | collective-permute-start | bytes 786440 | tf_op jit(solution)/shard_map/ppermute | solution.py:456
  61.3 23.6 %copy-start.32 = (f32[512]{0:T(512)S(1)}, f32[512]{0:T(512)}, u32[]{:S(2)}) copy-start(f32[512]{0:T(512)} %broadcast_maximum_fusion.1) | copy-start | bytes 6148
  91.7 10.5 %copy-start.8 = (bf16[3,128,128]{2,1,0:T(8,128)(2,1)S(1)}, bf16[3,128,128]{2,1,0:T(8,128)(2,1)}, u32[]{:S(2)}) copy-start(bf16[3,128,128]{2,1,0:T(8,128)(2,1)} %get-tuple-element.57.bb_ref) | copy-start | bytes 294916
  91.7 10.5 %copy-start.9 = (bf16[3,128,128]{2,1,0:T(8,128)(2,1)S(1)}, bf16[3,128,128]{2,1,0:T(8,128)(2,1)}, u32[]{:S(2)}) copy-start(bf16[3,128,128]{2,1,0:T(8,128)(2,1)} %get-tuple-element.61.bf_ref) | copy-start | bytes 294916
  91.7 10.5 %copy-start.15 = (bf16[1,128,128]{2,1,0:T(8,128)(2,1)S(1)}, bf16[1,128,128]{2,1,0:T(8,128)(2,1)}, u32[]{:S(2)}) copy-start(bf16[1,128,128]{2,1,0:T(8,128)(2,1)} %copy-done.14) | copy-start | bytes 98308
  91.7 10.5 %copy-start.19 = (bf16[1,128,128]{1,2,0:T(8,128)(2,1)S(1)}, bf16[1,128,128]{1,2,0:T(8,128)(2,1)}, u32[]{:S(2)}) copy-start(bf16[1,128,128]{1,2,0:T(8,128)(2,1)} %copy.20) | copy-start | bytes 98308
  102.2 10.8 %copy-start.6 = (bf16[3,128,128]{2,1,0:T(8,128)(2,1)S(1)}, bf16[3,128,128]{2,1,0:T(8,128)(2,1)}, u32[]{:S(2)}) copy-start(bf16[3,128,128]{2,1,0:T(8,128)(2,1)} %get-tuple-element.58.bb_ref) | copy-start | bytes 294916
  102.2 10.8 %copy-start.7 = (bf16[3,128,128]{2,1,0:T(8,128)(2,1)S(1)}, bf16[3,128,128]{2,1,0:T(8,128)(2,1)}, u32[]{:S(2)}) copy-start(bf16[3,128,128]{2,1,0:T(8,128)(2,1)} %get-tuple-element.62.bf_ref) | copy-start | bytes 294916
  102.2 10.8 %copy-start.13 = (bf16[1,128,128]{2,1,0:T(8,128)(2,1)S(1)}, bf16[1,128,128]{2,1,0:T(8,128)(2,1)}, u32[]{:S(2)}) copy-start(bf16[1,128,128]{2,1,0:T(8,128)(2,1)} %copy-done.12) | copy-start | bytes 98308
  102.2 10.8 %copy-start.18 = (bf16[1,128,128]{1,2,0:T(8,128)(2,1)S(1)}, bf16[1,128,128]{1,2,0:T(8,128)(2,1)}, u32[]{:S(2)}) copy-start(bf16[1,128,128]{1,2,0:T(8,128)(2,1)} %copy.18) | copy-start | bytes 98308
  (25 other events, 55.3 us)
Sparse Core Ops, SparseCore 0:
  9.0 35.4 all-gather.4
  46.0 38.7 all-gather.2

commit v7 on v6

--- a/solution.py
+++ b/solution.py
@@ -1,3 +1,5 @@
+import functools
+
 import jax
 import jax.numpy as jnp
 from jax import lax
@@ -100,17 +102,11 @@
     return estimate * from_blocks(correction, rows, plane_width).astype(jnp.float32)
 
 
-def plane_kernel(offs_ref, bg_ref, raw_ref, m_ref, mt_ref, s_ref, cnt_ref, g_ref, bf_ref, bb_ref,
-                 a_ref, at_ref, *rest):
-    *piece_refs, out_ref, est_whole, work, joined, across, ratio = rest
+def plane_kernel(est_count, raw_index, offs_ref, bg_ref, m_ref, mt_ref, raw_hbm, s_hbm, cnt_hbm,
+                 g_hbm, bf_hbm, bb_hbm, a_hbm, at_hbm, *rest):
+    *est_hbm, out_ref, est_ref, raw_ref, s_ref, cnt_ref, g_ref, bf_ref, bb_ref, a_ref, at_ref = rest[:-5]
+    work, joined, across, ratio, sems = rest[-5:]
     rows, plane_width = out_ref.shape
-    if len(piece_refs) == 1:
-        est_ref = piece_refs[0]
-    else:
-        est_ref = est_whole
-        for k, piece in enumerate(piece_refs):
-            piece_rows = piece.shape[0]
-            est_ref[pl.ds(pl.multiple_of(offs_ref[k], BR), piece_rows), :] = piece[...]
     nt = rows // BR
     nc = plane_width // BW
     f32 = jnp.float32
@@ -118,6 +114,25 @@
 
     def cols(c):
         return slice(c * BW, (c + 1) * BW)
+
+    est_copies = []
+    for k, piece in enumerate(est_hbm):
+        if est_count == 1:
+            target = est_ref
+        else:
+            target = est_ref.at[pl.ds(pl.multiple_of(offs_ref[k], BR), piece.shape[0])]
+        est_copies.append(pltpu.make_async_copy(piece, target, sems.at[k]))
+    sources = [raw_hbm.at[raw_index], s_hbm, cnt_hbm, g_hbm, bf_hbm, bb_hbm, a_hbm, at_hbm]
+    targets = [raw_ref, s_ref, cnt_ref, g_ref, bf_ref, bb_ref, a_ref, at_ref]
+    copies = [
+        pltpu.make_async_copy(src, dst, sems.at[est_count + i])
+        for i, (src, dst) in enumerate(zip(sources, targets))
+    ]
+    raw_copy, s_copy, cnt_copy, g_copy, bf_copy, bb_copy, a_copy, at_copy = copies
+    for copy in est_copies + copies:
+        copy.start()
+    for copy in est_copies:
+        copy.wait()
 
     for c in range(nc):
         blk = est_ref[:, cols(c)].astype(bf16)
@@ -134,6 +149,8 @@
             for c in range(nc):
                 dst[c, pl.ds(r, nt, stride=BR), :] = result[c * nt:(c + 1) * nt, :]
 
+    s_copy.wait()
+    cnt_copy.wait()
     regroup(work, s_ref, joined,
             lambda v: (v / cnt_ref[...]).astype(bf16).astype(f32))
 
@@ -146,17 +163,23 @@
                 total = part if total is None else total + part
         return total
 
+    bf_copy.wait()
     for c in range(nc):
         across[:, cols(c)] = column_blur(lambda i: joined[i], bf_ref, c).astype(bf16)
     level = bg_ref[0]
+    a_copy.wait()
+    at_copy.wait()
+    raw_copy.wait()
     for c in range(nc):
         blurred = jnp.dot(a_ref[...], across[:, cols(c)], preferred_element_type=f32) + level
         quotient = (raw_ref[:, cols(c)].astype(f32) / blurred).astype(bf16)
         ratio[:, cols(c)] = jnp.dot(at_ref[...], quotient, preferred_element_type=f32).astype(bf16)
+    bb_copy.wait()
     for c in range(nc):
         spread = column_blur(lambda i: ratio[:, cols(i)], bb_ref, c).astype(bf16)
         back = jnp.dot(spread, mt_ref[...], preferred_element_type=f32)
         work[c] = back.astype(bf16).astype(f32)
+    g_copy.wait()
     regroup(work, g_ref, joined, lambda v: v)
     for c in range(nc):
         out_ref[:, cols(c)] = est_ref[:, cols(c)] * joined[c]
@@ -217,9 +240,10 @@
     count = jnp.sum(sum_mat.astype(jnp.float32), axis=1)
     count = jnp.broadcast_to(jnp.maximum(count, 1.0)[:, None], (blocks, BW))
     smem = pl.BlockSpec(memory_space=pltpu.SMEM)
+    vmem = pl.BlockSpec(memory_space=pltpu.VMEM)
+    hbm = pl.BlockSpec(memory_space=pl.ANY)
     operands = [
-        matrix,
-        matrix.T,
+        raw_all,
         sum_mat.astype(jnp.bfloat16),
         count,
         pick_mat.astype(jnp.bfloat16),
@@ -229,23 +253,26 @@
         bands[1],
         *est_pieces,
     ]
-
-    def whole(x):
-        return pl.BlockSpec(x.shape, lambda i, dims=len(x.shape): (0,) * dims)
-
-    raw_spec = pl.BlockSpec((None, None, rows, plane_width), lambda i: raw_index + (0, 0))
     return pl.pallas_call(
-        plane_kernel,
-        grid=(1,),
+        functools.partial(plane_kernel, len(est_pieces), raw_index),
         out_shape=jax.ShapeDtypeStruct((rows, plane_width), jnp.float32),
-        in_specs=[smem, smem, raw_spec] + [whole(x) for x in operands],
-        out_specs=whole(jax.ShapeDtypeStruct((rows, plane_width), jnp.float32)),
+        in_specs=[smem, smem, vmem, vmem] + [hbm] * len(operands),
+        out_specs=vmem,
         scratch_shapes=[
             pltpu.VMEM((rows, plane_width), jnp.float32),
+            pltpu.VMEM((rows, plane_width), jnp.bfloat16),
+            pltpu.VMEM((blocks, blocks), jnp.bfloat16),
+            pltpu.VMEM((blocks, BW), jnp.float32),
+            pltpu.VMEM((blocks, blocks), jnp.bfloat16),
+            pltpu.VMEM((3, BW, BW), jnp.bfloat16),
+            pltpu.VMEM((3, BW, BW), jnp.bfloat16),
+            pltpu.VMEM((rows, rows), jnp.bfloat16),
+            pltpu.VMEM((rows, rows), jnp.bfloat16),
             pltpu.VMEM((nc, rows, BW), jnp.float32),
             pltpu.VMEM((nc, rows, BW), jnp.float32),
             pltpu.VMEM((rows, plane_width), jnp.bfloat16),
             pltpu.VMEM((rows, plane_width), jnp.bfloat16),
+            pltpu.SemaphoreType.DMA((len(est_pieces) + 8,)),
         ],
         compiler_params=pltpu.CompilerParams(vmem_limit_bytes=48 * 1024 * 1024),
         cost_estimate=pl.CostEstimate(
@@ -253,7 +280,7 @@
             bytes_accessed=rows * plane_width * 10,
             transcendentals=0,
         ),
-    )(offsets, jnp.reshape(level, (1,)).astype(jnp.float32), raw_all, *operands)
+    )(offsets, jnp.reshape(level, (1,)).astype(jnp.float32), matrix, matrix.T, *operands)
 
 
 def with_halo(cells, sides, width):

time: 132 us -> 134 us (1.015)
  Pallas kernels: 48.6 us -> 52.1 us
  waiting for transfers between devices: 14.3 us -> 12.8 us
    pallas_call x4, Pallas kernels: 43.6 us -> 47.1 us  [kernel_update(): pl.pallas_call(functools.partial(plane_kernel, len(est_pieces), raw_index...]
    all_gather x1, waiting for transfers between devices: 11.3 us -> 9.83 us  [local(): lax.all_gather(jnp.stack(pieces[1:]), 'tile', axis=2, tiled=True)]
  transfers between devices with their start and end apart: 12 -> 12, of which waited for: 3 -> 3; matrix products, arithmetic and copies ran while one was open for 16% -> 16% of each run, Pallas kernels for 13% -> 14%
where the time goes in v7:
time: 134 us; the launch traced here: 133 us
  Pallas kernels  52.1 us (39%)
  local copies, waits for them, and re-layouts  34.9 us (26%)
  between operations  15.7 us (12%)
  waiting for transfers between devices  12.8 us (10%)
  starting transfers between devices  11.7 us (9%)
  other arithmetic  5.79 us (4%)
    pallas_call x4, Pallas kernels, kernel_update(): pl.pallas_call(functools.partial(plane_kernel, len(est_pieces), raw_index...  47.1 us
    unnamed x74, local copies, waits for them, and re-layouts  16.2 us
    ppermute x6, starting transfers between devices, passed_along(): return lax.ppermute(x, axis, [(i, (i + by) % count) for i in range(count)])  10.6 us
    all_gather x1, waiting for transfers between devices, local(): lax.all_gather(jnp.stack(pieces[1:]), 'tile', axis=2, tiled=True)  9.83 us
    squeeze x4, local copies, waits for them, and re-layouts, local(): b[update_index * planes + p]  6.25 us
    pallas_call x1, Pallas kernels, all_bands(): pl.pallas_call(band_kernel, out_shape=(jax.ShapeDtypeStruct((count, rows,...  5.01 us
    ppermute x6, waiting for transfers between devices, passed_along(): return lax.ppermute(x, axis, [(i, (i + by) % count) for i in range(count)])  2.92 us
    dynamic_slice x5, local copies, waits for them, and re-layouts, local(): matrix = interp[view_index]  2.89 us
  transfers between devices with their start and end apart: 12, of which 3 were waited for; matrix products, arithmetic and copies ran while one was open for 16% of the time, Pallas kernels for 14%

profile of v7, /device:TPU:0, one launch (start us, length us, event | category | flops | bytes accessed | tf_op | source)
XLA Modules:
  0.0 133.1 jit_solution(3504640212041785556)
XLA Ops:
  6.5 1.8 %constant_dynamic-slice_fusion.4 = (bf16[1,1,32,2048]{3,2,1,0:T(8,128)(2,1)}, bf16[1,32,2048]{2,1,0:T(8,128)(2,1)S(1)}, bf16[1,32,2048]{2,1,0:T(8,128)(2,1)S(1)}, bf16[1,32,2048]{2,1,0:T(8,128)(2,1)S(1)}) fusion(bf16[1,4,32,2048]{3,2,1,0:T(8,128)(2,1)} %param.10, s32[]{:T(128)S(6)} %select_n.240, s32[]{:T(128)S(6)} %select_n.218, s32[]{:T(128)S(6)} %select_n.216, ...), kind=kLoop, calls=%fused_computation.57 | loop fusion | bytes 1048592 | tf_op jit(solution)/shard_map/dynamic_slice | solution.py:471
  8.4 3.1 %collective-permute-start.3 = (f32[1,32,2048]{2,1,0:T(8,128)}, f32[1,32,2048]{2,1,0:T(8,128)}, u32[]{:S(2)}, u32[]{:S(2)}) collective-permute-start(f32[1,32,2048]{2,1,0:T(8,128)} %param.9), channel_id=1, source_target_pairs={{0,2},{1,3},{2,4},{3,5},{4,6},{5,7},{6,0},{7,1},{8,10},{9,11},{10,... | collective-permute-start | bytes 786440 | tf_op jit(solution)/shard_map/ppermute | solution.py:17
  11.5 2.6 %collective-permute-start.4 = (f32[1,32,2048]{2,1,0:T(8,128)}, f32[1,32,2048]{2,1,0:T(8,128)}, u32[]{:S(2)}, u32[]{:S(2)}) collective-permute-start(f32[1,32,2048]{2,1,0:T(8,128)} %param.9), channel_id=1, source_target_pairs={{0,4},{1,5},{2,6},{3,7},{4,0},{5,1},{6,2},{7,3},{8,12},{9,13},{10,... | collective-permute-start | bytes 786440 | tf_op jit(solution)/shard_map/ppermute | solution.py:17
  14.1 2.4 %collective-permute-start = (bf16[1,32,2048]{2,1,0:T(8,128)(2,1)S(1)}, bf16[1,32,2048]{2,1,0:T(8,128)(2,1)S(1)}, u32[]{:S(2)}, u32[]{:S(2)}) collective-permute-start(bf16[1,32,2048]{2,1,0:T(8,128)(2,1)S(1)} %get-tuple-element.53), channel_id=1, source_target_pairs={{0,24},{8,0},{16,8},{24,16},{1,25},{9,1},{17,9},{25,17},{2,26},{10... | collective-permute-start | bytes 393224 | tf_op jit(solution)/shard_map/ppermute | solution.py:17
  20.2 1.3 %collective-permute-start.5 = (f32[1,32,2048]{2,1,0:T(8,128)}, f32[1,32,2048]{2,1,0:T(8,128)}, u32[]{:S(2)}, u32[]{:S(2)}) collective-permute-start(f32[1,32,2048]{2,1,0:T(8,128)} %param.9), channel_id=1, source_target_pairs={{0,6},{1,7},{2,0},{3,1},{4,2},{5,3},{6,4},{7,5},{8,14},{9,15},{10,... | collective-permute-start | bytes 786440 | tf_op jit(solution)/shard_map/ppermute | solution.py:17
  21.6 2.3 %collective-permute-done.1 = bf16[1,32,2048]{2,1,0:T(8,128)(2,1)S(1)} collective-permute-done((bf16[1,32,2048]{2,1,0:T(8,128)(2,1)S(1)}, bf16[1,32,2048]{2,1,0:T(8,128)(2,1)S(1)}, u32[]{:S(2)}, u32[]{:S(2)}) %collective-permute-start.1) | collective-permute-done | bytes 131104 | tf_op jit(solution)/shard_map/ppermute | solution.py:17
  30.8 5.0 %shard_map.91 = (bf16[4,256,256]{2,1,0:T(8,128)(2,1)}, bf16[4,256,256]{2,1,0:T(8,128)(2,1)}, bf16[4,3,128,128]{3,2,1,0:T(8,128)(2,1)}, bf16[4,3,128,128]{3,2,1,0:T(8,128)(2,1)}) custom-call(f32[68]{0:T(128)} %reshape.563.row_ref, f32[68]{0:T(128)} %reshape.564.col_ref), custom_call_target="tpu_custom_call" | custom-call | tf_op jit(solution)/shard_map/pallas_call | solution.py:217
  37.9 1.8 %slice_bitcast_fusion.8 = (bf16[3,128,128]{2,1,0:T(8,128)(2,1)}, bf16[3,128,128]{2,1,0:T(8,128)(2,1)}, bf16[3,128,128]{2,1,0:T(8,128)(2,1)}, bf16[3,128,128]{2,1,0:T(8,128)(2,1)}) fusion(bf16[4,3,128,128]{3,2,1,0:T(8,128)(2,1)} %get-tuple-element.10), kind=kLoop, calls=%fused_computation.41 | loop fusion | bytes 786432 | tf_op jit(solution)/shard_map/squeeze | solution.py:509
  39.7 1.8 %slice_bitcast_fusion.9 = (bf16[3,128,128]{2,1,0:T(8,128)(2,1)}, bf16[3,128,128]{2,1,0:T(8,128)(2,1)}, bf16[3,128,128]{2,1,0:T(8,128)(2,1)}, bf16[3,128,128]{2,1,0:T(8,128)(2,1)}) fusion(bf16[4,3,128,128]{3,2,1,0:T(8,128)(2,1)} %get-tuple-element.9), kind=kLoop, calls=%fused_computation.42 | loop fusion | bytes 786432 | tf_op jit(solution)/shard_map/squeeze | solution.py:509
  41.5 1.9 %slice_bitcast_fusion = (bf16[256,256]{1,0:T(8,128)(2,1)}, bf16[256,256]{1,0:T(8,128)(2,1)}, bf16[256,256]{1,0:T(8,128)(2,1)S(1)}, bf16[256,256]{1,0:T(8,128)(2,1)S(1)}) fusion(bf16[4,256,256]{2,1,0:T(8,128)(2,1)} %get-tuple-element.12), kind=kLoop, calls=%fused_computation.30 | loop fusion | bytes 1048576 | tf_op jit(solution)/shard_map/squeeze | solution.py:509
  44.2 1.1 fusion.13
  51.8 1.0 copy-done.4
  52.9 1.1 copy-done.5
  54.7 0.9 copy-done.23
  55.6 0.9 copy-done.24
  59.1 1.2 copy-done.28
  60.3 0.9 copy-done.29
  61.3 13.7 %shard_map.92.rest_0_ = f32[256,2048]{1,0:T(8,128)} custom-call(s32[8]{0:T(128)S(1)} %broadcast_multiply_fusion.offs_ref, f32[1]{0:T(128)} %get-tuple-element.75.bg_ref, bf16[128,128]{1,0:T(8,128)(2,1)S(1)} %bitcast.94, bf16[128,128]{1,0:T(8,128)(2,1)S(1)} %bitcast.95, bf16[1,1,256,2048]{3,2,1,0:T(8,128)(2,1)S(1)} %copy-done.28, ...), custom_call_target="tpu_custom_call" | custom-call | flops 2147483648 | bytes 5242880 | tf_op jit(solution)/shard_map/pallas_call | solution.py:256
  75.0 9.8 %all-gather.3.cloned.1.call-done.raw_hbm = bf16[3,1,256,2048]{3,2,1,0:T(8,128)(2,1)} async-done(((bf16[3,1,32,2048]{3,2,1,0:T(8,128)(2,1)}), bf16[3,1,256,2048]{3,2,1,0:T(8,128)(2,1)}) %all-gather.3.cloned.1.call-update) | async-done | bytes 3145744 | tf_op jit(solution)/shard_map/all_gather | solution.py:477
  85.0 1.6 %copy-done = f32[256,2048]{1,0:T(8,128)S(1)} copy-done((f32[256,2048]{1,0:T(8,128)S(1)}, f32[256,2048]{1,0:T(8,128)}, u32[]{:S(2)}) %copy-start) | copy-done | bytes 2097176
  87.4 0.9 copy-done.3
  91.7 11.1 %shard_map.93.rest_0_ = f32[256,2048]{1,0:T(8,128)S(1)} custom-call(s32[1]{0:T(128)} %constant.162.clone.1.offs_ref, f32[1]{0:T(128)} %get-tuple-element.78.bg_ref, bf16[128,128]{1,0:T(8,128)(2,1)S(1)} %bitcast.90, bf16[128,128]{1,0:T(8,128)(2,1)S(1)} %bitcast.93, bf16[3,1,256,2048]{3,2,1,0:T(8,128)(2,1)} %all-gather.3.cloned.1.call-done.raw_hbm, ...), custom_call_target="tpu_custom_call" | custom-call | flops 2147483648 | bytes 5242880 | tf_op jit(solution)/shard_map/pallas_call | solution.py:256
  103.0 11.2 %shard_map.94.rest_0_ = f32[256,2048]{1,0:T(8,128)S(1)} custom-call(s32[1]{0:T(128)} %constant.162.clone.1.offs_ref, f32[1]{0:T(128)} %get-tuple-element.76.bg_ref, bf16[128,128]{1,0:T(8,128)(2,1)S(1)} %bitcast.89, bf16[128,128]{1,0:T(8,128)(2,1)S(1)} %bitcast.92, bf16[3,1,256,2048]{3,2,1,0:T(8,128)(2,1)} %all-gather.3.cloned.1.call-done.raw_hbm, ...), custom_call_target="tpu_custom_call" | custom-call | flops 2147483648 | bytes 5242880 | tf_op jit(solution)/shard_map/pallas_call | solution.py:256
  114.3 11.2 %shard_map.95 = f32[256,2048]{1,0:T(8,128)S(1)} custom-call(s32[1]{0:T(128)} %constant.162.clone.1.offs_ref, f32[1]{0:T(128)} %get-tuple-element.77.bg_ref, bf16[128,128]{1,0:T(8,128)(2,1)S(1)} %bitcast.88, bf16[128,128]{1,0:T(8,128)(2,1)S(1)} %bitcast.91, bf16[3,1,256,2048]{3,2,1,0:T(8,128)(2,1)} %all-gather.3.cloned.1.call-done.raw_hbm, ...), custom_call_target="tpu_custom_call" | custom-call | flops 2147483648 | bytes 5242880 | tf_op jit(solution)/shard_map/pallas_call | solution.py:256
  (146 shorter events, 26.6 us)
Async XLA Ops:
  6.5 18.6 %copy-start.36 = (s32[4]{0:T(128)S(1)}, s32[4]{0:T(128)}, u32[]{:S(2)}) copy-start(s32[4]{0:T(128)} %param.16) | copy-start | bytes 52
  6.5 20.4 %copy-start.34 = (f32[4,4,17]{2,1,0:T(4,128)S(1)}, f32[4,4,17]{2,1,0:T(4,128)}, u32[]{:S(2)}) copy-start(f32[4,4,17]{2,1,0:T(4,128)} %param.14) | copy-start | bytes 3268
  6.5 21.1 %copy-start.35 = (f32[4,4,17]{2,1,0:T(4,128)S(1)}, f32[4,4,17]{2,1,0:T(4,128)}, u32[]{:S(2)}) copy-start(f32[4,4,17]{2,1,0:T(4,128)} %param.15) | copy-start | bytes 3268
  6.5 44.4 %all-gather.5.cloned.1.call-start = ((), (), s32[]{:S(2)}) async-start(), calls=%async_computation.1 | async-start | bytes 1179648 | tf_op jit(solution)/shard_map/all_gather | solution.py:476
  8.4 76.4 %all-gather.3.cloned.1.call-start = ((), (), s32[]{:S(2)}) async-start(), calls=%async_computation | async-start | bytes 3538944 | tf_op jit(solution)/shard_map/all_gather | solution.py:477
  8.4 37.5 %collective-permute-start.3 = (f32[1,32,2048]{2,1,0:T(8,128)}, f32[1,32,2048]{2,1,0:T(8,128)}, u32[]{:S(2)}, u32[]{:S(2)}) collective-permute-start(f32[1,32,2048]{2,1,0:T(8,128)} %param.9), channel_id=1, source_target_pairs={{0,2},{1,3},{2,4},{3,5},{4,6},{5,7},{6,0},{7,1},{8,10},{9,11},{10,... | collective-permute-start | bytes 786440 | tf_op jit(solution)/shard_map/ppermute | solution.py:17
  11.5 35.0 %collective-permute-start.4 = (f32[1,32,2048]{2,1,0:T(8,128)}, f32[1,32,2048]{2,1,0:T(8,128)}, u32[]{:S(2)}, u32[]{:S(2)}) collective-permute-start(f32[1,32,2048]{2,1,0:T(8,128)} %param.9), channel_id=1, source_target_pairs={{0,4},{1,5},{2,6},{3,7},{4,0},{5,1},{6,2},{7,3},{8,12},{9,13},{10,... | collective-permute-start | bytes 786440 | tf_op jit(solution)/shard_map/ppermute | solution.py:17
  14.1 6.1 %collective-permute-start = (bf16[1,32,2048]{2,1,0:T(8,128)(2,1)S(1)}, bf16[1,32,2048]{2,1,0:T(8,128)(2,1)S(1)}, u32[]{:S(2)}, u32[]{:S(2)}) collective-permute-start(bf16[1,32,2048]{2,1,0:T(8,128)(2,1)S(1)} %get-tuple-element.53), channel_id=1, source_target_pairs={{0,24},{8,0},{16,8},{24,16},{1,25},{9,1},{17,9},{25,17},{2,26},{10... | collective-permute-start | bytes 393224 | tf_op jit(solution)/shard_map/ppermute | solution.py:17
  16.6 7.3 %collective-permute-start.1 = (bf16[1,32,2048]{2,1,0:T(8,128)(2,1)S(1)}, bf16[1,32,2048]{2,1,0:T(8,128)(2,1)S(1)}, u32[]{:S(2)}, u32[]{:S(2)}) collective-permute-start(bf16[1,32,2048]{2,1,0:T(8,128)(2,1)S(1)} %get-tuple-element.52), channel_id=1, source_target_pairs={{0,16},{8,24},{16,0},{24,8},{1,17},{9,25},{17,1},{25,9},{2,18},{10... | collective-permute-start | bytes 393224 | tf_op jit(solution)/shard_map/ppermute | solution.py:17
  17.1 6.8 %collective-permute-start.2 = (bf16[1,32,2048]{2,1,0:T(8,128)(2,1)S(1)}, bf16[1,32,2048]{2,1,0:T(8,128)(2,1)S(1)}, u32[]{:S(2)}, u32[]{:S(2)}) collective-permute-start(bf16[1,32,2048]{2,1,0:T(8,128)(2,1)S(1)} %get-tuple-element.54), channel_id=1, source_target_pairs={{0,8},{8,16},{16,24},{24,0},{1,9},{9,17},{17,25},{25,1},{2,10},{10... | collective-permute-start | bytes 393224 | tf_op jit(solution)/shard_map/ppermute | solution.py:17
  20.2 26.4 %collective-permute-start.5 = (f32[1,32,2048]{2,1,0:T(8,128)}, f32[1,32,2048]{2,1,0:T(8,128)}, u32[]{:S(2)}, u32[]{:S(2)}) collective-permute-start(f32[1,32,2048]{2,1,0:T(8,128)} %param.9), channel_id=1, source_target_pairs={{0,6},{1,7},{2,0},{3,1},{4,2},{5,3},{6,4},{7,5},{8,14},{9,15},{10,... | collective-permute-start | bytes 786440 | tf_op jit(solution)/shard_map/ppermute | solution.py:17
  23.9 27.0 %collective-permute-start.6 = (f32[1,32,2048]{2,1,0:T(8,128)}, f32[1,32,2048]{2,1,0:T(8,128)}, u32[]{:S(2)}, u32[]{:S(2)}) collective-permute-start(f32[1,32,2048]{2,1,0:T(8,128)} %param.9), channel_id=1, source_target_pairs={{0,1},{1,0},{2,3},{3,2},{4,5},{5,4},{6,7},{7,6},{8,9},{9,8},{10,11... | collective-permute-start | bytes 786440 | tf_op jit(solution)/shard_map/ppermute | solution.py:483
  45.9 5.0 %collective-permute-start.7 = (f32[1,32,2048]{2,1,0:T(8,128)}, f32[1,32,2048]{2,1,0:T(8,128)}, u32[]{:S(2)}, u32[]{:S(2)}) collective-permute-start(f32[1,32,2048]{2,1,0:T(8,128)} %collective-permute-done.3), channel_id=1, source_target_pairs={{0,1},{1,0},{2,3},{3,2},{4,5},{5,4},{6,7},{7,6},{8,9},{9,8},{10,11... | collective-permute-start | bytes 786440 | tf_op jit(solution)/shard_map/ppermute | solution.py:483
  46.5 4.5 %collective-permute-start.8 = (f32[1,32,2048]{2,1,0:T(8,128)}, f32[1,32,2048]{2,1,0:T(8,128)}, u32[]{:S(2)}, u32[]{:S(2)}) collective-permute-start(f32[1,32,2048]{2,1,0:T(8,128)} %collective-permute-done.4), channel_id=1, source_target_pairs={{0,1},{1,0},{2,3},{3,2},{4,5},{5,4},{6,7},{7,6},{8,9},{9,8},{10,11... | collective-permute-start | bytes 786440 | tf_op jit(solution)/shard_map/ppermute | solution.py:483
  46.6 4.4 %collective-permute-start.9 = (f32[1,32,2048]{2,1,0:T(8,128)}, f32[1,32,2048]{2,1,0:T(8,128)}, u32[]{:S(2)}, u32[]{:S(2)}) collective-permute-start(f32[1,32,2048]{2,1,0:T(8,128)} %collective-permute-done.5), channel_id=1, source_target_pairs={{0,1},{1,0},{2,3},{3,2},{4,5},{5,4},{6,7},{7,6},{8,9},{9,8},{10,11... | collective-permute-start | bytes 786440 | tf_op jit(solution)/shard_map/ppermute | solution.py:483
  61.3 23.6 %copy-start.32 = (f32[512]{0:T(512)S(1)}, f32[512]{0:T(512)}, u32[]{:S(2)}) copy-start(f32[512]{0:T(512)} %broadcast_maximum_fusion.1) | copy-start | bytes 6148
  91.7 11.2 %copy-start.8 = (bf16[3,128,128]{2,1,0:T(8,128)(2,1)S(1)}, bf16[3,128,128]{2,1,0:T(8,128)(2,1)}, u32[]{:S(2)}) copy-start(bf16[3,128,128]{2,1,0:T(8,128)(2,1)} %get-tuple-element.57.bb_hbm) | copy-start | bytes 294916
  91.7 11.2 %copy-start.9 = (bf16[3,128,128]{2,1,0:T(8,128)(2,1)S(1)}, bf16[3,128,128]{2,1,0:T(8,128)(2,1)}, u32[]{:S(2)}) copy-start(bf16[3,128,128]{2,1,0:T(8,128)(2,1)} %get-tuple-element.61.bf_hbm) | copy-start | bytes 294916
  91.7 11.2 %copy-start.15 = (bf16[1,128,128]{2,1,0:T(8,128)(2,1)S(1)}, bf16[1,128,128]{2,1,0:T(8,128)(2,1)}, u32[]{:S(2)}) copy-start(bf16[1,128,128]{2,1,0:T(8,128)(2,1)} %copy-done.14) | copy-start | bytes 98308
  91.7 11.3 %copy-start.19 = (bf16[1,128,128]{1,2,0:T(8,128)(2,1)S(1)}, bf16[1,128,128]{1,2,0:T(8,128)(2,1)}, u32[]{:S(2)}) copy-start(bf16[1,128,128]{1,2,0:T(8,128)(2,1)} %copy.20) | copy-start | bytes 98308
  102.9 11.3 %copy-start.6 = (bf16[3,128,128]{2,1,0:T(8,128)(2,1)S(1)}, bf16[3,128,128]{2,1,0:T(8,128)(2,1)}, u32[]{:S(2)}) copy-start(bf16[3,128,128]{2,1,0:T(8,128)(2,1)} %get-tuple-element.58.bb_hbm) | copy-start | bytes 294916
  102.9 11.3 %copy-start.7 = (bf16[3,128,128]{2,1,0:T(8,128)(2,1)S(1)}, bf16[3,128,128]{2,1,0:T(8,128)(2,1)}, u32[]{:S(2)}) copy-start(bf16[3,128,128]{2,1,0:T(8,128)(2,1)} %get-tuple-element.62.bf_hbm) | copy-start | bytes 294916
  102.9 11.3 %copy-start.13 = (bf16[1,128,128]{2,1,0:T(8,128)(2,1)S(1)}, bf16[1,128,128]{2,1,0:T(8,128)(2,1)}, u32[]{:S(2)}) copy-start(bf16[1,128,128]{2,1,0:T(8,128)(2,1)} %copy-done.12) | copy-start | bytes 98308
  103.0 11.3 %copy-start.18 = (bf16[1,128,128]{1,2,0:T(8,128)(2,1)S(1)}, bf16[1,128,128]{1,2,0:T(8,128)(2,1)}, u32[]{:S(2)}) copy-start(bf16[1,128,128]{1,2,0:T(8,128)(2,1)} %copy.18) | copy-start | bytes 98308
  (25 other events, 56.0 us)
Sparse Core Ops, SparseCore 0:
  9.0 35.4 all-gather.4
  46.0 38.7 all-gather.2

commit v8 on v7

--- a/solution.py
+++ b/solution.py
@@ -274,7 +274,6 @@
             pltpu.VMEM((rows, plane_width), jnp.bfloat16),
             pltpu.SemaphoreType.DMA((len(est_pieces) + 8,)),
         ],
-        compiler_params=pltpu.CompilerParams(vmem_limit_bytes=48 * 1024 * 1024),
         cost_estimate=pl.CostEstimate(
             flops=2 * rows * plane_width * (4 * BW + 2 * rows + 2 * blocks // BR * BR),
             bytes_accessed=rows * plane_width * 10,

time: 134 us -> 138 us (1.030)
  local copies, waits for them, and re-layouts: 34.9 us -> 22.1 us
  Pallas kernels: 52.1 us -> 60.7 us
  waiting for transfers between devices: 12.8 us -> 19.6 us
  other arithmetic: 5.79 us -> 7.81 us
    unnamed x74 -> x34, local copies, waits for them, and re-layouts: 16.2 us -> 0.07 us
    pallas_call x4, Pallas kernels: 47.1 us -> 55.7 us  [kernel_update(): pl.pallas_call(functools.partial(plane_kernel, len(est_pieces), raw_index...]
    all_gather x1, waiting for transfers between devices: 9.83 us -> 16.6 us  [local(): lax.all_gather(jnp.stack(pieces[1:]), 'tile', axis=2, tiled=True)]
    convert_element_type x4, other arithmetic: 1.99 us -> 4.62 us  [kernel_update(): pick_mat.astype(jnp.bfloat16)]
    broadcast_in_dim x4, local copies, waits for them, and re-layouts: 1.18 us -> 3.47 us  [kernel_update(): count = jnp.broadcast_to(jnp.maximum(count, 1.0)[:, None], (blocks, BW))]
  transfers between devices with their start and end apart: 12 -> 12, of which waited for: 3 -> 3; matrix products, arithmetic and copies ran while one was open for 16% -> 17% of each run, Pallas kernels for 14% -> 14%
where the time goes in v8:
time: 138 us; the launch traced here: 137 us
  Pallas kernels  60.7 us (44%)
  local copies, waits for them, and re-layouts  22.1 us (16%)
  waiting for transfers between devices  19.6 us (14%)
  between operations  15.6 us (11%)
  starting transfers between devices  11.6 us (8%)
  other arithmetic  7.81 us (6%)
    pallas_call x4, Pallas kernels, kernel_update(): pl.pallas_call(functools.partial(plane_kernel, len(est_pieces), raw_index...  55.7 us
    all_gather x1, waiting for transfers between devices, local(): lax.all_gather(jnp.stack(pieces[1:]), 'tile', axis=2, tiled=True)  16.6 us
    ppermute x6, starting transfers between devices, passed_along(): return lax.ppermute(x, axis, [(i, (i + by) % count) for i in range(count)])  10.6 us
    squeeze x4, local copies, waits for them, and re-layouts, local(): b[update_index * planes + p]  6.33 us
    pallas_call x1, Pallas kernels, all_bands(): pl.pallas_call(band_kernel, out_shape=(jax.ShapeDtypeStruct((count, rows,...  5.03 us
    convert_element_type x4, other arithmetic, kernel_update(): pick_mat.astype(jnp.bfloat16)  4.62 us
    broadcast_in_dim x4, local copies, waits for them, and re-layouts, kernel_update(): count = jnp.broadcast_to(jnp.maximum(count, 1.0)[:, None], (blocks, BW))  3.47 us
    ppermute x6, waiting for transfers between devices, passed_along(): return lax.ppermute(x, axis, [(i, (i + by) % count) for i in range(count)])  2.92 us
  transfers between devices with their start and end apart: 12, of which 3 were waited for; matrix products, arithmetic and copies ran while one was open for 17% of the time, Pallas kernels for 14%

profile of v8, /device:TPU:0, one launch (start us, length us, event | category | flops | bytes accessed | tf_op | source)
XLA Modules:
  0.0 137.4 jit_solution(5770571091823131692)
XLA Ops:
  6.5 1.8 %constant_dynamic-slice_fusion.4 = (bf16[1,1,32,2048]{3,2,1,0:T(8,128)(2,1)}, bf16[1,32,2048]{2,1,0:T(8,128)(2,1)S(1)}, bf16[1,32,2048]{2,1,0:T(8,128)(2,1)S(1)}, bf16[1,32,2048]{2,1,0:T(8,128)(2,1)S(1)}) fusion(bf16[1,4,32,2048]{3,2,1,0:T(8,128)(2,1)} %param.10, s32[]{:T(128)S(6)} %select_n.240, s32[]{:T(128)S(6)} %select_n.218, s32[]{:T(128)S(6)} %select_n.216, ...), kind=kLoop, calls=%fused_computation.57 | loop fusion | bytes 1048592 | tf_op jit(solution)/shard_map/dynamic_slice | solution.py:470
  8.4 3.1 %collective-permute-start.3 = (f32[1,32,2048]{2,1,0:T(8,128)}, f32[1,32,2048]{2,1,0:T(8,128)S(1)}, u32[]{:S(2)}, u32[]{:S(2)}) collective-permute-start(f32[1,32,2048]{2,1,0:T(8,128)} %param.9), channel_id=1, source_target_pairs={{0,2},{1,3},{2,4},{3,5},{4,6},{5,7},{6,0},{7,1},{8,10},{9,11},{10,... | collective-permute-start | bytes 786440 | tf_op jit(solution)/shard_map/ppermute | solution.py:17
  11.5 2.6 %collective-permute-start.4 = (f32[1,32,2048]{2,1,0:T(8,128)}, f32[1,32,2048]{2,1,0:T(8,128)S(1)}, u32[]{:S(2)}, u32[]{:S(2)}) collective-permute-start(f32[1,32,2048]{2,1,0:T(8,128)} %param.9), channel_id=1, source_target_pairs={{0,4},{1,5},{2,6},{3,7},{4,0},{5,1},{6,2},{7,3},{8,12},{9,13},{10,... | collective-permute-start | bytes 786440 | tf_op jit(solution)/shard_map/ppermute | solution.py:17
  14.1 2.4 %collective-permute-start = (bf16[1,32,2048]{2,1,0:T(8,128)(2,1)S(1)}, bf16[1,32,2048]{2,1,0:T(8,128)(2,1)S(1)}, u32[]{:S(2)}, u32[]{:S(2)}) collective-permute-start(bf16[1,32,2048]{2,1,0:T(8,128)(2,1)S(1)} %get-tuple-element.53), channel_id=1, source_target_pairs={{0,24},{8,0},{16,8},{24,16},{1,25},{9,1},{17,9},{25,17},{2,26},{10... | collective-permute-start | bytes 393224 | tf_op jit(solution)/shard_map/ppermute | solution.py:17
  18.5 0.9 fusion.33
  20.2 1.3 collective-permute-start.5
  21.6 2.3 %collective-permute-done.1 = bf16[1,32,2048]{2,1,0:T(8,128)(2,1)S(1)} collective-permute-done((bf16[1,32,2048]{2,1,0:T(8,128)(2,1)S(1)}, bf16[1,32,2048]{2,1,0:T(8,128)(2,1)S(1)}, u32[]{:S(2)}, u32[]{:S(2)}) %collective-permute-start.1) | collective-permute-done | bytes 131104 | tf_op jit(solution)/shard_map/ppermute | solution.py:17
  30.8 5.0 %shard_map.91 = (bf16[4,256,256]{2,1,0:T(8,128)(2,1)}, bf16[4,256,256]{2,1,0:T(8,128)(2,1)}, bf16[4,3,128,128]{3,2,1,0:T(8,128)(2,1)}, bf16[4,3,128,128]{3,2,1,0:T(8,128)(2,1)}) custom-call(f32[68]{0:T(128)} %reshape.563.row_ref, f32[68]{0:T(128)} %reshape.564.col_ref), custom_call_target="tpu_custom_call" | custom-call | tf_op jit(solution)/shard_map/pallas_call | solution.py:217
  36.8 1.8 %slice_bitcast_fusion.8 = (bf16[3,128,128]{2,1,0:T(8,128)(2,1)}, bf16[3,128,128]{2,1,0:T(8,128)(2,1)}, bf16[3,128,128]{2,1,0:T(8,128)(2,1)}, bf16[3,128,128]{2,1,0:T(8,128)(2,1)}) fusion(bf16[4,3,128,128]{3,2,1,0:T(8,128)(2,1)} %get-tuple-element.10), kind=kLoop, calls=%fused_computation.41 | loop fusion | bytes 786432 | tf_op jit(solution)/shard_map/squeeze | solution.py:508
  38.6 1.8 %slice_bitcast_fusion.9 = (bf16[3,128,128]{2,1,0:T(8,128)(2,1)}, bf16[3,128,128]{2,1,0:T(8,128)(2,1)}, bf16[3,128,128]{2,1,0:T(8,128)(2,1)}, bf16[3,128,128]{2,1,0:T(8,128)(2,1)}) fusion(bf16[4,3,128,128]{3,2,1,0:T(8,128)(2,1)} %get-tuple-element.9), kind=kLoop, calls=%fused_computation.42 | loop fusion | bytes 786432 | tf_op jit(solution)/shard_map/squeeze | solution.py:508
  40.4 1.9 %slice_bitcast_fusion = (bf16[256,256]{1,0:T(8,128)(2,1)}, bf16[256,256]{1,0:T(8,128)(2,1)}, bf16[256,256]{1,0:T(8,128)(2,1)}, bf16[256,256]{1,0:T(8,128)(2,1)}) fusion(bf16[4,256,256]{2,1,0:T(8,128)(2,1)} %get-tuple-element.12), kind=kLoop, calls=%fused_computation.30 | loop fusion | bytes 1048576 | tf_op jit(solution)/shard_map/squeeze | solution.py:508
  43.1 1.2 fusion.13
  44.3 1.1 fusion.12
  46.0 1.1 fusion.11
  51.7 1.2 fusion.10
  53.0 1.0 broadcast_in_dim.14.cnt_hbm
  54.0 14.1 %shard_map.92.rest_0_ = f32[256,2048]{1,0:T(8,128)} custom-call(s32[8]{0:T(128)} %broadcast_multiply_fusion.offs_ref, f32[1]{0:T(128)} %get-tuple-element.75.bg_ref, bf16[128,128]{1,0:T(8,128)(2,1)} %bitcast.97, bf16[128,128]{1,0:T(8,128)(2,1)} %bitcast.98, bf16[1,1,256,2048]{3,2,1,0:T(8,128)(2,1)} %all-gather.5.cloned.1.call-done.raw_hbm, ...), custom_call_target="tpu_custom_call" | custom-call | flops 2147483648 | bytes 5242880 | tf_op jit(solution)/shard_map/pallas_call | solution.py:256
  68.2 16.6 %all-gather.3.cloned.1.call-done.raw_hbm = bf16[3,1,256,2048]{3,2,1,0:T(8,128)(2,1)} async-done(((bf16[3,1,32,2048]{3,2,1,0:T(8,128)(2,1)}), bf16[3,1,256,2048]{3,2,1,0:T(8,128)(2,1)}) %all-gather.3.cloned.1.call-update) | async-done | bytes 3145744 | tf_op jit(solution)/shard_map/all_gather | solution.py:476
  85.6 13.9 %shard_map.93.rest_0_ = f32[256,2048]{1,0:T(8,128)} custom-call(s32[1]{0:T(128)} %constant.162.clone.1.offs_ref, f32[1]{0:T(128)} %get-tuple-element.78.bg_ref, bf16[128,128]{1,0:T(8,128)(2,1)} %bitcast.90, bf16[128,128]{1,0:T(8,128)(2,1)} %bitcast.93, bf16[3,1,256,2048]{3,2,1,0:T(8,128)(2,1)} %all-gather.3.cloned.1.call-done.raw_hbm, ...), custom_call_target="tpu_custom_call" | custom-call | flops 2147483648 | bytes 5242880 | tf_op jit(solution)/shard_map/pallas_call | solution.py:256
  99.5 0.8 broadcast_in_dim.12.cnt_hbm
  100.3 14.0 %shard_map.94.rest_0_ = f32[256,2048]{1,0:T(8,128)} custom-call(s32[1]{0:T(128)} %constant.162.clone.1.offs_ref, f32[1]{0:T(128)} %get-tuple-element.76.bg_ref, bf16[128,128]{1,0:T(8,128)(2,1)} %bitcast.89, bf16[128,128]{1,0:T(8,128)(2,1)} %bitcast.92, bf16[3,1,256,2048]{3,2,1,0:T(8,128)(2,1)} %all-gather.3.cloned.1.call-done.raw_hbm, ...), custom_call_target="tpu_custom_call" | custom-call | flops 2147483648 | bytes 5242880 | tf_op jit(solution)/shard_map/pallas_call | solution.py:256
  114.3 0.8 broadcast_in_dim.10.cnt_hbm
  115.1 13.8 %shard_map.95 = f32[256,2048]{1,0:T(8,128)} custom-call(s32[1]{0:T(128)} %constant.162.clone.1.offs_ref, f32[1]{0:T(128)} %get-tuple-element.77.bg_ref, bf16[128,128]{1,0:T(8,128)(2,1)} %bitcast.88, bf16[128,128]{1,0:T(8,128)(2,1)} %bitcast.91, bf16[3,1,256,2048]{3,2,1,0:T(8,128)(2,1)} %all-gather.3.cloned.1.call-done.raw_hbm, ...), custom_call_target="tpu_custom_call" | custom-call | flops 2147483648 | bytes 5242880 | tf_op jit(solution)/shard_map/pallas_call | solution.py:256
  128.9 1.7 %dynamic-slice_bitcast_fusion = f32[1,32,2048]{2,1,0:T(8,128)} fusion(f32[256,2048]{1,0:T(8,128)} %shard_map.95, s32[]{:T(128)S(6)} %select_n.243), kind=kLoop, calls=%fused_computation.29 | loop fusion | bytes 524292 | tf_op jit(solution)/shard_map/dynamic_slice | solution.py:514
  (106 shorter events, 15.6 us)
Async XLA Ops:
  6.5 18.6 %copy-start.16 = (s32[4]{0:T(128)S(1)}, s32[4]{0:T(128)}, u32[]{:S(2)}) copy-start(s32[4]{0:T(128)} %param.16) | copy-start | bytes 52
  6.5 20.4 %copy-start.14 = (f32[4,4,17]{2,1,0:T(4,128)S(1)}, f32[4,4,17]{2,1,0:T(4,128)}, u32[]{:S(2)}) copy-start(f32[4,4,17]{2,1,0:T(4,128)} %param.14) | copy-start | bytes 3268
  6.5 21.1 %copy-start.15 = (f32[4,4,17]{2,1,0:T(4,128)S(1)}, f32[4,4,17]{2,1,0:T(4,128)}, u32[]{:S(2)}) copy-start(f32[4,4,17]{2,1,0:T(4,128)} %param.15) | copy-start | bytes 3268
  6.5 46.5 %all-gather.5.cloned.1.call-start = ((), (), s32[]{:S(2)}) async-start(), calls=%async_computation.1 | async-start | bytes 1179648 | tf_op jit(solution)/shard_map/all_gather | solution.py:475
  8.4 76.4 %all-gather.3.cloned.1.call-start = ((), (), s32[]{:S(2)}) async-start(), calls=%async_computation | async-start | bytes 3538944 | tf_op jit(solution)/shard_map/all_gather | solution.py:476
  8.4 38.7 %collective-permute-start.3 = (f32[1,32,2048]{2,1,0:T(8,128)}, f32[1,32,2048]{2,1,0:T(8,128)S(1)}, u32[]{:S(2)}, u32[]{:S(2)}) collective-permute-start(f32[1,32,2048]{2,1,0:T(8,128)} %param.9), channel_id=1, source_target_pairs={{0,2},{1,3},{2,4},{3,5},{4,6},{5,7},{6,0},{7,1},{8,10},{9,11},{10,... | collective-permute-start | bytes 786440 | tf_op jit(solution)/shard_map/ppermute | solution.py:17
  11.5 36.1 %collective-permute-start.4 = (f32[1,32,2048]{2,1,0:T(8,128)}, f32[1,32,2048]{2,1,0:T(8,128)S(1)}, u32[]{:S(2)}, u32[]{:S(2)}) collective-permute-start(f32[1,32,2048]{2,1,0:T(8,128)} %param.9), channel_id=1, source_target_pairs={{0,4},{1,5},{2,6},{3,7},{4,0},{5,1},{6,2},{7,3},{8,12},{9,13},{10,... | collective-permute-start | bytes 786440 | tf_op jit(solution)/shard_map/ppermute | solution.py:17
  14.1 6.1 %collective-permute-start = (bf16[1,32,2048]{2,1,0:T(8,128)(2,1)S(1)}, bf16[1,32,2048]{2,1,0:T(8,128)(2,1)S(1)}, u32[]{:S(2)}, u32[]{:S(2)}) collective-permute-start(bf16[1,32,2048]{2,1,0:T(8,128)(2,1)S(1)} %get-tuple-element.53), channel_id=1, source_target_pairs={{0,24},{8,0},{16,8},{24,16},{1,25},{9,1},{17,9},{25,17},{2,26},{10... | collective-permute-start | bytes 393224 | tf_op jit(solution)/shard_map/ppermute | solution.py:17
  16.6 7.3 %collective-permute-start.1 = (bf16[1,32,2048]{2,1,0:T(8,128)(2,1)S(1)}, bf16[1,32,2048]{2,1,0:T(8,128)(2,1)S(1)}, u32[]{:S(2)}, u32[]{:S(2)}) collective-permute-start(bf16[1,32,2048]{2,1,0:T(8,128)(2,1)S(1)} %get-tuple-element.52), channel_id=1, source_target_pairs={{0,16},{8,24},{16,0},{24,8},{1,17},{9,25},{17,1},{25,9},{2,18},{10... | collective-permute-start | bytes 393224 | tf_op jit(solution)/shard_map/ppermute | solution.py:17
  17.1 6.8 %collective-permute-start.2 = (bf16[1,32,2048]{2,1,0:T(8,128)(2,1)S(1)}, bf16[1,32,2048]{2,1,0:T(8,128)(2,1)S(1)}, u32[]{:S(2)}, u32[]{:S(2)}) collective-permute-start(bf16[1,32,2048]{2,1,0:T(8,128)(2,1)S(1)} %get-tuple-element.54), channel_id=1, source_target_pairs={{0,8},{8,16},{16,24},{24,0},{1,9},{9,17},{17,25},{25,1},{2,10},{10... | collective-permute-start | bytes 393224 | tf_op jit(solution)/shard_map/ppermute | solution.py:17
  20.2 27.5 %collective-permute-start.5 = (f32[1,32,2048]{2,1,0:T(8,128)}, f32[1,32,2048]{2,1,0:T(8,128)S(1)}, u32[]{:S(2)}, u32[]{:S(2)}) collective-permute-start(f32[1,32,2048]{2,1,0:T(8,128)} %param.9), channel_id=1, source_target_pairs={{0,6},{1,7},{2,0},{3,1},{4,2},{5,3},{6,4},{7,5},{8,14},{9,15},{10,... | collective-permute-start | bytes 786440 | tf_op jit(solution)/shard_map/ppermute | solution.py:17
  23.9 29.1 %collective-permute-start.6 = (f32[1,32,2048]{2,1,0:T(8,128)}, f32[1,32,2048]{2,1,0:T(8,128)S(1)}, u32[]{:S(2)}, u32[]{:S(2)}) collective-permute-start(f32[1,32,2048]{2,1,0:T(8,128)} %param.9), channel_id=1, source_target_pairs={{0,1},{1,0},{2,3},{3,2},{4,5},{5,4},{6,7},{7,6},{8,9},{9,8},{10,11... | collective-permute-start | bytes 786440 | tf_op jit(solution)/shard_map/ppermute | solution.py:482
  35.9 6.4 %copy-start = (bf16[4,256,256]{2,1,0:T(8,128)(2,1)S(1)}, bf16[4,256,256]{2,1,0:T(8,128)(2,1)}, u32[]{:S(2)}) copy-start(bf16[4,256,256]{2,1,0:T(8,128)(2,1)} %get-tuple-element.11) | copy-start | bytes 1572868
  43.1 7.9 %copy-start.6 = (f32[4]{0:T(128)S(1)}, f32[4]{0:T(128)}, u32[]{:S(2)}) copy-start(f32[4]{0:T(128)} %param.17) | copy-start | bytes 52
  47.1 6.9 %copy-start.7 = (f32[1,32,2048]{2,1,0:T(8,128)}, f32[1,32,2048]{2,1,0:T(8,128)S(1)}, u32[]{:S(2)}) copy-start(f32[1,32,2048]{2,1,0:T(8,128)S(1)} %collective-permute-done.3) | copy-start | bytes 786436
  47.1 5.8 %collective-permute-start.7 = (f32[1,32,2048]{2,1,0:T(8,128)S(1)}, f32[1,32,2048]{2,1,0:T(8,128)S(1)}, u32[]{:S(2)}, u32[]{:S(2)}) collective-permute-start(f32[1,32,2048]{2,1,0:T(8,128)S(1)} %collective-permute-done.3), channel_id=1, source_target_pairs={{0,1},{1,0},{2,3},{3,2},{4,5},{5,4},{6,7},{7,6},{8,9},{9,8},{10,11... | collective-permute-start | bytes 786440 | tf_op jit(solution)/shard_map/ppermute | solution.py:482
  47.6 6.4 %copy-start.8 = (f32[1,32,2048]{2,1,0:T(8,128)}, f32[1,32,2048]{2,1,0:T(8,128)S(1)}, u32[]{:S(2)}) copy-start(f32[1,32,2048]{2,1,0:T(8,128)S(1)} %collective-permute-done.4) | copy-start | bytes 786436
  47.6 5.3 %collective-permute-start.8 = (f32[1,32,2048]{2,1,0:T(8,128)S(1)}, f32[1,32,2048]{2,1,0:T(8,128)S(1)}, u32[]{:S(2)}, u32[]{:S(2)}) collective-permute-start(f32[1,32,2048]{2,1,0:T(8,128)S(1)} %collective-permute-done.4), channel_id=1, source_target_pairs={{0,1},{1,0},{2,3},{3,2},{4,5},{5,4},{6,7},{7,6},{8,9},{9,8},{10,11... | collective-permute-start | bytes 786440 | tf_op jit(solution)/shard_map/ppermute | solution.py:482
  47.7 6.3 %copy-start.9 = (f32[1,32,2048]{2,1,0:T(8,128)}, f32[1,32,2048]{2,1,0:T(8,128)S(1)}, u32[]{:S(2)}) copy-start(f32[1,32,2048]{2,1,0:T(8,128)S(1)} %collective-permute-done.5) | copy-start | bytes 786436
  47.7 5.3 %collective-permute-start.9 = (f32[1,32,2048]{2,1,0:T(8,128)S(1)}, f32[1,32,2048]{2,1,0:T(8,128)S(1)}, u32[]{:S(2)}, u32[]{:S(2)}) collective-permute-start(f32[1,32,2048]{2,1,0:T(8,128)S(1)} %collective-permute-done.5), channel_id=1, source_target_pairs={{0,1},{1,0},{2,3},{3,2},{4,5},{5,4},{6,7},{7,6},{8,9},{9,8},{10,11... | collective-permute-start | bytes 786440 | tf_op jit(solution)/shard_map/ppermute | solution.py:482
  48.2 5.8 %copy-start.5 = (bf16[1,128,128]{2,1,0:T(8,128)(2,1)}, bf16[1,128,128]{2,1,0:T(8,128)(2,1)S(1)}, u32[]{:S(2)}) copy-start(bf16[1,128,128]{2,1,0:T(8,128)(2,1)S(1)} %get-tuple-element.63) | copy-start | bytes 98308
  48.2 20.0 %copy-start.1 = (bf16[1,128,128]{2,1,0:T(8,128)(2,1)}, bf16[1,128,128]{2,1,0:T(8,128)(2,1)S(1)}, u32[]{:S(2)}) copy-start(bf16[1,128,128]{2,1,0:T(8,128)(2,1)S(1)} %get-tuple-element.65) | copy-start | bytes 98308
  48.2 20.0 %copy-start.2 = (bf16[1,128,128]{2,1,0:T(8,128)(2,1)}, bf16[1,128,128]{2,1,0:T(8,128)(2,1)S(1)}, u32[]{:S(2)}) copy-start(bf16[1,128,128]{2,1,0:T(8,128)(2,1)S(1)} %get-tuple-element.64) | copy-start | bytes 98308
  48.2 20.0 %copy-start.3 = (bf16[1,128,128]{2,1,0:T(8,128)(2,1)}, bf16[1,128,128]{2,1,0:T(8,128)(2,1)S(1)}, u32[]{:S(2)}) copy-start(bf16[1,128,128]{2,1,0:T(8,128)(2,1)S(1)} %get-tuple-element.66) | copy-start | bytes 98308
  (5 other events, 10.1 us)
Sparse Core Ops, SparseCore 0:
  9.0 35.4 all-gather.4
  46.0 38.6 all-gather.2

commit v9 on v8

--- a/solution.py
+++ b/solution.py
@@ -116,12 +116,12 @@
         return slice(c * BW, (c + 1) * BW)
 
     est_copies = []
-    for k, piece in enumerate(est_hbm):
-        if est_count == 1:
-            target = est_ref
-        else:
+    if est_count == 1:
+        est_ref = est_hbm[0]
+    else:
+        for k, piece in enumerate(est_hbm):
             target = est_ref.at[pl.ds(pl.multiple_of(offs_ref[k], BR), piece.shape[0])]
-        est_copies.append(pltpu.make_async_copy(piece, target, sems.at[k]))
+            est_copies.append(pltpu.make_async_copy(piece, target, sems.at[k]))
     sources = [raw_hbm.at[raw_index], s_hbm, cnt_hbm, g_hbm, bf_hbm, bb_hbm, a_hbm, at_hbm]
     targets = [raw_ref, s_ref, cnt_ref, g_ref, bf_ref, bb_ref, a_ref, at_ref]
     copies = [
@@ -256,7 +256,7 @@
     return pl.pallas_call(
         functools.partial(plane_kernel, len(est_pieces), raw_index),
         out_shape=jax.ShapeDtypeStruct((rows, plane_width), jnp.float32),
-        in_specs=[smem, smem, vmem, vmem] + [hbm] * len(operands),
+        in_specs=[smem, smem, vmem, vmem] + [hbm] * 8 + [vmem if len(est_pieces) == 1 else hbm] * len(est_pieces),
         out_specs=vmem,
         scratch_shapes=[
             pltpu.VMEM((rows, plane_width), jnp.float32),

time: 138 us -> 139 us (level)
  no operation moved by 1% of the time
where the time goes in v9:
time: 139 us; the launch traced here: 138 us
  Pallas kernels  61.4 us (44%)
  local copies, waits for them, and re-layouts  22.1 us (16%)
  waiting for transfers between devices  19.6 us (14%)
  between operations  15.6 us (11%)
  starting transfers between devices  11.6 us (8%)
  other arithmetic  7.81 us (6%)
    pallas_call x4, Pallas kernels, kernel_update(): pl.pallas_call(functools.partial(plane_kernel, len(est_pieces), raw_index...  56.4 us
    all_gather x1, waiting for transfers between devices, local(): lax.all_gather(jnp.stack(pieces[1:]), 'tile', axis=2, tiled=True)  16.6 us
    ppermute x6, starting transfers between devices, passed_along(): return lax.ppermute(x, axis, [(i, (i + by) % count) for i in range(count)])  10.6 us
    squeeze x4, local copies, waits for them, and re-layouts, local(): b[update_index * planes + p]  6.33 us
    pallas_call x1, Pallas kernels, all_bands(): pl.pallas_call(band_kernel, out_shape=(jax.ShapeDtypeStruct((count, rows,...  5.03 us
    convert_element_type x4, other arithmetic, kernel_update(): pick_mat.astype(jnp.bfloat16)  4.62 us
    broadcast_in_dim x4, local copies, waits for them, and re-layouts, kernel_update(): count = jnp.broadcast_to(jnp.maximum(count, 1.0)[:, None], (blocks, BW))  3.47 us
    ppermute x6, waiting for transfers between devices, passed_along(): return lax.ppermute(x, axis, [(i, (i + by) % count) for i in range(count)])  2.92 us
  transfers between devices with their start and end apart: 12, of which 3 were waited for; matrix products, arithmetic and copies ran while one was open for 17% of the time, Pallas kernels for 14%

profile of v9, /device:TPU:0, one launch (start us, length us, event | category | flops | bytes accessed | tf_op | source)
XLA Modules:
  0.0 138.1 jit_solution(9795362534978835283)
XLA Ops:
  6.5 1.8 %constant_dynamic-slice_fusion.4 = (bf16[1,1,32,2048]{3,2,1,0:T(8,128)(2,1)}, bf16[1,32,2048]{2,1,0:T(8,128)(2,1)S(1)}, bf16[1,32,2048]{2,1,0:T(8,128)(2,1)S(1)}, bf16[1,32,2048]{2,1,0:T(8,128)(2,1)S(1)}) fusion(bf16[1,4,32,2048]{3,2,1,0:T(8,128)(2,1)} %param.10, s32[]{:T(128)S(6)} %select_n.240, s32[]{:T(128)S(6)} %select_n.218, s32[]{:T(128)S(6)} %select_n.216, ...), kind=kLoop, calls=%fused_computation.57 | loop fusion | bytes 1048592 | tf_op jit(solution)/shard_map/dynamic_slice | solution.py:470
  8.4 3.1 %collective-permute-start.3 = (f32[1,32,2048]{2,1,0:T(8,128)}, f32[1,32,2048]{2,1,0:T(8,128)S(1)}, u32[]{:S(2)}, u32[]{:S(2)}) collective-permute-start(f32[1,32,2048]{2,1,0:T(8,128)} %param.9), channel_id=1, source_target_pairs={{0,2},{1,3},{2,4},{3,5},{4,6},{5,7},{6,0},{7,1},{8,10},{9,11},{10,... | collective-permute-start | bytes 786440 | tf_op jit(solution)/shard_map/ppermute | solution.py:17
  11.5 2.6 %collective-permute-start.4 = (f32[1,32,2048]{2,1,0:T(8,128)}, f32[1,32,2048]{2,1,0:T(8,128)S(1)}, u32[]{:S(2)}, u32[]{:S(2)}) collective-permute-start(f32[1,32,2048]{2,1,0:T(8,128)} %param.9), channel_id=1, source_target_pairs={{0,4},{1,5},{2,6},{3,7},{4,0},{5,1},{6,2},{7,3},{8,12},{9,13},{10,... | collective-permute-start | bytes 786440 | tf_op jit(solution)/shard_map/ppermute | solution.py:17
  14.1 2.4 %collective-permute-start = (bf16[1,32,2048]{2,1,0:T(8,128)(2,1)S(1)}, bf16[1,32,2048]{2,1,0:T(8,128)(2,1)S(1)}, u32[]{:S(2)}, u32[]{:S(2)}) collective-permute-start(bf16[1,32,2048]{2,1,0:T(8,128)(2,1)S(1)} %get-tuple-element.53), channel_id=1, source_target_pairs={{0,24},{8,0},{16,8},{24,16},{1,25},{9,1},{17,9},{25,17},{2,26},{10... | collective-permute-start | bytes 393224 | tf_op jit(solution)/shard_map/ppermute | solution.py:17
  18.5 0.9 fusion.33
  20.2 1.3 collective-permute-start.5
  21.6 2.3 %collective-permute-done.1 = bf16[1,32,2048]{2,1,0:T(8,128)(2,1)S(1)} collective-permute-done((bf16[1,32,2048]{2,1,0:T(8,128)(2,1)S(1)}, bf16[1,32,2048]{2,1,0:T(8,128)(2,1)S(1)}, u32[]{:S(2)}, u32[]{:S(2)}) %collective-permute-start.1) | collective-permute-done | bytes 131104 | tf_op jit(solution)/shard_map/ppermute | solution.py:17
  30.8 5.0 %shard_map.91 = (bf16[4,256,256]{2,1,0:T(8,128)(2,1)}, bf16[4,256,256]{2,1,0:T(8,128)(2,1)}, bf16[4,3,128,128]{3,2,1,0:T(8,128)(2,1)}, bf16[4,3,128,128]{3,2,1,0:T(8,128)(2,1)}) custom-call(f32[68]{0:T(128)} %reshape.563.row_ref, f32[68]{0:T(128)} %reshape.564.col_ref), custom_call_target="tpu_custom_call" | custom-call | tf_op jit(solution)/shard_map/pallas_call | solution.py:217
  36.8 1.8 %slice_bitcast_fusion.8 = (bf16[3,128,128]{2,1,0:T(8,128)(2,1)}, bf16[3,128,128]{2,1,0:T(8,128)(2,1)}, bf16[3,128,128]{2,1,0:T(8,128)(2,1)}, bf16[3,128,128]{2,1,0:T(8,128)(2,1)}) fusion(bf16[4,3,128,128]{3,2,1,0:T(8,128)(2,1)} %get-tuple-element.10), kind=kLoop, calls=%fused_computation.41 | loop fusion | bytes 786432 | tf_op jit(solution)/shard_map/squeeze | solution.py:508
  38.6 1.8 %slice_bitcast_fusion.9 = (bf16[3,128,128]{2,1,0:T(8,128)(2,1)}, bf16[3,128,128]{2,1,0:T(8,128)(2,1)}, bf16[3,128,128]{2,1,0:T(8,128)(2,1)}, bf16[3,128,128]{2,1,0:T(8,128)(2,1)}) fusion(bf16[4,3,128,128]{3,2,1,0:T(8,128)(2,1)} %get-tuple-element.9), kind=kLoop, calls=%fused_computation.42 | loop fusion | bytes 786432 | tf_op jit(solution)/shard_map/squeeze | solution.py:508
  40.4 1.9 %slice_bitcast_fusion = (bf16[256,256]{1,0:T(8,128)(2,1)}, bf16[256,256]{1,0:T(8,128)(2,1)}, bf16[256,256]{1,0:T(8,128)(2,1)}, bf16[256,256]{1,0:T(8,128)(2,1)}) fusion(bf16[4,256,256]{2,1,0:T(8,128)(2,1)} %get-tuple-element.12), kind=kLoop, calls=%fused_computation.30 | loop fusion | bytes 1048576 | tf_op jit(solution)/shard_map/squeeze | solution.py:508
  43.1 1.2 fusion.13
  44.3 1.1 fusion.12
  46.0 1.1 fusion.11
  51.7 1.2 fusion.10
  53.0 1.0 broadcast_in_dim.14.cnt_hbm
  54.0 14.1 %shard_map.92.rest_0_ = f32[256,2048]{1,0:T(8,128)} custom-call(s32[8]{0:T(128)} %broadcast_multiply_fusion.offs_ref, f32[1]{0:T(128)} %get-tuple-element.75.bg_ref, bf16[128,128]{1,0:T(8,128)(2,1)} %bitcast.97, bf16[128,128]{1,0:T(8,128)(2,1)} %bitcast.98, bf16[1,1,256,2048]{3,2,1,0:T(8,128)(2,1)} %all-gather.5.cloned.1.call-done.raw_hbm, ...), custom_call_target="tpu_custom_call" | custom-call | flops 2147483648 | bytes 5242880 | tf_op jit(solution)/shard_map/pallas_call | solution.py:256
  68.2 16.6 %all-gather.3.cloned.1.call-done.raw_hbm = bf16[3,1,256,2048]{3,2,1,0:T(8,128)(2,1)} async-done(((bf16[3,1,32,2048]{3,2,1,0:T(8,128)(2,1)}), bf16[3,1,256,2048]{3,2,1,0:T(8,128)(2,1)}) %all-gather.3.cloned.1.call-update) | async-done | bytes 3145744 | tf_op jit(solution)/shard_map/all_gather | solution.py:476
  85.6 14.1 %shard_map.93.rest_0_ = f32[256,2048]{1,0:T(8,128)} custom-call(s32[1]{0:T(128)} %constant.162.clone.1.offs_ref, f32[1]{0:T(128)} %get-tuple-element.78.bg_ref, bf16[128,128]{1,0:T(8,128)(2,1)} %bitcast.90, bf16[128,128]{1,0:T(8,128)(2,1)} %bitcast.93, bf16[3,1,256,2048]{3,2,1,0:T(8,128)(2,1)} %all-gather.3.cloned.1.call-done.raw_hbm, ...), custom_call_target="tpu_custom_call" | custom-call | flops 2147483648 | bytes 5242880 | tf_op jit(solution)/shard_map/pallas_call | solution.py:256
  99.7 0.8 broadcast_in_dim.12.cnt_hbm
  100.5 14.2 %shard_map.94.rest_0_ = f32[256,2048]{1,0:T(8,128)} custom-call(s32[1]{0:T(128)} %constant.162.clone.1.offs_ref, f32[1]{0:T(128)} %get-tuple-element.76.bg_ref, bf16[128,128]{1,0:T(8,128)(2,1)} %bitcast.89, bf16[128,128]{1,0:T(8,128)(2,1)} %bitcast.92, bf16[3,1,256,2048]{3,2,1,0:T(8,128)(2,1)} %all-gather.3.cloned.1.call-done.raw_hbm, ...), custom_call_target="tpu_custom_call" | custom-call | flops 2147483648 | bytes 5242880 | tf_op jit(solution)/shard_map/pallas_call | solution.py:256
  114.8 0.8 broadcast_in_dim.10.cnt_hbm
  115.6 14.0 %shard_map.95 = f32[256,2048]{1,0:T(8,128)} custom-call(s32[1]{0:T(128)} %constant.162.clone.1.offs_ref, f32[1]{0:T(128)} %get-tuple-element.77.bg_ref, bf16[128,128]{1,0:T(8,128)(2,1)} %bitcast.88, bf16[128,128]{1,0:T(8,128)(2,1)} %bitcast.91, bf16[3,1,256,2048]{3,2,1,0:T(8,128)(2,1)} %all-gather.3.cloned.1.call-done.raw_hbm, ...), custom_call_target="tpu_custom_call" | custom-call | flops 2147483648 | bytes 5242880 | tf_op jit(solution)/shard_map/pallas_call | solution.py:256
  129.6 1.7 %dynamic-slice_bitcast_fusion = f32[1,32,2048]{2,1,0:T(8,128)} fusion(f32[256,2048]{1,0:T(8,128)} %shard_map.95, s32[]{:T(128)S(6)} %select_n.243), kind=kLoop, calls=%fused_computation.29 | loop fusion | bytes 524292 | tf_op jit(solution)/shard_map/dynamic_slice | solution.py:514
  (106 shorter events, 15.6 us)
Async XLA Ops:
  6.5 18.6 %copy-start.16 = (s32[4]{0:T(128)S(1)}, s32[4]{0:T(128)}, u32[]{:S(2)}) copy-start(s32[4]{0:T(128)} %param.16) | copy-start | bytes 52
  6.5 20.4 %copy-start.14 = (f32[4,4,17]{2,1,0:T(4,128)S(1)}, f32[4,4,17]{2,1,0:T(4,128)}, u32[]{:S(2)}) copy-start(f32[4,4,17]{2,1,0:T(4,128)} %param.14) | copy-start | bytes 3268
  6.5 21.1 %copy-start.15 = (f32[4,4,17]{2,1,0:T(4,128)S(1)}, f32[4,4,17]{2,1,0:T(4,128)}, u32[]{:S(2)}) copy-start(f32[4,4,17]{2,1,0:T(4,128)} %param.15) | copy-start | bytes 3268
  6.5 46.5 %all-gather.5.cloned.1.call-start = ((), (), s32[]{:S(2)}) async-start(), calls=%async_computation.1 | async-start | bytes 1179648 | tf_op jit(solution)/shard_map/all_gather | solution.py:475
  8.4 76.4 %all-gather.3.cloned.1.call-start = ((), (), s32[]{:S(2)}) async-start(), calls=%async_computation | async-start | bytes 3538944 | tf_op jit(solution)/shard_map/all_gather | solution.py:476
  8.4 38.7 %collective-permute-start.3 = (f32[1,32,2048]{2,1,0:T(8,128)}, f32[1,32,2048]{2,1,0:T(8,128)S(1)}, u32[]{:S(2)}, u32[]{:S(2)}) collective-permute-start(f32[1,32,2048]{2,1,0:T(8,128)} %param.9), channel_id=1, source_target_pairs={{0,2},{1,3},{2,4},{3,5},{4,6},{5,7},{6,0},{7,1},{8,10},{9,11},{10,... | collective-permute-start | bytes 786440 | tf_op jit(solution)/shard_map/ppermute | solution.py:17
  11.5 36.1 %collective-permute-start.4 = (f32[1,32,2048]{2,1,0:T(8,128)}, f32[1,32,2048]{2,1,0:T(8,128)S(1)}, u32[]{:S(2)}, u32[]{:S(2)}) collective-permute-start(f32[1,32,2048]{2,1,0:T(8,128)} %param.9), channel_id=1, source_target_pairs={{0,4},{1,5},{2,6},{3,7},{4,0},{5,1},{6,2},{7,3},{8,12},{9,13},{10,... | collective-permute-start | bytes 786440 | tf_op jit(solution)/shard_map/ppermute | solution.py:17
  14.1 6.1 %collective-permute-start = (bf16[1,32,2048]{2,1,0:T(8,128)(2,1)S(1)}, bf16[1,32,2048]{2,1,0:T(8,128)(2,1)S(1)}, u32[]{:S(2)}, u32[]{:S(2)}) collective-permute-start(bf16[1,32,2048]{2,1,0:T(8,128)(2,1)S(1)} %get-tuple-element.53), channel_id=1, source_target_pairs={{0,24},{8,0},{16,8},{24,16},{1,25},{9,1},{17,9},{25,17},{2,26},{10... | collective-permute-start | bytes 393224 | tf_op jit(solution)/shard_map/ppermute | solution.py:17
  16.6 7.3 %collective-permute-start.1 = (bf16[1,32,2048]{2,1,0:T(8,128)(2,1)S(1)}, bf16[1,32,2048]{2,1,0:T(8,128)(2,1)S(1)}, u32[]{:S(2)}, u32[]{:S(2)}) collective-permute-start(bf16[1,32,2048]{2,1,0:T(8,128)(2,1)S(1)} %get-tuple-element.52), channel_id=1, source_target_pairs={{0,16},{8,24},{16,0},{24,8},{1,17},{9,25},{17,1},{25,9},{2,18},{10... | collective-permute-start | bytes 393224 | tf_op jit(solution)/shard_map/ppermute | solution.py:17
  17.1 6.8 %collective-permute-start.2 = (bf16[1,32,2048]{2,1,0:T(8,128)(2,1)S(1)}, bf16[1,32,2048]{2,1,0:T(8,128)(2,1)S(1)}, u32[]{:S(2)}, u32[]{:S(2)}) collective-permute-start(bf16[1,32,2048]{2,1,0:T(8,128)(2,1)S(1)} %get-tuple-element.54), channel_id=1, source_target_pairs={{0,8},{8,16},{16,24},{24,0},{1,9},{9,17},{17,25},{25,1},{2,10},{10... | collective-permute-start | bytes 393224 | tf_op jit(solution)/shard_map/ppermute | solution.py:17
  20.2 27.5 %collective-permute-start.5 = (f32[1,32,2048]{2,1,0:T(8,128)}, f32[1,32,2048]{2,1,0:T(8,128)S(1)}, u32[]{:S(2)}, u32[]{:S(2)}) collective-permute-start(f32[1,32,2048]{2,1,0:T(8,128)} %param.9), channel_id=1, source_target_pairs={{0,6},{1,7},{2,0},{3,1},{4,2},{5,3},{6,4},{7,5},{8,14},{9,15},{10,... | collective-permute-start | bytes 786440 | tf_op jit(solution)/shard_map/ppermute | solution.py:17
  23.9 29.1 %collective-permute-start.6 = (f32[1,32,2048]{2,1,0:T(8,128)}, f32[1,32,2048]{2,1,0:T(8,128)S(1)}, u32[]{:S(2)}, u32[]{:S(2)}) collective-permute-start(f32[1,32,2048]{2,1,0:T(8,128)} %param.9), channel_id=1, source_target_pairs={{0,1},{1,0},{2,3},{3,2},{4,5},{5,4},{6,7},{7,6},{8,9},{9,8},{10,11... | collective-permute-start | bytes 786440 | tf_op jit(solution)/shard_map/ppermute | solution.py:482
  35.9 6.4 %copy-start = (bf16[4,256,256]{2,1,0:T(8,128)(2,1)S(1)}, bf16[4,256,256]{2,1,0:T(8,128)(2,1)}, u32[]{:S(2)}) copy-start(bf16[4,256,256]{2,1,0:T(8,128)(2,1)} %get-tuple-element.11) | copy-start | bytes 1572868
  43.1 7.9 %copy-start.6 = (f32[4]{0:T(128)S(1)}, f32[4]{0:T(128)}, u32[]{:S(2)}) copy-start(f32[4]{0:T(128)} %param.17) | copy-start | bytes 52
  47.1 6.9 %copy-start.7 = (f32[1,32,2048]{2,1,0:T(8,128)}, f32[1,32,2048]{2,1,0:T(8,128)S(1)}, u32[]{:S(2)}) copy-start(f32[1,32,2048]{2,1,0:T(8,128)S(1)} %collective-permute-done.3) | copy-start | bytes 786436
  47.1 5.8 %collective-permute-start.7 = (f32[1,32,2048]{2,1,0:T(8,128)S(1)}, f32[1,32,2048]{2,1,0:T(8,128)S(1)}, u32[]{:S(2)}, u32[]{:S(2)}) collective-permute-start(f32[1,32,2048]{2,1,0:T(8,128)S(1)} %collective-permute-done.3), channel_id=1, source_target_pairs={{0,1},{1,0},{2,3},{3,2},{4,5},{5,4},{6,7},{7,6},{8,9},{9,8},{10,11... | collective-permute-start | bytes 786440 | tf_op jit(solution)/shard_map/ppermute | solution.py:482
  47.6 6.4 %copy-start.8 = (f32[1,32,2048]{2,1,0:T(8,128)}, f32[1,32,2048]{2,1,0:T(8,128)S(1)}, u32[]{:S(2)}) copy-start(f32[1,32,2048]{2,1,0:T(8,128)S(1)} %collective-permute-done.4) | copy-start | bytes 786436
  47.6 5.3 %collective-permute-start.8 = (f32[1,32,2048]{2,1,0:T(8,128)S(1)}, f32[1,32,2048]{2,1,0:T(8,128)S(1)}, u32[]{:S(2)}, u32[]{:S(2)}) collective-permute-start(f32[1,32,2048]{2,1,0:T(8,128)S(1)} %collective-permute-done.4), channel_id=1, source_target_pairs={{0,1},{1,0},{2,3},{3,2},{4,5},{5,4},{6,7},{7,6},{8,9},{9,8},{10,11... | collective-permute-start | bytes 786440 | tf_op jit(solution)/shard_map/ppermute | solution.py:482
  47.7 6.3 %copy-start.9 = (f32[1,32,2048]{2,1,0:T(8,128)}, f32[1,32,2048]{2,1,0:T(8,128)S(1)}, u32[]{:S(2)}) copy-start(f32[1,32,2048]{2,1,0:T(8,128)S(1)} %collective-permute-done.5) | copy-start | bytes 786436
  47.7 5.3 %collective-permute-start.9 = (f32[1,32,2048]{2,1,0:T(8,128)S(1)}, f32[1,32,2048]{2,1,0:T(8,128)S(1)}, u32[]{:S(2)}, u32[]{:S(2)}) collective-permute-start(f32[1,32,2048]{2,1,0:T(8,128)S(1)} %collective-permute-done.5), channel_id=1, source_target_pairs={{0,1},{1,0},{2,3},{3,2},{4,5},{5,4},{6,7},{7,6},{8,9},{9,8},{10,11... | collective-permute-start | bytes 786440 | tf_op jit(solution)/shard_map/ppermute | solution.py:482
  48.2 5.8 %copy-start.5 = (bf16[1,128,128]{2,1,0:T(8,128)(2,1)}, bf16[1,128,128]{2,1,0:T(8,128)(2,1)S(1)}, u32[]{:S(2)}) copy-start(bf16[1,128,128]{2,1,0:T(8,128)(2,1)S(1)} %get-tuple-element.63) | copy-start | bytes 98308
  48.2 20.0 %copy-start.1 = (bf16[1,128,128]{2,1,0:T(8,128)(2,1)}, bf16[1,128,128]{2,1,0:T(8,128)(2,1)S(1)}, u32[]{:S(2)}) copy-start(bf16[1,128,128]{2,1,0:T(8,128)(2,1)S(1)} %get-tuple-element.65) | copy-start | bytes 98308
  48.2 20.0 %copy-start.2 = (bf16[1,128,128]{2,1,0:T(8,128)(2,1)}, bf16[1,128,128]{2,1,0:T(8,128)(2,1)S(1)}, u32[]{:S(2)}) copy-start(bf16[1,128,128]{2,1,0:T(8,128)(2,1)S(1)} %get-tuple-element.64) | copy-start | bytes 98308
  48.2 20.0 %copy-start.3 = (bf16[1,128,128]{2,1,0:T(8,128)(2,1)}, bf16[1,128,128]{2,1,0:T(8,128)(2,1)S(1)}, u32[]{:S(2)}) copy-start(bf16[1,128,128]{2,1,0:T(8,128)(2,1)S(1)} %get-tuple-element.66) | copy-start | bytes 98308
  (5 other events, 10.1 us)
Sparse Core Ops, SparseCore 0:
  9.0 35.4 all-gather.4
  46.0 38.6 all-gather.2

commit v10 on v4

--- a/solution.py
+++ b/solution.py
@@ -119,8 +119,12 @@
     def cols(c):
         return slice(c * BW, (c + 1) * BW)
 
-    for c in range(nc):
-        blk = est_ref[:, cols(c)].astype(bf16)
+    def lanes(c):
+        return pl.ds(pl.multiple_of(c * BW, BW), BW)
+
+    @pl.loop(0, nc)
+    def _(c):
+        blk = est_ref[:, lanes(c)].astype(bf16)
         moved = jnp.dot(blk, m_ref[...], preferred_element_type=f32)
         work[c] = moved.astype(bf16).astype(f32)
 
@@ -149,17 +153,19 @@
     for c in range(nc):
         across[:, cols(c)] = column_blur(lambda i: joined[i], bf_ref, c).astype(bf16)
     level = bg_ref[0]
-    for c in range(nc):
-        blurred = jnp.dot(a_ref[...], across[:, cols(c)], preferred_element_type=f32) + level
-        quotient = (raw_ref[:, cols(c)].astype(f32) / blurred).astype(bf16)
-        ratio[:, cols(c)] = jnp.dot(at_ref[...], quotient, preferred_element_type=f32).astype(bf16)
+    @pl.loop(0, nc)
+    def _(c):
+        blurred = jnp.dot(a_ref[...], across[:, lanes(c)], preferred_element_type=f32) + level
+        quotient = (raw_ref[:, lanes(c)].astype(f32) / blurred).astype(bf16)
+        ratio[:, lanes(c)] = jnp.dot(at_ref[...], quotient, preferred_element_type=f32).astype(bf16)
     for c in range(nc):
         spread = column_blur(lambda i: ratio[:, cols(i)], bb_ref, c).astype(bf16)
         back = jnp.dot(spread, mt_ref[...], preferred_element_type=f32)
         work[c] = back.astype(bf16).astype(f32)
     regroup(work, g_ref, joined, lambda v: v)
-    for c in range(nc):
-        out_ref[:, cols(c)] = est_ref[:, cols(c)] * joined[c]
+    @pl.loop(0, nc)
+    def _(c):
+        out_ref[:, lanes(c)] = est_ref[:, lanes(c)] * joined[c]
 
 
 def band_kernel(row_ref, col_ref, a_ref, at_ref, bf_ref, bb_ref):

time: 132 us -> 155 us (1.17)
  Pallas kernels: 48.6 us -> 79.2 us
  waiting for transfers between devices: 14.3 us -> 6.59 us
    pallas_call x4, Pallas kernels: 43.6 us -> 74.2 us  [kernel_update(): pl.pallas_call(plane_kernel, grid=(1,), out_shape=jax.ShapeDtypeStruct((r...]
    all_gather x1, waiting for transfers between devices: 11.3 us -> 3.6 us  [local(): lax.all_gather(jnp.stack(pieces[1:]), 'tile', axis=2, tiled=True)]
  transfers between devices with their start and end apart: 12 -> 12, of which waited for: 3 -> 3; matrix products, arithmetic and copies ran while one was open for 16% -> 14% of each run, Pallas kernels for 13% -> 16%
where the time goes in v10:
time: 155 us; the launch traced here: 154 us
  Pallas kernels  79.2 us (51%)
  local copies, waits for them, and re-layouts  34.9 us (23%)
  between operations  15.7 us (10%)
  starting transfers between devices  11.7 us (8%)
  waiting for transfers between devices  6.59 us (4%)
  other arithmetic  5.79 us (4%)
    pallas_call x4, Pallas kernels, kernel_update(): pl.pallas_call(plane_kernel, grid=(1,), out_shape=jax.ShapeDtypeStruct((r...  74.2 us
    unnamed x74, local copies, waits for them, and re-layouts  16.2 us
    ppermute x6, starting transfers between devices, passed_along(): return lax.ppermute(x, axis, [(i, (i + by) % count) for i in range(count)])  10.6 us
    squeeze x4, local copies, waits for them, and re-layouts, local(): b[update_index * planes + p]  6.25 us
    pallas_call x1, Pallas kernels, all_bands(): pl.pallas_call(band_kernel, out_shape=(jax.ShapeDtypeStruct((count, rows,...  5.01 us
    all_gather x1, waiting for transfers between devices, local(): lax.all_gather(jnp.stack(pieces[1:]), 'tile', axis=2, tiled=True)  3.6 us
  transfers between devices with their start and end apart: 12, of which 3 were waited for; matrix products, arithmetic and copies ran while one was open for 14% of the time, Pallas kernels for 16%

profile of v10, /device:TPU:0, one launch (start us, length us, event | category | flops | bytes accessed | tf_op | source)
XLA Modules:
  0.0 153.9 jit_solution(385998124615091490)
XLA Ops:
  6.5 1.8 %constant_dynamic-slice_fusion.5 = (bf16[1,1,32,2048]{3,2,1,0:T(8,128)(2,1)}, bf16[1,32,2048]{2,1,0:T(8,128)(2,1)S(1)}, bf16[1,32,2048]{2,1,0:T(8,128)(2,1)S(1)}, bf16[1,32,2048]{2,1,0:T(8,128)(2,1)S(1)}) fusion(bf16[1,4,32,2048]{3,2,1,0:T(8,128)(2,1)} %param.10, s32[]{:T(128)S(6)} %select_n.240, s32[]{:T(128)S(6)} %select_n.218, s32[]{:T(128)S(6)} %select_n.216, ...), kind=kLoop, calls=%fused_computation.58 | loop fusion | bytes 1048592 | tf_op jit(solution)/shard_map/dynamic_slice | solution.py:449
  8.4 3.1 %collective-permute-start.3 = (f32[1,32,2048]{2,1,0:T(8,128)}, f32[1,32,2048]{2,1,0:T(8,128)}, u32[]{:S(2)}, u32[]{:S(2)}) collective-permute-start(f32[1,32,2048]{2,1,0:T(8,128)} %param.9), channel_id=1, source_target_pairs={{0,2},{1,3},{2,4},{3,5},{4,6},{5,7},{6,0},{7,1},{8,10},{9,11},{10,... | collective-permute-start | bytes 786440 | tf_op jit(solution)/shard_map/ppermute | solution.py:15
  11.5 2.6 %collective-permute-start.4 = (f32[1,32,2048]{2,1,0:T(8,128)}, f32[1,32,2048]{2,1,0:T(8,128)}, u32[]{:S(2)}, u32[]{:S(2)}) collective-permute-start(f32[1,32,2048]{2,1,0:T(8,128)} %param.9), channel_id=1, source_target_pairs={{0,4},{1,5},{2,6},{3,7},{4,0},{5,1},{6,2},{7,3},{8,12},{9,13},{10,... | collective-permute-start | bytes 786440 | tf_op jit(solution)/shard_map/ppermute | solution.py:15
  14.1 2.4 %collective-permute-start = (bf16[1,32,2048]{2,1,0:T(8,128)(2,1)S(1)}, bf16[1,32,2048]{2,1,0:T(8,128)(2,1)S(1)}, u32[]{:S(2)}, u32[]{:S(2)}) collective-permute-start(bf16[1,32,2048]{2,1,0:T(8,128)(2,1)S(1)} %get-tuple-element.53), channel_id=1, source_target_pairs={{0,24},{8,0},{16,8},{24,16},{1,25},{9,1},{17,9},{25,17},{2,26},{10... | collective-permute-start | bytes 393224 | tf_op jit(solution)/shard_map/ppermute | solution.py:15
  20.2 1.3 collective-permute-start.5
  21.6 2.3 %collective-permute-done.1 = bf16[1,32,2048]{2,1,0:T(8,128)(2,1)S(1)} collective-permute-done((bf16[1,32,2048]{2,1,0:T(8,128)(2,1)S(1)}, bf16[1,32,2048]{2,1,0:T(8,128)(2,1)S(1)}, u32[]{:S(2)}, u32[]{:S(2)}) %collective-permute-start.1) | collective-permute-done | bytes 131104 | tf_op jit(solution)/shard_map/ppermute | solution.py:15
  30.8 5.0 %shard_map.91 = (bf16[4,256,256]{2,1,0:T(8,128)(2,1)}, bf16[4,256,256]{2,1,0:T(8,128)(2,1)}, bf16[4,3,128,128]{3,2,1,0:T(8,128)(2,1)}, bf16[4,3,128,128]{3,2,1,0:T(8,128)(2,1)}) custom-call(f32[68]{0:T(128)} %reshape.563.row_ref, f32[68]{0:T(128)} %reshape.564.col_ref), custom_call_target="tpu_custom_call" | custom-call | tf_op jit(solution)/shard_map/pallas_call | solution.py:200
  37.9 1.8 %slice_bitcast_fusion.8 = (bf16[3,128,128]{2,1,0:T(8,128)(2,1)}, bf16[3,128,128]{2,1,0:T(8,128)(2,1)}, bf16[3,128,128]{2,1,0:T(8,128)(2,1)}, bf16[3,128,128]{2,1,0:T(8,128)(2,1)}) fusion(bf16[4,3,128,128]{3,2,1,0:T(8,128)(2,1)} %get-tuple-element.10), kind=kLoop, calls=%fused_computation.41 | loop fusion | bytes 786432 | tf_op jit(solution)/shard_map/squeeze | solution.py:487
  39.7 1.8 %slice_bitcast_fusion.9 = (bf16[3,128,128]{2,1,0:T(8,128)(2,1)}, bf16[3,128,128]{2,1,0:T(8,128)(2,1)}, bf16[3,128,128]{2,1,0:T(8,128)(2,1)}, bf16[3,128,128]{2,1,0:T(8,128)(2,1)}) fusion(bf16[4,3,128,128]{3,2,1,0:T(8,128)(2,1)} %get-tuple-element.9), kind=kLoop, calls=%fused_computation.42 | loop fusion | bytes 786432 | tf_op jit(solution)/shard_map/squeeze | solution.py:487
  41.5 1.9 %slice_bitcast_fusion = (bf16[256,256]{1,0:T(8,128)(2,1)}, bf16[256,256]{1,0:T(8,128)(2,1)}, bf16[256,256]{1,0:T(8,128)(2,1)S(1)}, bf16[256,256]{1,0:T(8,128)(2,1)S(1)}) fusion(bf16[4,256,256]{2,1,0:T(8,128)(2,1)} %get-tuple-element.12), kind=kLoop, calls=%fused_computation.30 | loop fusion | bytes 1048576 | tf_op jit(solution)/shard_map/squeeze | solution.py:487
  44.2 1.1 fusion.13
  51.8 1.0 copy-done.4
  52.9 1.1 copy-done.5
  54.7 0.9 copy-done.23
  55.6 0.9 copy-done.24
  59.1 1.2 copy-done.28
  60.3 0.9 copy-done.29
  61.3 20.0 %shard_map.92.rest_0_ = f32[256,2048]{1,0:T(8,128)} custom-call(s32[8]{0:T(128)S(1)} %broadcast_multiply_fusion.offs_ref, f32[1]{0:T(128)} %get-tuple-element.75.bg_ref, bf16[1,1,256,2048]{3,2,1,0:T(8,128)(2,1)S(1)} %copy-done.28, bf16[128,128]{1,0:T(8,128)(2,1)S(1)} %bitcast.94, bf16[128,128]{1,0:T(8,128)(2,1)S(1)} %bitcast.95, ...), custom_call_target="tpu_custom_call" | custom-call | flops 2147483648 | bytes 5242880 | tf_op jit(solution)/shard_map/pallas_call | solution.py:228
  81.2 3.6 %all-gather.3.cloned.1.call-done.raw_ref = bf16[3,1,256,2048]{3,2,1,0:T(8,128)(2,1)} async-done(((bf16[3,1,32,2048]{3,2,1,0:T(8,128)(2,1)}), bf16[3,1,256,2048]{3,2,1,0:T(8,128)(2,1)}) %all-gather.3.cloned.1.call-update) | async-done | bytes 3145744 | tf_op jit(solution)/shard_map/all_gather | solution.py:455
  85.0 1.6 %copy-done = f32[256,2048]{1,0:T(8,128)S(1)} copy-done((f32[256,2048]{1,0:T(8,128)S(1)}, f32[256,2048]{1,0:T(8,128)}, u32[]{:S(2)}) %copy-start) | copy-done | bytes 2097176
  87.4 0.9 copy-done.3
  91.7 18.0 %shard_map.93.rest_0_ = f32[256,2048]{1,0:T(8,128)S(1)} custom-call(s32[1]{0:T(128)} %constant.162.clone.1.offs_ref, f32[1]{0:T(128)} %get-tuple-element.78.bg_ref, bf16[3,1,256,2048]{3,2,1,0:T(8,128)(2,1)} %all-gather.3.cloned.1.call-done.raw_ref, bf16[128,128]{1,0:T(8,128)(2,1)S(1)} %bitcast.90, bf16[128,128]{1,0:T(8,128)(2,1)S(1)} %bitcast.93, ...), custom_call_target="tpu_custom_call" | custom-call | flops 2147483648 | bytes 5242880 | tf_op jit(solution)/shard_map/pallas_call | solution.py:228
  109.9 18.3 %shard_map.94.rest_0_ = f32[256,2048]{1,0:T(8,128)S(1)} custom-call(s32[1]{0:T(128)} %constant.162.clone.1.offs_ref, f32[1]{0:T(128)} %get-tuple-element.76.bg_ref, bf16[3,1,256,2048]{3,2,1,0:T(8,128)(2,1)} %all-gather.3.cloned.1.call-done.raw_ref, bf16[128,128]{1,0:T(8,128)(2,1)S(1)} %bitcast.89, bf16[128,128]{1,0:T(8,128)(2,1)S(1)} %bitcast.92, ...), custom_call_target="tpu_custom_call" | custom-call | flops 2147483648 | bytes 5242880 | tf_op jit(solution)/shard_map/pallas_call | solution.py:228
  128.3 18.0 %shard_map.95 = f32[256,2048]{1,0:T(8,128)S(1)} custom-call(s32[1]{0:T(128)} %constant.162.clone.1.offs_ref, f32[1]{0:T(128)} %get-tuple-element.77.bg_ref, bf16[3,1,256,2048]{3,2,1,0:T(8,128)(2,1)} %all-gather.3.cloned.1.call-done.raw_ref, bf16[128,128]{1,0:T(8,128)(2,1)S(1)} %bitcast.88, bf16[128,128]{1,0:T(8,128)(2,1)S(1)} %bitcast.91, ...), custom_call_target="tpu_custom_call" | custom-call | flops 2147483648 | bytes 5242880 | tf_op jit(solution)/shard_map/pallas_call | solution.py:228
  (146 shorter events, 26.6 us)
Async XLA Ops:
  6.5 18.6 %copy-start.36 = (s32[4]{0:T(128)S(1)}, s32[4]{0:T(128)}, u32[]{:S(2)}) copy-start(s32[4]{0:T(128)} %param.16) | copy-start | bytes 52
  6.5 20.4 %copy-start.34 = (f32[4,4,17]{2,1,0:T(4,128)S(1)}, f32[4,4,17]{2,1,0:T(4,128)}, u32[]{:S(2)}) copy-start(f32[4,4,17]{2,1,0:T(4,128)} %param.14) | copy-start | bytes 3268
  6.5 21.1 %copy-start.35 = (f32[4,4,17]{2,1,0:T(4,128)S(1)}, f32[4,4,17]{2,1,0:T(4,128)}, u32[]{:S(2)}) copy-start(f32[4,4,17]{2,1,0:T(4,128)} %param.15) | copy-start | bytes 3268
  6.5 44.4 %all-gather.5.cloned.1.call-start = ((), (), s32[]{:S(2)}) async-start(), calls=%async_computation.1 | async-start | bytes 1179648 | tf_op jit(solution)/shard_map/all_gather | solution.py:454
  8.4 76.4 %all-gather.3.cloned.1.call-start = ((), (), s32[]{:S(2)}) async-start(), calls=%async_computation | async-start | bytes 3538944 | tf_op jit(solution)/shard_map/all_gather | solution.py:455
  8.4 37.5 %collective-permute-start.3 = (f32[1,32,2048]{2,1,0:T(8,128)}, f32[1,32,2048]{2,1,0:T(8,128)}, u32[]{:S(2)}, u32[]{:S(2)}) collective-permute-start(f32[1,32,2048]{2,1,0:T(8,128)} %param.9), channel_id=1, source_target_pairs={{0,2},{1,3},{2,4},{3,5},{4,6},{5,7},{6,0},{7,1},{8,10},{9,11},{10,... | collective-permute-start | bytes 786440 | tf_op jit(solution)/shard_map/ppermute | solution.py:15
  11.5 35.0 %collective-permute-start.4 = (f32[1,32,2048]{2,1,0:T(8,128)}, f32[1,32,2048]{2,1,0:T(8,128)}, u32[]{:S(2)}, u32[]{:S(2)}) collective-permute-start(f32[1,32,2048]{2,1,0:T(8,128)} %param.9), channel_id=1, source_target_pairs={{0,4},{1,5},{2,6},{3,7},{4,0},{5,1},{6,2},{7,3},{8,12},{9,13},{10,... | collective-permute-start | bytes 786440 | tf_op jit(solution)/shard_map/ppermute | solution.py:15
  14.1 6.1 %collective-permute-start = (bf16[1,32,2048]{2,1,0:T(8,128)(2,1)S(1)}, bf16[1,32,2048]{2,1,0:T(8,128)(2,1)S(1)}, u32[]{:S(2)}, u32[]{:S(2)}) collective-permute-start(bf16[1,32,2048]{2,1,0:T(8,128)(2,1)S(1)} %get-tuple-element.53), channel_id=1, source_target_pairs={{0,24},{8,0},{16,8},{24,16},{1,25},{9,1},{17,9},{25,17},{2,26},{10... | collective-permute-start | bytes 393224 | tf_op jit(solution)/shard_map/ppermute | solution.py:15
  16.6 7.3 %collective-permute-start.1 = (bf16[1,32,2048]{2,1,0:T(8,128)(2,1)S(1)}, bf16[1,32,2048]{2,1,0:T(8,128)(2,1)S(1)}, u32[]{:S(2)}, u32[]{:S(2)}) collective-permute-start(bf16[1,32,2048]{2,1,0:T(8,128)(2,1)S(1)} %get-tuple-element.52), channel_id=1, source_target_pairs={{0,16},{8,24},{16,0},{24,8},{1,17},{9,25},{17,1},{25,9},{2,18},{10... | collective-permute-start | bytes 393224 | tf_op jit(solution)/shard_map/ppermute | solution.py:15
  17.1 6.8 %collective-permute-start.2 = (bf16[1,32,2048]{2,1,0:T(8,128)(2,1)S(1)}, bf16[1,32,2048]{2,1,0:T(8,128)(2,1)S(1)}, u32[]{:S(2)}, u32[]{:S(2)}) collective-permute-start(bf16[1,32,2048]{2,1,0:T(8,128)(2,1)S(1)} %get-tuple-element.54), channel_id=1, source_target_pairs={{0,8},{8,16},{16,24},{24,0},{1,9},{9,17},{17,25},{25,1},{2,10},{10... | collective-permute-start | bytes 393224 | tf_op jit(solution)/shard_map/ppermute | solution.py:15
  20.2 26.4 %collective-permute-start.5 = (f32[1,32,2048]{2,1,0:T(8,128)}, f32[1,32,2048]{2,1,0:T(8,128)}, u32[]{:S(2)}, u32[]{:S(2)}) collective-permute-start(f32[1,32,2048]{2,1,0:T(8,128)} %param.9), channel_id=1, source_target_pairs={{0,6},{1,7},{2,0},{3,1},{4,2},{5,3},{6,4},{7,5},{8,14},{9,15},{10,... | collective-permute-start | bytes 786440 | tf_op jit(solution)/shard_map/ppermute | solution.py:15
  23.9 27.0 %collective-permute-start.6 = (f32[1,32,2048]{2,1,0:T(8,128)}, f32[1,32,2048]{2,1,0:T(8,128)}, u32[]{:S(2)}, u32[]{:S(2)}) collective-permute-start(f32[1,32,2048]{2,1,0:T(8,128)} %param.9), channel_id=1, source_target_pairs={{0,1},{1,0},{2,3},{3,2},{4,5},{5,4},{6,7},{7,6},{8,9},{9,8},{10,11... | collective-permute-start | bytes 786440 | tf_op jit(solution)/shard_map/ppermute | solution.py:461
  45.9 5.0 %collective-permute-start.7 = (f32[1,32,2048]{2,1,0:T(8,128)}, f32[1,32,2048]{2,1,0:T(8,128)}, u32[]{:S(2)}, u32[]{:S(2)}) collective-permute-start(f32[1,32,2048]{2,1,0:T(8,128)} %collective-permute-done.3), channel_id=1, source_target_pairs={{0,1},{1,0},{2,3},{3,2},{4,5},{5,4},{6,7},{7,6},{8,9},{9,8},{10,11... | collective-permute-start | bytes 786440 | tf_op jit(solution)/shard_map/ppermute | solution.py:461
  46.5 4.5 %collective-permute-start.8 = (f32[1,32,2048]{2,1,0:T(8,128)}, f32[1,32,2048]{2,1,0:T(8,128)}, u32[]{:S(2)}, u32[]{:S(2)}) collective-permute-start(f32[1,32,2048]{2,1,0:T(8,128)} %collective-permute-done.4), channel_id=1, source_target_pairs={{0,1},{1,0},{2,3},{3,2},{4,5},{5,4},{6,7},{7,6},{8,9},{9,8},{10,11... | collective-permute-start | bytes 786440 | tf_op jit(solution)/shard_map/ppermute | solution.py:461
  46.6 4.4 %collective-permute-start.9 = (f32[1,32,2048]{2,1,0:T(8,128)}, f32[1,32,2048]{2,1,0:T(8,128)}, u32[]{:S(2)}, u32[]{:S(2)}) collective-permute-start(f32[1,32,2048]{2,1,0:T(8,128)} %collective-permute-done.5), channel_id=1, source_target_pairs={{0,1},{1,0},{2,3},{3,2},{4,5},{5,4},{6,7},{7,6},{8,9},{9,8},{10,11... | collective-permute-start | bytes 786440 | tf_op jit(solution)/shard_map/ppermute | solution.py:461
  61.3 23.6 %copy-start.32 = (f32[512]{0:T(512)S(1)}, f32[512]{0:T(512)}, u32[]{:S(2)}) copy-start(f32[512]{0:T(512)} %broadcast_maximum_fusion.1) | copy-start | bytes 6148
  91.7 18.1 %copy-start.8 = (bf16[3,128,128]{2,1,0:T(8,128)(2,1)S(1)}, bf16[3,128,128]{2,1,0:T(8,128)(2,1)}, u32[]{:S(2)}) copy-start(bf16[3,128,128]{2,1,0:T(8,128)(2,1)} %get-tuple-element.57.bb_ref) | copy-start | bytes 294916
  91.7 18.1 %copy-start.9 = (bf16[3,128,128]{2,1,0:T(8,128)(2,1)S(1)}, bf16[3,128,128]{2,1,0:T(8,128)(2,1)}, u32[]{:S(2)}) copy-start(bf16[3,128,128]{2,1,0:T(8,128)(2,1)} %get-tuple-element.61.bf_ref) | copy-start | bytes 294916
  91.7 18.2 %copy-start.15 = (bf16[1,128,128]{2,1,0:T(8,128)(2,1)S(1)}, bf16[1,128,128]{2,1,0:T(8,128)(2,1)}, u32[]{:S(2)}) copy-start(bf16[1,128,128]{2,1,0:T(8,128)(2,1)} %copy-done.14) | copy-start | bytes 98308
  91.7 18.2 %copy-start.19 = (bf16[1,128,128]{1,2,0:T(8,128)(2,1)S(1)}, bf16[1,128,128]{1,2,0:T(8,128)(2,1)}, u32[]{:S(2)}) copy-start(bf16[1,128,128]{1,2,0:T(8,128)(2,1)} %copy.20) | copy-start | bytes 98308
  109.8 18.5 %copy-start.6 = (bf16[3,128,128]{2,1,0:T(8,128)(2,1)S(1)}, bf16[3,128,128]{2,1,0:T(8,128)(2,1)}, u32[]{:S(2)}) copy-start(bf16[3,128,128]{2,1,0:T(8,128)(2,1)} %get-tuple-element.58.bb_ref) | copy-start | bytes 294916
  109.8 18.5 %copy-start.7 = (bf16[3,128,128]{2,1,0:T(8,128)(2,1)S(1)}, bf16[3,128,128]{2,1,0:T(8,128)(2,1)}, u32[]{:S(2)}) copy-start(bf16[3,128,128]{2,1,0:T(8,128)(2,1)} %get-tuple-element.62.bf_ref) | copy-start | bytes 294916
  109.9 18.5 %copy-start.13 = (bf16[1,128,128]{2,1,0:T(8,128)(2,1)S(1)}, bf16[1,128,128]{2,1,0:T(8,128)(2,1)}, u32[]{:S(2)}) copy-start(bf16[1,128,128]{2,1,0:T(8,128)(2,1)} %copy-done.12) | copy-start | bytes 98308
  109.9 18.5 %copy-start.18 = (bf16[1,128,128]{1,2,0:T(8,128)(2,1)S(1)}, bf16[1,128,128]{1,2,0:T(8,128)(2,1)}, u32[]{:S(2)}) copy-start(bf16[1,128,128]{1,2,0:T(8,128)(2,1)} %copy.18) | copy-start | bytes 98308
  (25 other events, 62.9 us)
Sparse Core Ops, SparseCore 0:
  9.0 35.4 all-gather.4
  46.0 38.7 all-gather.2

commit v11 on v10

--- a/solution.py
+++ b/solution.py
@@ -153,11 +153,10 @@
     for c in range(nc):
         across[:, cols(c)] = column_blur(lambda i: joined[i], bf_ref, c).astype(bf16)
     level = bg_ref[0]
-    @pl.loop(0, nc)
-    def _(c):
-        blurred = jnp.dot(a_ref[...], across[:, lanes(c)], preferred_element_type=f32) + level
-        quotient = (raw_ref[:, lanes(c)].astype(f32) / blurred).astype(bf16)
-        ratio[:, lanes(c)] = jnp.dot(at_ref[...], quotient, preferred_element_type=f32).astype(bf16)
+    for c in range(nc):
+        blurred = jnp.dot(a_ref[...], across[:, cols(c)], preferred_element_type=f32) + level
+        quotient = (raw_ref[:, cols(c)].astype(f32) / blurred).astype(bf16)
+        ratio[:, cols(c)] = jnp.dot(at_ref[...], quotient, preferred_element_type=f32).astype(bf16)
     for c in range(nc):
         spread = column_blur(lambda i: ratio[:, cols(i)], bb_ref, c).astype(bf16)
         back = jnp.dot(spread, mt_ref[...], preferred_element_type=f32)
@@ -182,7 +181,8 @@
             result = jnp.where(diff == tap_index, taps_ref[base + tap_index], result)
         return result.astype(jnp.bfloat16)
 
-    for i in range(count):
+    @pl.loop(0, count)
+    def _(i):
         base = i * TAPS
         a_ref[i] = build(src_row - out_row + radius, row_ref, base)
         at_ref[i] = build(out_row - src_row + radius, row_ref, base)

time: 155 us -> 139 us (0.90)
  Pallas kernels: 79.2 us -> 58.4 us
  waiting for transfers between devices: 6.59 us -> 11.4 us
    pallas_call x4, Pallas kernels: 74.2 us -> 52.6 us  [kernel_update(): pl.pallas_call(plane_kernel, grid=(1,), out_shape=jax.ShapeDtypeStruct((r...]
    all_gather x1, waiting for transfers between devices: 3.6 us -> 8.43 us  [local(): lax.all_gather(jnp.stack(pieces[1:]), 'tile', axis=2, tiled=True)]
  transfers between devices with their start and end apart: 12 -> 12, of which waited for: 3 -> 3; matrix products, arithmetic and copies ran while one was open for 14% -> 16% of each run, Pallas kernels for 16% -> 15%
where the time goes in v11:
time: 139 us; the launch traced here: 138 us
  Pallas kernels  58.4 us (42%)
  local copies, waits for them, and re-layouts  34.9 us (25%)
  between operations  15.7 us (11%)
  starting transfers between devices  11.7 us (8%)
  waiting for transfers between devices  11.4 us (8%)
  other arithmetic  5.79 us (4%)
    pallas_call x4, Pallas kernels, kernel_update(): pl.pallas_call(plane_kernel, grid=(1,), out_shape=jax.ShapeDtypeStruct((r...  52.6 us
    unnamed x74, local copies, waits for them, and re-layouts  16.2 us
    ppermute x6, starting transfers between devices, passed_along(): return lax.ppermute(x, axis, [(i, (i + by) % count) for i in range(count)])  10.6 us
    all_gather x1, waiting for transfers between devices, local(): lax.all_gather(jnp.stack(pieces[1:]), 'tile', axis=2, tiled=True)  8.43 us
    squeeze x4, local copies, waits for them, and re-layouts, local(): b[update_index * planes + p]  6.26 us
    pallas_call x1, Pallas kernels, all_bands(): pl.pallas_call(band_kernel, out_shape=(jax.ShapeDtypeStruct((count, rows,...  5.78 us
    ppermute x6, waiting for transfers between devices, passed_along(): return lax.ppermute(x, axis, [(i, (i + by) % count) for i in range(count)])  2.92 us
    dynamic_slice x5, local copies, waits for them, and re-layouts, local(): matrix = interp[view_index]  2.89 us
  transfers between devices with their start and end apart: 12, of which 3 were waited for; matrix products, arithmetic and copies ran while one was open for 16% of the time, Pallas kernels for 15%

profile of v11, /device:TPU:0, one launch (start us, length us, event | category | flops | bytes accessed | tf_op | source)
XLA Modules:
  0.0 137.9 jit_solution(12318965207734926241)
XLA Ops:
  6.5 1.8 %constant_dynamic-slice_fusion.5 = (bf16[1,1,32,2048]{3,2,1,0:T(8,128)(2,1)}, bf16[1,32,2048]{2,1,0:T(8,128)(2,1)S(1)}, bf16[1,32,2048]{2,1,0:T(8,128)(2,1)S(1)}, bf16[1,32,2048]{2,1,0:T(8,128)(2,1)S(1)}) fusion(bf16[1,4,32,2048]{3,2,1,0:T(8,128)(2,1)} %param.10, s32[]{:T(128)S(6)} %select_n.240, s32[]{:T(128)S(6)} %select_n.218, s32[]{:T(128)S(6)} %select_n.216, ...), kind=kLoop, calls=%fused_computation.58 | loop fusion | bytes 1048592 | tf_op jit(solution)/shard_map/dynamic_slice | solution.py:449
  8.4 3.1 %collective-permute-start.3 = (f32[1,32,2048]{2,1,0:T(8,128)}, f32[1,32,2048]{2,1,0:T(8,128)}, u32[]{:S(2)}, u32[]{:S(2)}) collective-permute-start(f32[1,32,2048]{2,1,0:T(8,128)} %param.9), channel_id=1, source_target_pairs={{0,2},{1,3},{2,4},{3,5},{4,6},{5,7},{6,0},{7,1},{8,10},{9,11},{10,... | collective-permute-start | bytes 786440 | tf_op jit(solution)/shard_map/ppermute | solution.py:15
  11.5 2.6 %collective-permute-start.4 = (f32[1,32,2048]{2,1,0:T(8,128)}, f32[1,32,2048]{2,1,0:T(8,128)}, u32[]{:S(2)}, u32[]{:S(2)}) collective-permute-start(f32[1,32,2048]{2,1,0:T(8,128)} %param.9), channel_id=1, source_target_pairs={{0,4},{1,5},{2,6},{3,7},{4,0},{5,1},{6,2},{7,3},{8,12},{9,13},{10,... | collective-permute-start | bytes 786440 | tf_op jit(solution)/shard_map/ppermute | solution.py:15
  14.1 2.4 %collective-permute-start = (bf16[1,32,2048]{2,1,0:T(8,128)(2,1)S(1)}, bf16[1,32,2048]{2,1,0:T(8,128)(2,1)S(1)}, u32[]{:S(2)}, u32[]{:S(2)}) collective-permute-start(bf16[1,32,2048]{2,1,0:T(8,128)(2,1)S(1)} %get-tuple-element.53), channel_id=1, source_target_pairs={{0,24},{8,0},{16,8},{24,16},{1,25},{9,1},{17,9},{25,17},{2,26},{10... | collective-permute-start | bytes 393224 | tf_op jit(solution)/shard_map/ppermute | solution.py:15
  20.2 1.3 collective-permute-start.5
  21.6 2.3 %collective-permute-done.1 = bf16[1,32,2048]{2,1,0:T(8,128)(2,1)S(1)} collective-permute-done((bf16[1,32,2048]{2,1,0:T(8,128)(2,1)S(1)}, bf16[1,32,2048]{2,1,0:T(8,128)(2,1)S(1)}, u32[]{:S(2)}, u32[]{:S(2)}) %collective-permute-start.1) | collective-permute-done | bytes 131104 | tf_op jit(solution)/shard_map/ppermute | solution.py:15
  30.8 5.8 %shard_map.91 = (bf16[4,256,256]{2,1,0:T(8,128)(2,1)}, bf16[4,256,256]{2,1,0:T(8,128)(2,1)}, bf16[4,3,128,128]{3,2,1,0:T(8,128)(2,1)}, bf16[4,3,128,128]{3,2,1,0:T(8,128)(2,1)}) custom-call(f32[68]{0:T(128)} %reshape.563.row_ref, f32[68]{0:T(128)} %reshape.564.col_ref), custom_call_target="tpu_custom_call" | custom-call | tf_op jit(solution)/shard_map/pallas_call | solution.py:200
  38.7 1.8 %slice_bitcast_fusion.8 = (bf16[3,128,128]{2,1,0:T(8,128)(2,1)}, bf16[3,128,128]{2,1,0:T(8,128)(2,1)}, bf16[3,128,128]{2,1,0:T(8,128)(2,1)}, bf16[3,128,128]{2,1,0:T(8,128)(2,1)}) fusion(bf16[4,3,128,128]{3,2,1,0:T(8,128)(2,1)} %get-tuple-element.10), kind=kLoop, calls=%fused_computation.41 | loop fusion | bytes 786432 | tf_op jit(solution)/shard_map/squeeze | solution.py:487
  40.5 1.8 %slice_bitcast_fusion.9 = (bf16[3,128,128]{2,1,0:T(8,128)(2,1)}, bf16[3,128,128]{2,1,0:T(8,128)(2,1)}, bf16[3,128,128]{2,1,0:T(8,128)(2,1)}, bf16[3,128,128]{2,1,0:T(8,128)(2,1)}) fusion(bf16[4,3,128,128]{3,2,1,0:T(8,128)(2,1)} %get-tuple-element.9), kind=kLoop, calls=%fused_computation.42 | loop fusion | bytes 786432 | tf_op jit(solution)/shard_map/squeeze | solution.py:487
  42.3 1.9 %slice_bitcast_fusion = (bf16[256,256]{1,0:T(8,128)(2,1)}, bf16[256,256]{1,0:T(8,128)(2,1)}, bf16[256,256]{1,0:T(8,128)(2,1)S(1)}, bf16[256,256]{1,0:T(8,128)(2,1)S(1)}) fusion(bf16[4,256,256]{2,1,0:T(8,128)(2,1)} %get-tuple-element.12), kind=kLoop, calls=%fused_computation.30 | loop fusion | bytes 1048576 | tf_op jit(solution)/shard_map/squeeze | solution.py:487
  44.9 1.1 fusion.13
  52.6 1.1 copy-done.4
  53.6 1.1 copy-done.5
  55.5 0.9 copy-done.23
  56.4 0.9 copy-done.24
  59.8 1.2 copy-done.28
  61.0 1.0 copy-done.29
  62.0 14.4 %shard_map.92.rest_0_ = f32[256,2048]{1,0:T(8,128)} custom-call(s32[8]{0:T(128)S(1)} %broadcast_multiply_fusion.offs_ref, f32[1]{0:T(128)} %get-tuple-element.75.bg_ref, bf16[1,1,256,2048]{3,2,1,0:T(8,128)(2,1)S(1)} %copy-done.28, bf16[128,128]{1,0:T(8,128)(2,1)S(1)} %bitcast.94, bf16[128,128]{1,0:T(8,128)(2,1)S(1)} %bitcast.95, ...), custom_call_target="tpu_custom_call" | custom-call | flops 2147483648 | bytes 5242880 | tf_op jit(solution)/shard_map/pallas_call | solution.py:228
  76.4 8.4 %all-gather.3.cloned.1.call-done.raw_ref = bf16[3,1,256,2048]{3,2,1,0:T(8,128)(2,1)} async-done(((bf16[3,1,32,2048]{3,2,1,0:T(8,128)(2,1)}), bf16[3,1,256,2048]{3,2,1,0:T(8,128)(2,1)}) %all-gather.3.cloned.1.call-update) | async-done | bytes 3145744 | tf_op jit(solution)/shard_map/all_gather | solution.py:455
  85.0 1.6 %copy-done = f32[256,2048]{1,0:T(8,128)S(1)} copy-done((f32[256,2048]{1,0:T(8,128)S(1)}, f32[256,2048]{1,0:T(8,128)}, u32[]{:S(2)}) %copy-start) | copy-done | bytes 2097176
  86.5 0.9 copy-done.2
  91.7 12.7 %shard_map.93.rest_0_ = f32[256,2048]{1,0:T(8,128)S(1)} custom-call(s32[1]{0:T(128)} %constant.162.clone.1.offs_ref, f32[1]{0:T(128)} %get-tuple-element.78.bg_ref, bf16[3,1,256,2048]{3,2,1,0:T(8,128)(2,1)} %all-gather.3.cloned.1.call-done.raw_ref, bf16[128,128]{1,0:T(8,128)(2,1)S(1)} %bitcast.90, bf16[128,128]{1,0:T(8,128)(2,1)S(1)} %bitcast.93, ...), custom_call_target="tpu_custom_call" | custom-call | flops 2147483648 | bytes 5242880 | tf_op jit(solution)/shard_map/pallas_call | solution.py:228
  104.6 12.7 %shard_map.94.rest_0_ = f32[256,2048]{1,0:T(8,128)S(1)} custom-call(s32[1]{0:T(128)} %constant.162.clone.1.offs_ref, f32[1]{0:T(128)} %get-tuple-element.76.bg_ref, bf16[3,1,256,2048]{3,2,1,0:T(8,128)(2,1)} %all-gather.3.cloned.1.call-done.raw_ref, bf16[128,128]{1,0:T(8,128)(2,1)S(1)} %bitcast.89, bf16[128,128]{1,0:T(8,128)(2,1)S(1)} %bitcast.92, ...), custom_call_target="tpu_custom_call" | custom-call | flops 2147483648 | bytes 5242880 | tf_op jit(solution)/shard_map/pallas_call | solution.py:228
  117.5 12.8 %shard_map.95 = f32[256,2048]{1,0:T(8,128)S(1)} custom-call(s32[1]{0:T(128)} %constant.162.clone.1.offs_ref, f32[1]{0:T(128)} %get-tuple-element.77.bg_ref, bf16[3,1,256,2048]{3,2,1,0:T(8,128)(2,1)} %all-gather.3.cloned.1.call-done.raw_ref, bf16[128,128]{1,0:T(8,128)(2,1)S(1)} %bitcast.88, bf16[128,128]{1,0:T(8,128)(2,1)S(1)} %bitcast.91, ...), custom_call_target="tpu_custom_call" | custom-call | flops 2147483648 | bytes 5242880 | tf_op jit(solution)/shard_map/pallas_call | solution.py:228
  (146 shorter events, 26.5 us)
Async XLA Ops:
  6.5 18.6 %copy-start.36 = (s32[4]{0:T(128)S(1)}, s32[4]{0:T(128)}, u32[]{:S(2)}) copy-start(s32[4]{0:T(128)} %param.16) | copy-start | bytes 52
  6.5 20.4 %copy-start.34 = (f32[4,4,17]{2,1,0:T(4,128)S(1)}, f32[4,4,17]{2,1,0:T(4,128)}, u32[]{:S(2)}) copy-start(f32[4,4,17]{2,1,0:T(4,128)} %param.14) | copy-start | bytes 3268
  6.5 21.1 %copy-start.35 = (f32[4,4,17]{2,1,0:T(4,128)S(1)}, f32[4,4,17]{2,1,0:T(4,128)}, u32[]{:S(2)}) copy-start(f32[4,4,17]{2,1,0:T(4,128)} %param.15) | copy-start | bytes 3268
  6.5 45.2 %all-gather.5.cloned.1.call-start = ((), (), s32[]{:S(2)}) async-start(), calls=%async_computation.1 | async-start | bytes 1179648 | tf_op jit(solution)/shard_map/all_gather | solution.py:454
  8.4 76.4 %all-gather.3.cloned.1.call-start = ((), (), s32[]{:S(2)}) async-start(), calls=%async_computation | async-start | bytes 3538944 | tf_op jit(solution)/shard_map/all_gather | solution.py:455
  8.4 38.2 %collective-permute-start.3 = (f32[1,32,2048]{2,1,0:T(8,128)}, f32[1,32,2048]{2,1,0:T(8,128)}, u32[]{:S(2)}, u32[]{:S(2)}) collective-permute-start(f32[1,32,2048]{2,1,0:T(8,128)} %param.9), channel_id=1, source_target_pairs={{0,2},{1,3},{2,4},{3,5},{4,6},{5,7},{6,0},{7,1},{8,10},{9,11},{10,... | collective-permute-start | bytes 786440 | tf_op jit(solution)/shard_map/ppermute | solution.py:15
  11.5 35.7 %collective-permute-start.4 = (f32[1,32,2048]{2,1,0:T(8,128)}, f32[1,32,2048]{2,1,0:T(8,128)}, u32[]{:S(2)}, u32[]{:S(2)}) collective-permute-start(f32[1,32,2048]{2,1,0:T(8,128)} %param.9), channel_id=1, source_target_pairs={{0,4},{1,5},{2,6},{3,7},{4,0},{5,1},{6,2},{7,3},{8,12},{9,13},{10,... | collective-permute-start | bytes 786440 | tf_op jit(solution)/shard_map/ppermute | solution.py:15
  14.1 6.1 %collective-permute-start = (bf16[1,32,2048]{2,1,0:T(8,128)(2,1)S(1)}, bf16[1,32,2048]{2,1,0:T(8,128)(2,1)S(1)}, u32[]{:S(2)}, u32[]{:S(2)}) collective-permute-start(bf16[1,32,2048]{2,1,0:T(8,128)(2,1)S(1)} %get-tuple-element.53), channel_id=1, source_target_pairs={{0,24},{8,0},{16,8},{24,16},{1,25},{9,1},{17,9},{25,17},{2,26},{10... | collective-permute-start | bytes 393224 | tf_op jit(solution)/shard_map/ppermute | solution.py:15
  16.6 7.3 %collective-permute-start.1 = (bf16[1,32,2048]{2,1,0:T(8,128)(2,1)S(1)}, bf16[1,32,2048]{2,1,0:T(8,128)(2,1)S(1)}, u32[]{:S(2)}, u32[]{:S(2)}) collective-permute-start(bf16[1,32,2048]{2,1,0:T(8,128)(2,1)S(1)} %get-tuple-element.52), channel_id=1, source_target_pairs={{0,16},{8,24},{16,0},{24,8},{1,17},{9,25},{17,1},{25,9},{2,18},{10... | collective-permute-start | bytes 393224 | tf_op jit(solution)/shard_map/ppermute | solution.py:15
  17.1 6.8 %collective-permute-start.2 = (bf16[1,32,2048]{2,1,0:T(8,128)(2,1)S(1)}, bf16[1,32,2048]{2,1,0:T(8,128)(2,1)S(1)}, u32[]{:S(2)}, u32[]{:S(2)}) collective-permute-start(bf16[1,32,2048]{2,1,0:T(8,128)(2,1)S(1)} %get-tuple-element.54), channel_id=1, source_target_pairs={{0,8},{8,16},{16,24},{24,0},{1,9},{9,17},{17,25},{25,1},{2,10},{10... | collective-permute-start | bytes 393224 | tf_op jit(solution)/shard_map/ppermute | solution.py:15
  20.2 27.1 %collective-permute-start.5 = (f32[1,32,2048]{2,1,0:T(8,128)}, f32[1,32,2048]{2,1,0:T(8,128)}, u32[]{:S(2)}, u32[]{:S(2)}) collective-permute-start(f32[1,32,2048]{2,1,0:T(8,128)} %param.9), channel_id=1, source_target_pairs={{0,6},{1,7},{2,0},{3,1},{4,2},{5,3},{6,4},{7,5},{8,14},{9,15},{10,... | collective-permute-start | bytes 786440 | tf_op jit(solution)/shard_map/ppermute | solution.py:15
  23.9 27.8 %collective-permute-start.6 = (f32[1,32,2048]{2,1,0:T(8,128)}, f32[1,32,2048]{2,1,0:T(8,128)}, u32[]{:S(2)}, u32[]{:S(2)}) collective-permute-start(f32[1,32,2048]{2,1,0:T(8,128)} %param.9), channel_id=1, source_target_pairs={{0,1},{1,0},{2,3},{3,2},{4,5},{5,4},{6,7},{7,6},{8,9},{9,8},{10,11... | collective-permute-start | bytes 786440 | tf_op jit(solution)/shard_map/ppermute | solution.py:461
  46.7 5.0 %collective-permute-start.7 = (f32[1,32,2048]{2,1,0:T(8,128)}, f32[1,32,2048]{2,1,0:T(8,128)}, u32[]{:S(2)}, u32[]{:S(2)}) collective-permute-start(f32[1,32,2048]{2,1,0:T(8,128)} %collective-permute-done.3), channel_id=1, source_target_pairs={{0,1},{1,0},{2,3},{3,2},{4,5},{5,4},{6,7},{7,6},{8,9},{9,8},{10,11... | collective-permute-start | bytes 786440 | tf_op jit(solution)/shard_map/ppermute | solution.py:461
  47.2 4.5 %collective-permute-start.8 = (f32[1,32,2048]{2,1,0:T(8,128)}, f32[1,32,2048]{2,1,0:T(8,128)}, u32[]{:S(2)}, u32[]{:S(2)}) collective-permute-start(f32[1,32,2048]{2,1,0:T(8,128)} %collective-permute-done.4), channel_id=1, source_target_pairs={{0,1},{1,0},{2,3},{3,2},{4,5},{5,4},{6,7},{7,6},{8,9},{9,8},{10,11... | collective-permute-start | bytes 786440 | tf_op jit(solution)/shard_map/ppermute | solution.py:461
  47.3 4.4 %collective-permute-start.9 = (f32[1,32,2048]{2,1,0:T(8,128)}, f32[1,32,2048]{2,1,0:T(8,128)}, u32[]{:S(2)}, u32[]{:S(2)}) collective-permute-start(f32[1,32,2048]{2,1,0:T(8,128)} %collective-permute-done.5), channel_id=1, source_target_pairs={{0,1},{1,0},{2,3},{3,2},{4,5},{5,4},{6,7},{7,6},{8,9},{9,8},{10,11... | collective-permute-start | bytes 786440 | tf_op jit(solution)/shard_map/ppermute | solution.py:461
  62.0 22.8 %copy-start.32 = (f32[512]{0:T(512)S(1)}, f32[512]{0:T(512)}, u32[]{:S(2)}) copy-start(f32[512]{0:T(512)} %broadcast_maximum_fusion.1) | copy-start | bytes 6148
  91.7 12.9 %copy-start.1 = (bf16[256,256]{1,0:T(8,128)(2,1)S(1)}, bf16[256,256]{1,0:T(8,128)(2,1)}, u32[]{:S(2)}) copy-start(bf16[256,256]{1,0:T(8,128)(2,1)} %get-tuple-element.49.a_ref) | copy-start | bytes 393220
  91.7 12.9 %copy-start.8 = (bf16[3,128,128]{2,1,0:T(8,128)(2,1)S(1)}, bf16[3,128,128]{2,1,0:T(8,128)(2,1)}, u32[]{:S(2)}) copy-start(bf16[3,128,128]{2,1,0:T(8,128)(2,1)} %get-tuple-element.57.bb_ref) | copy-start | bytes 294916
  91.7 12.9 %copy-start.9 = (bf16[3,128,128]{2,1,0:T(8,128)(2,1)S(1)}, bf16[3,128,128]{2,1,0:T(8,128)(2,1)}, u32[]{:S(2)}) copy-start(bf16[3,128,128]{2,1,0:T(8,128)(2,1)} %get-tuple-element.61.bf_ref) | copy-start | bytes 294916
  91.7 12.9 %copy-start.15 = (bf16[1,128,128]{2,1,0:T(8,128)(2,1)S(1)}, bf16[1,128,128]{2,1,0:T(8,128)(2,1)}, u32[]{:S(2)}) copy-start(bf16[1,128,128]{2,1,0:T(8,128)(2,1)} %copy-done.14) | copy-start | bytes 98308
  91.7 12.9 %copy-start.19 = (bf16[1,128,128]{1,2,0:T(8,128)(2,1)S(1)}, bf16[1,128,128]{1,2,0:T(8,128)(2,1)}, u32[]{:S(2)}) copy-start(bf16[1,128,128]{1,2,0:T(8,128)(2,1)} %copy.20) | copy-start | bytes 98308
  104.6 12.8 %copy-start.6 = (bf16[3,128,128]{2,1,0:T(8,128)(2,1)S(1)}, bf16[3,128,128]{2,1,0:T(8,128)(2,1)}, u32[]{:S(2)}) copy-start(bf16[3,128,128]{2,1,0:T(8,128)(2,1)} %get-tuple-element.58.bb_ref) | copy-start | bytes 294916
  104.6 12.8 %copy-start.7 = (bf16[3,128,128]{2,1,0:T(8,128)(2,1)S(1)}, bf16[3,128,128]{2,1,0:T(8,128)(2,1)}, u32[]{:S(2)}) copy-start(bf16[3,128,128]{2,1,0:T(8,128)(2,1)} %get-tuple-element.62.bf_ref) | copy-start | bytes 294916
  104.6 12.8 %copy-start.13 = (bf16[1,128,128]{2,1,0:T(8,128)(2,1)S(1)}, bf16[1,128,128]{2,1,0:T(8,128)(2,1)}, u32[]{:S(2)}) copy-start(bf16[1,128,128]{2,1,0:T(8,128)(2,1)} %copy-done.12) | copy-start | bytes 98308
  (25 other events, 57.6 us)
Sparse Core Ops, SparseCore 0:
  9.0 35.4 all-gather.4
  46.0 38.7 all-gather.2
